TPU v7x, 128 devices: a whole 4x4x4 slice. The times are simulated.
128 devices in a mesh: dp: 16 (over x, y_hi, core), tensor: 8 (over y_lo, z).
Axes of the slice: x: 4, y: 4 (y_hi: 2, y_lo: 2; y = y_hi * 2 + y_lo), z: 4, core: 2. Of those that a mesh axis runs over, the one named last changes fastest.
Arguments:
- hidden_state_input: bfloat16 [16384, 3584], P(('dp', 'tensor')), may hold values from -500 to 500
- token_embedding_input: bfloat16 [16384, 3584], P(('dp', 'tensor')), may hold values from -500 to 500
- input_norm_gain: float32 [7168], replicated, may hold values from 0.1 to 1.9
- query_projection_weight: bfloat16 [7168, 3584], P('dp', 'tensor'), may hold values from -0.0625 to 0.0625
- key_projection_weight: bfloat16 [7168, 3584], P('dp', 'tensor'), may hold values from -0.0625 to 0.0625
- value_projection_weight: bfloat16 [7168, 3584], P('dp', 'tensor'), may hold values from -0.0625 to 0.0625
- adapter_down_maps: bfloat16 [7168, 384], replicated, may hold values from -1 to 1
- adapter_up_maps: bfloat16 [3, 128, 3584], P(None, None, 'tensor'), may hold values from -2 to 2
- output_projection_weight: bfloat16 [3584, 3584], P('tensor'), may hold values from -0.09375 to 0.09375
- segment: int32 [16384], P('dp'), may hold values from 0 to 3, as said below
- live_token_length: int32 [16], P('dp'), may hold values from 512 to 1024, as said below
- request_cache_row: int32 [64], P('dp'), may hold values from 0 to 63, as said below
Outputs:
- block_out: bfloat16 [16384, 3584], P(('dp', 'tensor'))
- kv_cache: bfloat16 [64, 256, 2, 3584], P(None, 'dp', None, 'tensor')
Inputs may be any that keep to these rules, and one draw needn't show every extreme that they name: `segment`: within a stream, the live slots carry request numbers that never fall, every request 0 to 3 appears, each on (257) // 2 to 256 slots, some request in every draw on exactly 256; slots at or past live_token_length hold 3. `live_token_length`: each stream's live tokens; some stream is full in every draw. `request_cache_row`: A permutation of the 64 cache rows.
All inputs are finite; a program needn't handle non-finite values.
Results may differ from a plain program's by a relative error of at most 0.015.
The roundings to bfloat16 on the way count: a program that leaves them out, or rounds other values in their place, can miss the bound.
Values may be sent and summed in bfloat16 or wider, within the bound.
No kernel may reach another device: no remote copies, remote signals or barrier semaphores. Data moves between devices by JAX's collectives and lax.ppermute only.
A program may use at most 128 MiB of HBM per device.

v0:
```python
import math

import jax
import jax.numpy as jnp
from jax import lax
from jax.sharding import PartitionSpec as P

HD = 224


epsilon = 1e-05
negative = -1e30


def normalize(hidden_state_input, token_embedding_input, input_norm_gain):
    combined = jnp.concatenate([hidden_state_input, token_embedding_input], 1).astype(jnp.float32)
    factor = lax.rsqrt(jnp.mean(combined * combined, axis=1, keepdims=True) + epsilon)
    return (combined * factor * input_norm_gain).astype(jnp.bfloat16)


def attend_block(query, keys, values, segment, position, live, first, count, key_end):
    heads = query.shape[1] // HD
    block_query = query[first : first + count].reshape(count, heads, HD)
    block_keys = keys.reshape(key_end, heads, HD)
    block_values = values.reshape(key_end, heads, HD)
    scores = jnp.einsum(
        "qhd,khd->hqk", block_query, block_keys, preferred_element_type=jnp.float32
    ) / math.sqrt(HD)
    query_at = position[first : first + count]
    allowed = (
        (segment[first : first + count, None] == segment[None, :key_end])
        & (position[None, :] <= query_at[:, None])
        & (position[None, :] < live)
    )
    scores = jnp.where(allowed[None], scores, negative)
    top = jnp.max(scores, axis=-1, keepdims=True)
    expo = jnp.exp(scores - top)
    weights = (expo / jnp.sum(expo, axis=-1, keepdims=True)).astype(jnp.bfloat16)
    mixed = jnp.einsum("hqk,khd->qhd", weights, block_values, preferred_element_type=jnp.float32)
    mixed = jnp.where((query_at < live)[:, None, None], mixed, 0.0)
    return mixed.astype(jnp.bfloat16).reshape(count, heads * HD)


def body(
    hidden_state_input,
    token_embedding_input,
    input_norm_gain,
    query_projection_weight,
    key_projection_weight,
    value_projection_weight,
    adapter_down_maps,
    adapter_up_maps,
    output_projection_weight,
    segment,
    live_token_length,
    request_cache_row,
):
    adapter_rank_width = adapter_up_maps.shape[1]
    head_cols = query_projection_weight.shape[1]
    normalized_hidden = normalize(hidden_state_input, token_embedding_input, input_norm_gain)
    adapter_update = jnp.dot(
        normalized_hidden, adapter_down_maps, preferred_element_type=jnp.float32
    ).astype(jnp.bfloat16)
    stream_in, stream_low = (
        lax.all_gather(normalized_hidden, "tensor", axis=0, tiled=True),
        lax.all_gather(adapter_update, "tensor", axis=0, tiled=True),
    )
    pieces = (
        lax.all_gather(query_projection_weight, "dp", axis=0, tiled=True),
        lax.all_gather(key_projection_weight, "dp", axis=0, tiled=True),
        lax.all_gather(value_projection_weight, "dp", axis=0, tiled=True),
    )
    folded = tuple(
        (jnp.dot(stream_in, piece, preferred_element_type=jnp.float32) for piece in pieces)
    )
    projected = []
    for adapter_selector in range(3):
        adapter = jnp.dot(
            stream_low[
                :,
                adapter_selector * adapter_rank_width : (adapter_selector + 1) * adapter_rank_width,
            ],
            adapter_up_maps[adapter_selector],
            preferred_element_type=jnp.float32,
        )
        projected.append((folded[adapter_selector] + adapter).astype(jnp.bfloat16))
    query, keys, values = projected
    stream = query.shape[0]
    position = jnp.arange(stream, dtype=jnp.int32)
    live = live_token_length[0]
    block = min(512, stream)
    attended_parts = []
    for block_index in range(stream // block):
        first = block_index * block
        attended_parts.append(
            attend_block(query, keys, values, segment, position, live, first, block, stream)
        )
    attended = jnp.concatenate(attended_parts, 0)
    block_out = lax.psum_scatter(
        jnp.dot(attended, output_projection_weight, preferred_element_type=jnp.float32).astype(
            jnp.bfloat16
        ),
        "tensor",
        scatter_dimension=0,
        tiled=True,
    )
    requests = request_cache_row.shape[0]
    longest = stream // requests
    groups = lax.axis_size("dp")
    piece_len = longest // groups
    numbers = jnp.arange(requests, dtype=jnp.int32)
    membership = ((segment[:, None] == numbers[None, :]) & (position < live)[:, None]).astype(
        jnp.int32
    )
    lengths = jnp.sum(membership, axis=0)
    starts = jnp.cumsum(lengths) - lengths
    offsets = (
        jnp.arange(groups, dtype=jnp.int32)[:, None] * piece_len
        + jnp.arange(piece_len, dtype=jnp.int32)[None, :]
    )
    source_rows = jnp.minimum(starts[None, :, None] + offsets[:, None, :], stream - 1)
    alive_mask = offsets[:, None, :] < lengths[None, :, None]
    stacked = jnp.stack([keys, values], 1).reshape(stream, 2 * head_cols)
    taken = jnp.take(stacked, source_rows.reshape(-1), axis=0)
    taken = jnp.where(alive_mask.reshape(-1)[:, None], taken, jnp.zeros((), jnp.bfloat16))
    taken = taken.reshape(groups, requests, piece_len * 2 * head_cols)
    row_send = jnp.broadcast_to(request_cache_row[None, :], (groups, requests))
    received, received_rows = (
        lax.all_to_all(taken, "dp", split_axis=0, concat_axis=0, tiled=True),
        lax.all_to_all(row_send, "dp", split_axis=0, concat_axis=0, tiled=True),
    )
    total_reqs = groups * requests
    placing = (
        received_rows.reshape(-1)[:, None] == jnp.arange(total_reqs, dtype=jnp.int32)[None, :]
    ).astype(jnp.bfloat16)
    flat_received = received.reshape(total_reqs, piece_len * 2 * head_cols)
    cache_rows = lax.dot_general(
        placing, flat_received, (((0,), (0,)), ((), ())), preferred_element_type=jnp.float32
    )
    kv_cache = cache_rows.astype(jnp.bfloat16).reshape(total_reqs, piece_len, 2, head_cols)
    return (block_out, kv_cache)


def solution(mesh):
    return jax.shard_map(
        body,
        mesh=mesh,
        in_specs=(
            P(("dp", "tensor"), None),
            P(("dp", "tensor"), None),
            P(),
            P("dp", "tensor"),
            P("dp", "tensor"),
            P("dp", "tensor"),
            P(),
            P(None, None, "tensor"),
            P("tensor", None),
            P("dp"),
            P("dp"),
            P("dp"),
        ),
        out_specs=(P(("dp", "tensor"), None), P(None, "dp", None, "tensor")),
        check_vma=False,
    )
```

profile of v0, /device:TPU:1, one launch (start us, length us, event | category | flops | bytes accessed | tf_op | source)
XLA Modules:
  0.0 503.1 jit_solution(3945014618020465741)
XLA Ops:
  7.2 0.0 copy-start
  7.2 0.0 all-gather.9.cloned.1.call-start
  7.2 0.7 all-gather.9.cloned.1.call-update
  7.9 0.0 all-gather.5.cloned.1.call-start
  8.0 2.1 fusion.2
  10.0 0.0 copy-start.3
  10.0 3.2 fusion.4
  13.3 0.0 all-gather.5.cloned.1.call-update
  13.3 0.0 all-gather.11.cloned.1.call-start
  13.3 0.7 all-gather.11.cloned.1.call-update
  14.0 0.0 all-gather.7.cloned.1.call-start
  14.1 0.5 all-gather.7.cloned.1.call-update
  14.6 0.0 reduce-scatter.2.cloned.1.call-start
  14.7 0.0 copy-start.4
  15.4 0.0 copy-start.2
  15.4 4.3 convolution_convert_fusion.2
  19.7 28.2 %all_gather.17 = bf16[1024,384]{1,0:T(8,128)(2,1)S(1)} all-gather(bf16[128,384]{1,0:T(8,128)(2,1)S(1)} %convolution_convert_fusion.2), channel_id=1, replica_groups=mesh['dp'=16,'tensor'=8] {'tensor'}, dimensions={0}, use_global_device_ids=true | all-gather | bytes 884736 | tf_op jit(solution)/shard_map/all_gather | solution.py:66
  47.9 1.7 fusion.30
  49.7 1.7 fusion.28
  51.4 1.6 fusion.26
  53.0 2.1 fusion.14
  55.1 27.7 %all-gather.9.cloned.1.call-done = bf16[7168,448]{1,0:T(8,128)(2,1)} async-done(((bf16[448,448]{1,0:T(8,128)(2,1)}), bf16[7168,448]{1,0:T(8,128)(2,1)}) %all-gather.9.cloned.1.call-update) | async-done | bytes 6422544 | tf_op jit(solution)/shard_map/all_gather | solution.py:69
  82.9 150.3 %all-gather.5.cloned.1.call-done = bf16[1024,7168]{1,0:T(8,128)(2,1)} async-done(((bf16[128,7168]{1,0:T(8,128)(2,1)}), bf16[1024,7168]{1,0:T(8,128)(2,1)}) %all-gather.5.cloned.1.call-update) | async-done | bytes 14680080 | tf_op jit(solution)/shard_map/all_gather | solution.py:65
  233.2 13.3 %add_convert_fusion.1 = bf16[1024,448]{0,1:T(8,128)(2,1)} fusion(f32[1024,448]{0,1:T(8,128)} %fusion.28, bf16[1024,7168]{1,0:T(8,128)(2,1)} %all-gather.5.cloned.1.call-done, bf16[7168,448]{1,0:T(8,128)(2,1)} %all-gather.9.cloned.1.call-done), kind=kOutput, calls=%fused_computation.36 | convolution fusion | flops 6577586176 | bytes 23855104 | tf_op jit(solution)/shard_map/dot_general | solution.py:74
  246.4 2.2 fusion.49
  248.6 54.5 %all-gather.11.cloned.1.call-done = bf16[7168,448]{1,0:T(8,128)(2,1)} async-done(((bf16[448,448]{1,0:T(8,128)(2,1)}), bf16[7168,448]{1,0:T(8,128)(2,1)}) %all-gather.11.cloned.1.call-update) | async-done | bytes 6422544 | tf_op jit(solution)/shard_map/all_gather | solution.py:70
  303.1 13.3 %add_convert_fusion = bf16[1024,448]{0,1:T(8,128)(2,1)} fusion(f32[1024,448]{0,1:T(8,128)} %fusion.26, bf16[1024,7168]{1,0:T(8,128)(2,1)} %all-gather.5.cloned.1.call-done, bf16[7168,448]{1,0:T(8,128)(2,1)} %all-gather.11.cloned.1.call-done), kind=kOutput, calls=%fused_computation.35 | convolution fusion | flops 6577586176 | bytes 23855104 | tf_op jit(solution)/shard_map/dot_general | solution.py:74
  316.4 5.2 %fusion.51 = (f32[2,512]{1,0:T(2,128)S(1)}, f32[2,512,1024]{2,1,0:T(8,128)}) fusion(pred[512,1024]{1,0:T(8,128)(4,1)} %get-tuple-element.7, bf16[512,2,224]{0,2,1:T(8,128)(2,1)} %bitcast.61, bf16[1024,2,224]{0,2,1:T(8,128)(2,1)} %bitcast.54), kind=kOutput, calls=%fused_computation.85 | convolution fusion | flops 473957376 | bytes 6098944 | tf_op jit(solution)/shard_map/sub | solution.py:37
  321.6 5.3 %fusion.52 = (f32[2,512]{1,0:T(2,128)S(1)}, f32[2,512,1024]{2,1,0:T(8,128)}) fusion(pred[512,1024]{1,0:T(8,128)(4,1)} %get-tuple-element.6, bf16[512,2,224]{0,2,1:T(8,128)(2,1)} %bitcast.60, bf16[1024,2,224]{0,2,1:T(8,128)(2,1)} %bitcast.55), kind=kOutput, calls=%fused_computation.86 | convolution fusion | flops 473957376 | bytes 6098944 | tf_op jit(solution)/shard_map/sub | solution.py:37
  326.9 44.8 %all-gather.7.cloned.1.call-done = bf16[7168,448]{1,0:T(8,128)(2,1)} async-done(((bf16[448,448]{1,0:T(8,128)(2,1)}), bf16[7168,448]{1,0:T(8,128)(2,1)}) %all-gather.7.cloned.1.call-update) | async-done | bytes 6422544 | tf_op jit(solution)/shard_map/all_gather | solution.py:71
  371.7 13.3 %add_convert_fusion.2 = bf16[1024,448]{0,1:T(8,128)(2,1)} fusion(f32[1024,448]{0,1:T(8,128)} %fusion.30, bf16[1024,7168]{1,0:T(8,128)(2,1)} %all-gather.5.cloned.1.call-done, bf16[7168,448]{1,0:T(8,128)(2,1)} %all-gather.7.cloned.1.call-done), kind=kOutput, calls=%fused_computation.37 | convolution fusion | flops 6577586176 | bytes 23855104 | tf_op jit(solution)/shard_map/dot_general | solution.py:74
  385.0 3.5 fusion.20
  388.6 0.5 copy-done.6
  389.0 0.9 fusion.22
  390.0 6.1 %convolution_convert_fusion.1 = bf16[1024,3584]{1,0:T(8,128)(2,1)} fusion(bf16[448,3584]{1,0:T(8,128)(2,1)S(1)} %copy-done, bf16[512,448]{0,1:T(8,128)(2,1)S(1)} %bitcast.64, bf16[512,448]{0,1:T(8,128)(2,1)S(1)} %bitcast.65), kind=kOutput, calls=%fused_computation.4 | convolution fusion | flops 3293839360 | bytes 11468800 | tf_op jit(solution)/shard_map/dot_general | solution.py:100
  396.1 0.0 reduce-scatter.2.cloned.1.call-update
  396.1 0.6 copy-done.5
  396.7 0.6 broadcast_in_dim.104
  397.3 3.6 all-to-all-start
  400.9 0.1 convert_reduce_fusion
  401.1 0.2 reduce-window.8
  401.3 0.1 iota_add_fusion
  401.3 0.1 compare_and_fusion
  401.4 1.2 broadcast_in_dim.105
  402.7 4.0 broadcast_in_dim.106
  406.7 1.2 broadcast_in_dim.107
  407.9 3.9 broadcast_in_dim.108
  411.8 0.1 add_minimum_fusion
  411.9 0.1 min.22
  412.0 2.9 pad_maximum_fusion.1
  414.9 3.9 copy.17
  418.8 7.5 %gather_fusion = bf16[1024,896]{1,0:T(8,128)(2,1)} fusion(bf16[1024,896]{1,0:T(8,128)(2,1)} %copy.17, s32[1024]{0:T(1024)S(1)} %broadcast_clamp_fusion), kind=kCustom, calls=%fused_computation | custom fusion | bytes 3674112 | tf_op jit(solution)/shard_map/jit(_take)/gather | solution.py:124
  426.3 4.4 gather.7
  430.6 5.5 %select_select_fusion = bf16[16,4,14336]{2,1,0:T(4,128)(2,1)} fusion(pred[16,4,14336]{2,1,0:T(4,128)(4,1)} %broadcast_in_dim.106, pred[16,4,14336]{2,1,0:T(4,128)(4,1)} %broadcast_in_dim.108, bf16[16,4,14336]{2,1,0:T(4,128)(2,1)} %gather.7), kind=kLoop, calls=%fused_computation.34 | loop fusion | flops 1835008 | bytes 5505024 | tf_op jit(solution)/shard_map/jit(_where)/select_n | solution.py:125
  436.2 0.0 all-to-all-done
  436.2 7.1 %all-to-all-start.1 = ((bf16[16,4,14336]{2,1,0:T(4,128)(2,1)}), bf16[16,4,14336]{2,1,0:T(4,128)(2,1)}, u32[]{:S(2)}, u32[]{:S(2)}) async-start(bf16[16,4,14336]{2,1,0:T(4,128)(2,1)} %select_select_fusion), calls=%async_computation.2 | async-start | bytes 3670016 | tf_op jit(solution)/shard_map/all_to_all | solution.py:129
  443.3 0.5 broadcast.211
  443.8 0.6 reduce.3
  444.5 0.1 eq.65
  444.5 28.2 %all-to-all-done.1 = bf16[16,4,14336]{2,1,0:T(4,128)(2,1)} async-done(((bf16[16,4,14336]{2,1,0:T(4,128)(2,1)}), bf16[16,4,14336]{2,1,0:T(4,128)(2,1)}, u32[]{:S(2)}, u32[]{:S(2)}) %all-to-all-start.1) | async-done | bytes 1835040 | tf_op jit(solution)/shard_map/all_to_all | solution.py:129
  472.7 3.9 reshape.308
  476.6 3.6 convolution_convert_fusion
  480.1 6.8 %reshape.309 = bf16[64,16,2,448]{3,2,1,0:T(2,128)(2,1)} reshape(bf16[64,14336]{1,0:T(8,128)(2,1)} %convolution_convert_fusion) | data formatting | bytes 3670016 | tf_op jit(solution)/shard_map/reshape | solution.py:140
  486.9 9.7 %reduce-scatter.2.cloned.1.call-done = bf16[128,3584]{1,0:T(8,128)(2,1)} async-done(((bf16[1024,3584]{1,0:T(8,128)(2,1)}), bf16[128,3584]{1,0:T(8,128)(2,1)}) %reduce-scatter.2.cloned.1.call-update) | async-done | bytes 917520 | tf_op jit(solution)/shard_map/reduce_scatter | solution.py:99
  (21 shorter events, 0.1 us)
Async XLA Ops:
  7.2 382.8 %copy-start = (bf16[448,3584]{1,0:T(8,128)(2,1)S(1)}, bf16[448,3584]{1,0:T(8,128)(2,1)}, u32[]{:S(2)}) copy-start(bf16[448,3584]{1,0:T(8,128)(2,1)} %param.20) | copy-start | bytes 9633796
  7.2 75.7 %all-gather.9.cloned.1.call-start = ((), (), s32[]{:S(2)}) async-start(), calls=%async_computation.5 | async-start | bytes 7798784 | tf_op jit(solution)/shard_map/all_gather | solution.py:69
  7.9 225.2 %all-gather.5.cloned.1.call-start = ((), (), s32[]{:S(2)}) async-start(), calls=%async_computation.3 | async-start | bytes 16515072 | tf_op jit(solution)/shard_map/all_gather | solution.py:65
  10.0 5.3 %copy-start.3 = (s32[1024]{0:T(1024)S(1)}, s32[1024]{0:T(1024)}, u32[]{:S(2)}) copy-start(s32[1024]{0:T(1024)} %param.21) | copy-start | bytes 12292
  13.3 289.8 %all-gather.11.cloned.1.call-start = ((), (), s32[]{:S(2)}) async-start(), calls=%async_computation.6 | async-start | bytes 7798784 | tf_op jit(solution)/shard_map/all_gather | solution.py:70
  14.0 357.7 %all-gather.7.cloned.1.call-start = ((), (), s32[]{:S(2)}) async-start(), calls=%async_computation.4 | async-start | bytes 7798784 | tf_op jit(solution)/shard_map/all_gather | solution.py:71
  14.6 482.0 %reduce-scatter.2.cloned.1.call-start = ((), (), s32[]{:S(2)}) async-start(), calls=%async_computation.7 | async-start | bytes 8257536 | tf_op jit(solution)/shard_map/reduce_scatter | solution.py:99
  14.7 5.0 %copy-start.4 = (s32[1024]{0:T(1024)}, s32[1024]{0:T(1024)S(1)}, u32[]{:S(2)}) copy-start(s32[1024]{0:T(1024)S(1)} %iota.48) | copy-start | bytes 12292
  15.4 32.5 %copy-start.2 = (bf16[3,128,448]{1,2,0:T(8,128)(2,1)S(1)}, bf16[3,128,448]{1,2,0:T(8,128)(2,1)}, u32[]{:S(2)}) copy-start(bf16[3,128,448]{1,2,0:T(8,128)(2,1)} %param.19) | copy-start | bytes 1032196
  47.9 5.0 %slice-start = ((s32[1024]{0:T(1024)}), s32[512]{0:T(512)S(1)}, s32[]{:S(2)}) async-start(s32[1024]{0:T(1024)} %copy-done.4), calls=%async_computation.8 | async-start | bytes 4096 | tf_op jit(solution)/shard_map/slice | solution.py:29
  385.0 3.5 copy-start.1
  385.0 4.0 copy-start.6
  396.1 0.7 copy-start.5
  397.3 38.9 %all-to-all-start = ((s32[16,1,4]{2,1,0:T(1,128)}), s32[16,1,4]{2,1,0:T(1,128)S(1)}, u32[]{:S(2)}, u32[]{:S(2)}) async-start(s32[16,1,4]{2,1,0:T(1,128)} %broadcast_in_dim.104), calls=%async_computation.1 | async-start | bytes 16384 | tf_op jit(solution)/shard_map/all_to_all | solution.py:130
  436.2 36.5 %all-to-all-start.1 = ((bf16[16,4,14336]{2,1,0:T(4,128)(2,1)}), bf16[16,4,14336]{2,1,0:T(4,128)(2,1)}, u32[]{:S(2)}, u32[]{:S(2)}) async-start(bf16[16,4,14336]{2,1,0:T(4,128)(2,1)} %select_select_fusion), calls=%async_computation.2 | async-start | bytes 3670016 | tf_op jit(solution)/shard_map/all_to_all | solution.py:129
Sparse Core Ops, SparseCore 0:
  10.4 72.4 all-gather.8
  85.1 148.0 all-gather.4
  235.6 67.4 all-gather.10
  305.3 66.3 all-gather.6
  396.2 100.3 reduce-scatter.1
where the time goes:
time: 504 us; the launch traced here: 503 us
  waiting for transfers between devices  317 us (63%)
  matrix products  73.9 us (15%)
  local copies, waits for them, and re-layouts  41.3 us (8%)
  blocking collectives  28.2 us (6%)
  other arithmetic  17.1 us (3%)
  between operations  14.6 us (3%)
  starting transfers between devices  10.9 us (2%)
    all_gather x1, waiting for transfers between devices, body(): lax.all_gather(normalized_hidden, 'tensor', axis=0, tiled=True)  150 us
    all_gather x1, waiting for transfers between devices, body(): lax.all_gather(key_projection_weight, 'dp', axis=0, tiled=True)  54.5 us
    all_gather x1, waiting for transfers between devices, body(): lax.all_gather(value_projection_weight, 'dp', axis=0, tiled=True)  44.8 us
    dot_general x3, matrix products, body(): jnp.dot(stream_in, piece, preferred_element_type=jnp.float32)  39.9 us
    all_gather x1, blocking collectives, body(): lax.all_gather(adapter_update, 'tensor', axis=0, tiled=True)  28.2 us
    all_to_all x1, waiting for transfers between devices, body(): lax.all_to_all(taken, 'dp', split_axis=0, concat_axis=0, tiled=True)  28.2 us
    all_gather x1, waiting for transfers between devices, body(): lax.all_gather(query_projection_weight, 'dp', axis=0, tiled=True)  27.7 us
    gather x2, local copies, waits for them, and re-layouts, body(): taken = jnp.take(stacked, source_rows.reshape(-1), axis=0)  11.8 us
  transfers between devices with their start and end apart: 7, of which 6 were waited for; matrix products, arithmetic and copies ran while one was open for 21% of the time, Pallas kernels for 0%

commit v1 on v0

--- a/solution.py
+++ b/solution.py
@@ -39,6 +39,41 @@
     mixed = jnp.einsum("hqk,khd->qhd", weights, block_values, preferred_element_type=jnp.float32)
     mixed = jnp.where((query_at < live)[:, None, None], mixed, 0.0)
     return mixed.astype(jnp.bfloat16).reshape(count, heads * HD)
+
+
+def dp_index(x, yh, c):
+    return x * 4 + yh * 2 + c
+
+
+def dp_perm(move):
+    return [
+        (dp_index(x, yh, c), dp_index(*move(x, yh, c)))
+        for x in range(4)
+        for yh in range(2)
+        for c in range(2)
+    ]
+
+
+def gather_weights(weight_shard):
+    to_yh = dp_perm(lambda x, yh, c: (x, 1 - yh, c))
+    to_next = dp_perm(lambda x, yh, c: ((x + 1) % 4, yh, c))
+    to_prev = dp_perm(lambda x, yh, c: ((x - 1) % 4, yh, c))
+    to_core = dp_perm(lambda x, yh, c: (x, yh, 1 - c))
+    pair = jnp.stack([weight_shard, lax.ppermute(weight_shard, "dp", to_yh)])
+    from_prev = lax.ppermute(pair, "dp", to_next)
+    from_next = lax.ppermute(pair, "dp", to_prev)
+    far = jnp.stack(
+        [lax.ppermute(from_prev[0], "dp", to_next), lax.ppermute(from_next[1], "dp", to_prev)]
+    )
+    mine = jnp.concatenate([pair, from_prev, from_next, far], 0)
+    other = lax.ppermute(mine, "dp", to_core)
+    d = lax.axis_index("dp")
+    x, yh, c = d // 4, (d // 2) % 2, d % 2
+    x_off = jnp.array([0, 0, -1, -1, 1, 1, 2, 2] * 2, jnp.int32)
+    y_flip = jnp.array([0, 1] * 8, jnp.int32)
+    c_flip = jnp.array([0] * 8 + [1] * 8, jnp.int32)
+    order = ((x + x_off) % 4) * 4 + (yh ^ y_flip) * 2 + (c ^ c_flip)
+    return mine, other, order
 
 
 def body(
@@ -57,26 +92,34 @@
 ):
     adapter_rank_width = adapter_up_maps.shape[1]
     head_cols = query_projection_weight.shape[1]
+    block_rows = query_projection_weight.shape[0]
     normalized_hidden = normalize(hidden_state_input, token_embedding_input, input_norm_gain)
+    stream_in = lax.all_gather(normalized_hidden, "tensor", axis=0, tiled=True)
     adapter_update = jnp.dot(
-        normalized_hidden, adapter_down_maps, preferred_element_type=jnp.float32
+        stream_in, adapter_down_maps, preferred_element_type=jnp.float32
     ).astype(jnp.bfloat16)
-    stream_in, stream_low = (
-        lax.all_gather(normalized_hidden, "tensor", axis=0, tiled=True),
-        lax.all_gather(adapter_update, "tensor", axis=0, tiled=True),
-    )
-    pieces = (
-        lax.all_gather(query_projection_weight, "dp", axis=0, tiled=True),
-        lax.all_gather(key_projection_weight, "dp", axis=0, tiled=True),
-        lax.all_gather(value_projection_weight, "dp", axis=0, tiled=True),
-    )
-    folded = tuple(
-        (jnp.dot(stream_in, piece, preferred_element_type=jnp.float32) for piece in pieces)
-    )
+    weight_shard = jnp.concatenate(
+        [query_projection_weight, key_projection_weight, value_projection_weight], 1
+    )
+    mine, other, order = gather_weights(weight_shard)
+    stream = stream_in.shape[0]
+    blocks = stream_in.reshape(stream, -1, block_rows)
+    permuted = jnp.take(blocks, order, axis=1)
+    half = mine.shape[0] * block_rows
+    folded_all = jnp.dot(
+        permuted[:, : mine.shape[0]].reshape(stream, half),
+        mine.reshape(half, 3 * head_cols),
+        preferred_element_type=jnp.float32,
+    ) + jnp.dot(
+        permuted[:, mine.shape[0] :].reshape(stream, half),
+        other.reshape(half, 3 * head_cols),
+        preferred_element_type=jnp.float32,
+    )
+    folded = [folded_all[:, k * head_cols : (k + 1) * head_cols] for k in range(3)]
     projected = []
     for adapter_selector in range(3):
         adapter = jnp.dot(
-            stream_low[
+            adapter_update[
                 :,
                 adapter_selector * adapter_rank_width : (adapter_selector + 1) * adapter_rank_width,
             ],

time: 504 us -> 411 us (0.82); the launches traced: 503 us -> 405 us
  waiting for transfers between devices: 317 us -> 190 us
  blocking collectives: 28.2 us -> 0 us
  local copies, waits for them, and re-layouts: 41.3 us -> 68.9 us
  starting transfers between devices: 10.9 us -> 27.8 us
  matrix products: 73.9 us -> 80.9 us
    all_gather x4 -> x1, waiting for transfers between devices: 277 us -> 33 us  [body(): stream_in = lax.all_gather(normalized_hidden, 'tensor', axis=0, tiled=True)]
    ppermute x0 -> x6, waiting for transfers between devices: none -> 120 us  [the longest x1 52 us: gather_weights(): from_prev = lax.ppermute(pair, 'dp', to_next)]
    all_gather x1 -> x0, blocking collectives: 28.2 us -> none  [body(): lax.all_gather(adapter_update, 'tensor', axis=0, tiled=True)]
    ppermute x0 -> x6, starting transfers between devices: none -> 12.7 us  [the longest x1 3.73 us: gather_weights(): pair = jnp.stack([weight_shard, lax.ppermute(weight_shard, 'dp', to_yh)])]
    gather x0 -> x1, local copies, waits for them, and re-layouts: none -> 12.5 us  [body(): permuted = jnp.take(blocks, order, axis=1)]
    unnamed x14 -> x29, local copies, waits for them, and re-layouts: 1.12 us -> 12.6 us
    dot_general x7 -> x6, matrix products: 49.2 us -> 56.2 us  [the longest x1 18.5 us: body(): jnp.dot(permuted[:, mine.shape[0]:].reshape(stream, half), other.reshape(...]
  transfers between devices with their start and end apart: 7 -> 10, of which waited for: 6 -> 6; matrix products, arithmetic and copies ran while one was open for 21% -> 27% of each run, Pallas kernels for 0% -> 0%
where the time goes in v1:
time: 411 us; the launch traced here: 405 us
  waiting for transfers between devices  190 us (46%)
  matrix products  80.9 us (20%)
  local copies, waits for them, and re-layouts  68.9 us (17%)
  starting transfers between devices  27.8 us (7%)
  other arithmetic  21.6 us (5%)
  between operations  15.5 us (4%)
    ppermute x1, waiting for transfers between devices, gather_weights(): from_prev = lax.ppermute(pair, 'dp', to_next)  52 us
    ppermute x1, waiting for transfers between devices, gather_weights(): pair = jnp.stack([weight_shard, lax.ppermute(weight_shard, 'dp', to_yh)])  46.9 us
    all_gather x1, waiting for transfers between devices, body(): stream_in = lax.all_gather(normalized_hidden, 'tensor', axis=0, tiled=True)  33 us
    all_to_all x1, waiting for transfers between devices, body(): lax.all_to_all(taken, 'dp', split_axis=0, concat_axis=0, tiled=True)  28 us
    ppermute x1, waiting for transfers between devices, gather_weights(): lax.ppermute(from_prev[0], 'dp', to_next)  20.7 us
    dot_general x1, matrix products, body(): jnp.dot(permuted[:, mine.shape[0]:].reshape(stream, half), other.reshape(...  18.5 us
    dot_general x1, matrix products, body(): jnp.dot(permuted[:, :mine.shape[0]].reshape(stream, half), mine.reshape(h...  17.4 us
    dot_general x1, matrix products, body(): jnp.dot(stream_in, adapter_down_maps, preferred_element_type=jnp.float32)  12.7 us
  transfers between devices with their start and end apart: 10, of which 6 were waited for; matrix products, arithmetic and copies ran while one was open for 27% of the time, Pallas kernels for 0%

profile of v1, /device:TPU:1, one launch (start us, length us, event | category | flops | bytes accessed | tf_op | source)
XLA Modules:
  0.0 404.7 jit_solution(8163427628613574957)
XLA Ops:
  7.2 2.4 copy.24
  9.6 2.2 copy.25
  11.8 2.4 fusion.8
  14.2 5.8 %fusion.10 = bf16[128,7168]{0,1:T(8,128)(2,1)} fusion(f32[7168]{0:T(1024)S(1)} %copy-done.5, f32[128]{0:T(128)S(1)} %add_rsqrt_fusion, bf16[128,3584]{0,1:T(8,128)(2,1)} %copy.25, bf16[128,3584]{0,1:T(8,128)(2,1)} %copy.24), kind=kLoop, calls=%fused_computation.22 | loop fusion | flops 6422528 | bytes 3699200 | tf_op jit(solution)/shard_map/convert_element_type | solution.py:18
  20.1 3.5 concatenate.14
  23.6 3.7 collective-permute-start
  27.4 46.9 %collective-permute-done = bf16[448,1344]{1,0:T(8,128)(2,1)S(1)} collective-permute-done((bf16[448,1344]{1,0:T(8,128)(2,1)}, bf16[448,1344]{1,0:T(8,128)(2,1)S(1)}, u32[]{:S(2)}, u32[]{:S(2)}) %collective-permute-start) | collective-permute-done | bytes 1204256 | tf_op jit(solution)/shard_map/ppermute | solution.py:62
  74.2 1.6 pad_maximum_fusion
  75.8 1.1 collective-permute-start.1
  76.9 1.7 collective-permute-start.2
  78.5 1.2 constant_dynamic-update-slice_fusion.3
  79.7 52.0 %collective-permute-done.1 = bf16[2,448,1344]{2,1,0:T(8,128)(2,1)S(1)} collective-permute-done((bf16[2,448,1344]{2,1,0:T(8,128)(2,1)S(1)}, bf16[2,448,1344]{2,1,0:T(8,128)(2,1)S(1)}, u32[]{:S(2)}, u32[]{:S(2)}) %collective-permute-start.1) | collective-permute-done | bytes 2408480 | tf_op jit(solution)/shard_map/ppermute | solution.py:63
  131.7 0.1 slice_bitcast_fusion.1
  131.9 0.1 slice_bitcast_fusion
  132.0 2.7 collective-permute-start.4
  134.8 1.2 constant_dynamic-update-slice_fusion.2
  135.9 1.7 constant_dynamic-update-slice_fusion.1
  137.6 1.7 constant_dynamic-update-slice_fusion
  139.3 20.7 %collective-permute-done.3 = bf16[448,1344]{1,0:T(8,128)(2,1)S(1)} collective-permute-done((bf16[448,1344]{1,0:T(8,128)(2,1)S(1)}, bf16[448,1344]{1,0:T(8,128)(2,1)S(1)}, u32[]{:S(2)}, u32[]{:S(2)}) %collective-permute-start.3) | collective-permute-done | bytes 1204256 | tf_op jit(solution)/shard_map/ppermute | solution.py:66
  160.0 1.2 bitcast_dynamic-update-slice_fusion.1
  161.2 1.1 bitcast_dynamic-update-slice_fusion
  162.3 3.4 collective-permute-start.5
  166.6 2.2 fusion.20
  168.7 33.0 %all-gather.2.cloned.1.call-done = bf16[1024,7168]{0,1:T(8,128)(2,1)} async-done(((bf16[128,7168]{0,1:T(8,128)(2,1)}), bf16[1024,7168]{0,1:T(8,128)(2,1)}) %all-gather.2.cloned.1.call-update) | async-done | bytes 14680080 | tf_op jit(solution)/shard_map/all_gather | solution.py:97
  201.7 12.5 %gather_fusion = bf16[16,1024,448]{1,2,0:T(8,128)(2,1)} fusion(bf16[1024,16,448]{0,2,1:T(8,128)(2,1)} %bitcast.73, s32[1024]{0:T(1024)S(1)} %pad_clamp_fusion), kind=kCustom, calls=%fused_computation | custom fusion | bytes 29360192 | tf_op jit(solution)/shard_map/jit(_take)/gather | solution.py:107
  214.2 12.7 %convolution_convert_fusion.2 = bf16[1024,384]{1,0:T(8,128)(2,1)S(1)} fusion(bf16[1024,7168]{0,1:T(8,128)(2,1)} %all-gather.2.cloned.1.call-done, bf16[7168,384]{1,0:T(8,128)(2,1)} %param.21), kind=kOutput, calls=%fused_computation.49 | convolution fusion | flops 5637537792 | bytes 20971520 | tf_op jit(solution)/shard_map/dot_general | solution.py:98
  226.8 17.4 %fusion.4 = f32[1024,1344,1]{0,1,2:T(8,128)} fusion(bf16[8,448,1344]{2,1,0:T(8,128)(2,1)} %bitcast_dynamic-update-slice_fusion, bf16[16,1024,448]{1,2,0:T(8,128)(2,1)} %gather_fusion, pred[16]{0:T(512)(128)(4,1)S(1)} %get-tuple-element.2), kind=kOutput, calls=%fused_computation.7 | convolution fusion | flops 9872343040 | bytes 29818896 | tf_op jit(solution)/shard_map/dot_general | solution.py:109
  244.3 18.5 %bitcast_add_fusion = f32[1024,1344]{0,1:T(8,128)} fusion(f32[1024,1344,1]{0,1,2:T(8,128)} %fusion.4, bf16[8,448,1344]{2,1,0:T(8,128)(2,1)} %collective-permute-done.5, bf16[16,1024,448]{1,2,0:T(8,128)(2,1)} %gather_fusion, pred[16]{0:T(512)(128)(4,1)S(1)} %get-tuple-element.2), kind=kOutput, calls=%fused_computation.11 | convolution fusion | flops 9873719296 | bytes 35323920 | tf_op jit(solution)/shard_map/dot_general | solution.py:113
  262.8 2.8 fusion.25
  265.6 2.9 fusion.27
  268.5 1.9 fusion.26
  270.4 1.0 fusion.61
  271.4 5.1 %fusion.63 = (f32[2,512]{1,0:T(2,128)S(1)}, f32[2,512,1024]{2,1,0:T(8,128)}) fusion(pred[512,1024]{1,0:T(8,128)(4,1)} %get-tuple-element.9, bf16[512,2,224]{0,2,1:T(8,128)(2,1)} %bitcast.84, bf16[1024,2,224]{0,2,1:T(8,128)(2,1)} %bitcast.77), kind=kOutput, calls=%fused_computation.113 | convolution fusion | flops 473957376 | bytes 6098944 | tf_op jit(solution)/shard_map/sub | solution.py:37
  276.6 5.2 %fusion.64 = (f32[2,512]{1,0:T(2,128)S(1)}, f32[2,512,1024]{2,1,0:T(8,128)}) fusion(pred[512,1024]{1,0:T(8,128)(4,1)} %get-tuple-element.8, bf16[512,2,224]{0,2,1:T(8,128)(2,1)} %bitcast.83, bf16[1024,2,224]{0,2,1:T(8,128)(2,1)} %bitcast.78), kind=kOutput, calls=%fused_computation.114 | convolution fusion | flops 473957376 | bytes 6098944 | tf_op jit(solution)/shard_map/sub | solution.py:37
  281.8 3.5 fusion.29
  285.3 0.4 copy-done.10
  285.7 0.9 fusion.31
  286.7 6.4 %convolution_convert_fusion.1 = bf16[1024,3584]{1,0:T(8,128)(2,1)} fusion(bf16[448,3584]{1,0:T(8,128)(2,1)S(1)} %copy-done, bf16[512,448]{0,1:T(8,128)(2,1)S(1)} %bitcast.87, bf16[512,448]{0,1:T(8,128)(2,1)S(1)} %bitcast.88), kind=kOutput, calls=%fused_computation.10 | convolution fusion | flops 3293839360 | bytes 11468800 | tf_op jit(solution)/shard_map/dot_general | solution.py:143
  293.1 0.6 copy-done.6
  293.7 0.6 broadcast_in_dim.119
  294.3 7.4 %all-to-all-start = ((s32[16,1,4]{2,1,0:T(1,128)}), s32[16,1,4]{2,1,0:T(1,128)S(1)}, u32[]{:S(2)}, u32[]{:S(2)}) async-start(s32[16,1,4]{2,1,0:T(1,128)} %broadcast_in_dim.119), calls=%async_computation.1 | async-start | bytes 16384 | tf_op jit(solution)/shard_map/all_to_all | solution.py:173
  301.7 0.1 convert_reduce_fusion
  301.8 0.2 reduce-window.8
  302.0 0.1 add_minimum_fusion
  302.1 0.1 min.22
  302.2 0.1 compare_and_fusion
  302.3 1.2 broadcast_in_dim.122
  303.6 4.0 broadcast_in_dim.123
  307.6 1.2 broadcast_in_dim.120
  308.8 3.9 broadcast_in_dim.121
  312.7 2.9 pad_maximum_fusion.2
  315.6 3.9 copy.26
  319.5 7.5 %gather_fusion.1 = bf16[1024,896]{1,0:T(8,128)(2,1)} fusion(bf16[1024,896]{1,0:T(8,128)(2,1)} %copy.26, s32[1024]{0:T(1024)S(1)} %broadcast_clamp_fusion), kind=kCustom, calls=%fused_computation.1 | custom fusion | bytes 3674112 | tf_op jit(solution)/shard_map/jit(_take)/gather | solution.py:167
  327.0 4.4 %gather.12 = bf16[16,4,14336]{2,1,0:T(4,128)(2,1)} reshape(bf16[1024,896]{1,0:T(8,128)(2,1)} %gather_fusion.1) | data formatting | bytes 3670016 | tf_op jit(solution)/shard_map/jit(_take)/gather | solution.py:167
  331.3 5.5 %select_select_fusion = bf16[16,4,14336]{2,1,0:T(4,128)(2,1)} fusion(pred[16,4,14336]{2,1,0:T(4,128)(4,1)} %broadcast_in_dim.121, pred[16,4,14336]{2,1,0:T(4,128)(4,1)} %broadcast_in_dim.123, bf16[16,4,14336]{2,1,0:T(4,128)(2,1)} %gather.12), kind=kLoop, calls=%fused_computation.48 | loop fusion | flops 1835008 | bytes 5505024 | tf_op jit(solution)/shard_map/jit(_where)/select_n | solution.py:168
  336.9 7.6 %all-to-all-start.1 = ((bf16[16,4,14336]{2,1,0:T(4,128)(2,1)}), bf16[16,4,14336]{2,1,0:T(4,128)(2,1)}, u32[]{:S(2)}, u32[]{:S(2)}) async-start(bf16[16,4,14336]{2,1,0:T(4,128)(2,1)} %select_select_fusion), calls=%async_computation.2 | async-start | bytes 3670016 | tf_op jit(solution)/shard_map/all_to_all | solution.py:172
  344.5 0.5 broadcast.262
  345.0 0.6 reduce.3
  345.7 0.1 eq.70
  345.8 28.0 %all-to-all-done.1 = bf16[16,4,14336]{2,1,0:T(4,128)(2,1)} async-done(((bf16[16,4,14336]{2,1,0:T(4,128)(2,1)}), bf16[16,4,14336]{2,1,0:T(4,128)(2,1)}, u32[]{:S(2)}, u32[]{:S(2)}) %all-to-all-start.1) | async-done | bytes 1835040 | tf_op jit(solution)/shard_map/all_to_all | solution.py:172
  373.8 3.8 reshape.321
  377.7 3.6 convolution_convert_fusion
  381.2 6.8 %reshape.322 = bf16[64,16,2,448]{3,2,1,0:T(2,128)(2,1)} reshape(bf16[64,14336]{1,0:T(8,128)(2,1)} %convolution_convert_fusion) | data formatting | bytes 3670016 | tf_op jit(solution)/shard_map/reshape | solution.py:183
  388.0 9.4 %reduce-scatter.2.cloned.1.call-done = bf16[128,3584]{1,0:T(8,128)(2,1)} async-done(((bf16[1024,3584]{1,0:T(8,128)(2,1)}), bf16[128,3584]{1,0:T(8,128)(2,1)}) %reduce-scatter.2.cloned.1.call-update) | async-done | bytes 917520 | tf_op jit(solution)/shard_map/reduce_scatter | solution.py:142
  (44 shorter events, 0.4 us)
Async XLA Ops:
  7.2 279.5 %copy-start = (bf16[448,3584]{1,0:T(8,128)(2,1)S(1)}, bf16[448,3584]{1,0:T(8,128)(2,1)}, u32[]{:S(2)}) copy-start(bf16[448,3584]{1,0:T(8,128)(2,1)} %param.23) | copy-start | bytes 9633796
  7.2 7.1 %copy-start.5 = (f32[7168]{0:T(1024)S(1)}, f32[7168]{0:T(1024)}, u32[]{:S(2)}) copy-start(f32[7168]{0:T(1024)} %param.17) | copy-start | bytes 86020
  7.2 194.5 %all-gather.2.cloned.1.call-start = ((), (), s32[]{:S(2)}) async-start(), calls=%async_computation.3 | async-start | bytes 16515072 | tf_op jit(solution)/shard_map/all_gather | solution.py:97
  20.0 377.3 %reduce-scatter.2.cloned.1.call-start = ((), (), s32[]{:S(2)}) async-start(), calls=%async_computation.4 | async-start | bytes 8257536 | tf_op jit(solution)/shard_map/reduce_scatter | solution.py:142
  23.6 54.9 %copy-start.1 = (bf16[448,1344]{1,0:T(8,128)(2,1)S(1)}, bf16[448,1344]{1,0:T(8,128)(2,1)}, u32[]{:S(2)}) copy-start(bf16[448,1344]{1,0:T(8,128)(2,1)} %concatenate.14) | copy-start | bytes 3612676
  23.6 50.6 %collective-permute-start = (bf16[448,1344]{1,0:T(8,128)(2,1)}, bf16[448,1344]{1,0:T(8,128)(2,1)S(1)}, u32[]{:S(2)}, u32[]{:S(2)}) collective-permute-start(bf16[448,1344]{1,0:T(8,128)(2,1)} %concatenate.14), channel_id=1, source_target_pairs={{0,16},{8,24},{16,0},{24,8},{32,48},{40,56},{48,32},{56,40},{64,80... | collective-permute-start | bytes 3612680 | tf_op jit(solution)/shard_map/ppermute | solution.py:62
  75.8 55.9 %collective-permute-start.1 = (bf16[2,448,1344]{2,1,0:T(8,128)(2,1)S(1)}, bf16[2,448,1344]{2,1,0:T(8,128)(2,1)S(1)}, u32[]{:S(2)}, u32[]{:S(2)}) collective-permute-start(bf16[2,448,1344]{2,1,0:T(8,128)(2,1)S(1)} %pad_maximum_fusion), channel_id=1, source_target_pairs={{0,32},{8,40},{16,48},{24,56},{32,64},{40,72},{48,80},{56,88},{64,... | collective-permute-start | bytes 7225352 | tf_op jit(solution)/shard_map/ppermute | solution.py:63
  76.9 55.0 %collective-permute-start.2 = (bf16[2,448,1344]{2,1,0:T(8,128)(2,1)S(1)}, bf16[2,448,1344]{2,1,0:T(8,128)(2,1)S(1)}, u32[]{:S(2)}, u32[]{:S(2)}) collective-permute-start(bf16[2,448,1344]{2,1,0:T(8,128)(2,1)S(1)} %pad_maximum_fusion), channel_id=1, source_target_pairs={{0,96},{8,104},{16,112},{24,120},{32,0},{40,8},{48,16},{56,24},{64... | collective-permute-start | bytes 7225352 | tf_op jit(solution)/shard_map/ppermute | solution.py:64
  131.8 28.2 %collective-permute-start.3 = (bf16[448,1344]{1,0:T(8,128)(2,1)S(1)}, bf16[448,1344]{1,0:T(8,128)(2,1)S(1)}, u32[]{:S(2)}, u32[]{:S(2)}) collective-permute-start(bf16[448,1344]{1,0:T(8,128)(2,1)S(1)} %slice_bitcast_fusion.1), channel_id=1, source_target_pairs={{0,32},{8,40},{16,48},{24,56},{32,64},{40,72},{48,80},{56,88},{64,... | collective-permute-start | bytes 3612680 | tf_op jit(solution)/shard_map/ppermute | solution.py:66
  132.0 29.1 %collective-permute-start.4 = (bf16[448,1344]{1,0:T(8,128)(2,1)S(1)}, bf16[448,1344]{1,0:T(8,128)(2,1)S(1)}, u32[]{:S(2)}, u32[]{:S(2)}) collective-permute-start(bf16[448,1344]{1,0:T(8,128)(2,1)S(1)} %slice_bitcast_fusion), channel_id=1, source_target_pairs={{0,96},{8,104},{16,112},{24,120},{32,0},{40,8},{48,16},{56,24},{64... | collective-permute-start | bytes 3612680 | tf_op jit(solution)/shard_map/ppermute | solution.py:66
  139.3 27.2 %copy-start.7 = (s32[16]{0:T(128)S(1)}, s32[16]{0:T(128)}, u32[]{:S(2)}) copy-start(s32[16]{0:T(128)} %constant.118.clone) | copy-start | bytes 196
  139.3 27.2 %copy-start.8 = (s32[16]{0:T(128)S(1)}, s32[16]{0:T(128)}, u32[]{:S(2)}) copy-start(s32[16]{0:T(128)} %constant.117.clone) | copy-start | bytes 196
  139.3 27.2 %copy-start.9 = (s32[16]{0:T(128)S(1)}, s32[16]{0:T(128)}, u32[]{:S(2)}) copy-start(s32[16]{0:T(128)} %constant.116.clone) | copy-start | bytes 196
  139.3 27.2 %copy-start.4 = (s32[1024]{0:T(1024)S(1)}, s32[1024]{0:T(1024)}, u32[]{:S(2)}) copy-start(s32[1024]{0:T(1024)} %param.24) | copy-start | bytes 12292
  162.3 82.0 %collective-permute-start.5 = (bf16[8,448,1344]{2,1,0:T(8,128)(2,1)}, bf16[8,448,1344]{2,1,0:T(8,128)(2,1)}, u32[]{:S(2)}, u32[]{:S(2)}) collective-permute-start(bf16[8,448,1344]{2,1,0:T(8,128)(2,1)} %bitcast_dynamic-update-slice_fusion), channel_id=1, source_target_pairs={{0,8},{8,0},{16,24},{24,16},{32,40},{40,32},{48,56},{56,48},{64,72... | collective-permute-start | bytes 28901384 | tf_op jit(solution)/shard_map/ppermute | solution.py:69
  244.3 18.5 %copy-start.3 = (bf16[3,128,448]{1,2,0:T(8,128)(2,1)S(1)}, bf16[3,128,448]{1,2,0:T(8,128)(2,1)}, u32[]{:S(2)}) copy-start(bf16[3,128,448]{1,2,0:T(8,128)(2,1)} %param.22) | copy-start | bytes 1032196
  281.8 3.5 copy-start.2
  281.8 4.0 copy-start.10
  293.0 0.7 copy-start.6
  294.3 42.6 %all-to-all-start = ((s32[16,1,4]{2,1,0:T(1,128)}), s32[16,1,4]{2,1,0:T(1,128)S(1)}, u32[]{:S(2)}, u32[]{:S(2)}) async-start(s32[16,1,4]{2,1,0:T(1,128)} %broadcast_in_dim.119), calls=%async_computation.1 | async-start | bytes 16384 | tf_op jit(solution)/shard_map/all_to_all | solution.py:173
  336.9 36.9 %all-to-all-start.1 = ((bf16[16,4,14336]{2,1,0:T(4,128)(2,1)}), bf16[16,4,14336]{2,1,0:T(4,128)(2,1)}, u32[]{:S(2)}, u32[]{:S(2)}) async-start(bf16[16,4,14336]{2,1,0:T(4,128)(2,1)} %select_select_fusion), calls=%async_computation.2 | async-start | bytes 3670016 | tf_op jit(solution)/shard_map/all_to_all | solution.py:172
Sparse Core Ops, SparseCore 0:
  20.2 181.5 all-gather.1
  293.2 104.1 reduce-scatter.1

commit v2 on v1

--- a/solution.py
+++ b/solution.py
@@ -94,27 +94,23 @@
     head_cols = query_projection_weight.shape[1]
     block_rows = query_projection_weight.shape[0]
     normalized_hidden = normalize(hidden_state_input, token_embedding_input, input_norm_gain)
-    stream_in = lax.all_gather(normalized_hidden, "tensor", axis=0, tiled=True)
-    adapter_update = jnp.dot(
-        stream_in, adapter_down_maps, preferred_element_type=jnp.float32
-    ).astype(jnp.bfloat16)
     weight_shard = jnp.concatenate(
         [query_projection_weight, key_projection_weight, value_projection_weight], 1
     )
     mine, other, order = gather_weights(weight_shard)
-    stream = stream_in.shape[0]
-    blocks = stream_in.reshape(stream, -1, block_rows)
-    permuted = jnp.take(blocks, order, axis=1)
-    half = mine.shape[0] * block_rows
-    folded_all = jnp.dot(
-        permuted[:, : mine.shape[0]].reshape(stream, half),
-        mine.reshape(half, 3 * head_cols),
-        preferred_element_type=jnp.float32,
-    ) + jnp.dot(
-        permuted[:, mine.shape[0] :].reshape(stream, half),
-        other.reshape(half, 3 * head_cols),
-        preferred_element_type=jnp.float32,
-    )
+    place = jnp.zeros_like(order).at[order].set(jnp.arange(order.shape[0], dtype=jnp.int32))
+    gathered = jnp.take(jnp.concatenate([mine, other], 0), place, axis=0)
+    full_rows = gathered.shape[0] * block_rows
+    augmented = jnp.concatenate(
+        [gathered.reshape(full_rows, 3 * head_cols), adapter_down_maps], 1
+    )
+    split = hidden_state_input.shape[1]
+    folded_all = None
+    for lo, hi in ((0, split), (split, full_rows)):
+        part = lax.all_gather(normalized_hidden[:, lo:hi], "tensor", axis=0, tiled=True)
+        term = jnp.dot(part, augmented[lo:hi], preferred_element_type=jnp.float32)
+        folded_all = term if folded_all is None else folded_all + term
+    adapter_update = folded_all[:, 3 * head_cols :].astype(jnp.bfloat16)
     folded = [folded_all[:, k * head_cols : (k + 1) * head_cols] for k in range(3)]
     projected = []
     for adapter_selector in range(3):
@@ -131,6 +127,40 @@
     stream = query.shape[0]
     position = jnp.arange(stream, dtype=jnp.int32)
     live = live_token_length[0]
+    requests = request_cache_row.shape[0]
+    longest = stream // requests
+    groups = lax.axis_size("dp")
+    piece_len = longest // groups
+    numbers = jnp.arange(requests, dtype=jnp.int32)
+    membership = ((segment[:, None] == numbers[None, :]) & (position < live)[:, None]).astype(
+        jnp.int32
+    )
+    lengths = jnp.sum(membership, axis=0)
+    starts = jnp.cumsum(lengths) - lengths
+    offsets = (
+        jnp.arange(groups, dtype=jnp.int32)[:, None] * piece_len
+        + jnp.arange(piece_len, dtype=jnp.int32)[None, :]
+    )
+    source_rows = jnp.minimum(starts[None, :, None] + offsets[:, None, :], stream - 1)
+    alive_mask = offsets[:, None, :] < lengths[None, :, None]
+    stacked = jnp.stack([keys, values], 1).reshape(stream, 2 * head_cols)
+    taken = jnp.take(stacked, source_rows.reshape(-1), axis=0)
+    taken = jnp.where(alive_mask.reshape(-1)[:, None], taken, jnp.zeros((), jnp.bfloat16))
+    taken = taken.reshape(groups, requests, piece_len * 2 * head_cols)
+    row_send = jnp.broadcast_to(request_cache_row[None, :], (groups, requests))
+    received, received_rows = (
+        lax.all_to_all(taken, "dp", split_axis=0, concat_axis=0, tiled=True),
+        lax.all_to_all(row_send, "dp", split_axis=0, concat_axis=0, tiled=True),
+    )
+    total_reqs = groups * requests
+    placing = (
+        received_rows.reshape(-1)[:, None] == jnp.arange(total_reqs, dtype=jnp.int32)[None, :]
+    ).astype(jnp.bfloat16)
+    flat_received = received.reshape(total_reqs, piece_len * 2 * head_cols)
+    cache_rows = lax.dot_general(
+        placing, flat_received, (((0,), (0,)), ((), ())), preferred_element_type=jnp.float32
+    )
+    kv_cache = cache_rows.astype(jnp.bfloat16).reshape(total_reqs, piece_len, 2, head_cols)
     block = min(512, stream)
     attended_parts = []
     for block_index in range(stream // block):
@@ -147,40 +177,6 @@
         scatter_dimension=0,
         tiled=True,
     )
-    requests = request_cache_row.shape[0]
-    longest = stream // requests
-    groups = lax.axis_size("dp")
-    piece_len = longest // groups
-    numbers = jnp.arange(requests, dtype=jnp.int32)
-    membership = ((segment[:, None] == numbers[None, :]) & (position < live)[:, None]).astype(
-        jnp.int32
-    )
-    lengths = jnp.sum(membership, axis=0)
-    starts = jnp.cumsum(lengths) - lengths
-    offsets = (
-        jnp.arange(groups, dtype=jnp.int32)[:, None] * piece_len
-        + jnp.arange(piece_len, dtype=jnp.int32)[None, :]
-    )
-    source_rows = jnp.minimum(starts[None, :, None] + offsets[:, None, :], stream - 1)
-    alive_mask = offsets[:, None, :] < lengths[None, :, None]
-    stacked = jnp.stack([keys, values], 1).reshape(stream, 2 * head_cols)
-    taken = jnp.take(stacked, source_rows.reshape(-1), axis=0)
-    taken = jnp.where(alive_mask.reshape(-1)[:, None], taken, jnp.zeros((), jnp.bfloat16))
-    taken = taken.reshape(groups, requests, piece_len * 2 * head_cols)
-    row_send = jnp.broadcast_to(request_cache_row[None, :], (groups, requests))
-    received, received_rows = (
-        lax.all_to_all(taken, "dp", split_axis=0, concat_axis=0, tiled=True),
-        lax.all_to_all(row_send, "dp", split_axis=0, concat_axis=0, tiled=True),
-    )
-    total_reqs = groups * requests
-    placing = (
-        received_rows.reshape(-1)[:, None] == jnp.arange(total_reqs, dtype=jnp.int32)[None, :]
-    ).astype(jnp.bfloat16)
-    flat_received = received.reshape(total_reqs, piece_len * 2 * head_cols)
-    cache_rows = lax.dot_general(
-        placing, flat_received, (((0,), (0,)), ((), ())), preferred_element_type=jnp.float32
-    )
-    kv_cache = cache_rows.astype(jnp.bfloat16).reshape(total_reqs, piece_len, 2, head_cols)
     return (block_out, kv_cache)
 
 

time: 411 us -> 403 us (0.981)
  waiting for transfers between devices: 190 us -> 147 us
  local copies, waits for them, and re-layouts: 68.9 us -> 83.7 us
  other arithmetic: 21.6 us -> 36.3 us
    all_gather x1 -> x2, waiting for transfers between devices: 33 us -> 1.72 us  [body(): lax.all_gather(normalized_hidden[:, lo:hi], 'tensor', axis=0, tiled=True)]
    select_n x0 -> x3, other arithmetic: none -> 18.1 us  [the longest x2 18.1 us: body(): gathered = jnp.take(jnp.concatenate([mine, other], 0), place, axis=0)]
    ppermute x1, waiting for transfers between devices: 46.9 us -> 33.4 us  [gather_weights(): pair = jnp.stack([weight_shard, lax.ppermute(weight_shard, 'dp', to_yh)])]
    ppermute x1, waiting for transfers between devices: 0.01 us -> 10.6 us  [gather_weights(): other = lax.ppermute(mine, 'dp', to_core)]
    concatenate x0 -> x1, local copies, waits for them, and re-layouts: none -> 8.4 us  [body(): gathered = jnp.take(jnp.concatenate([mine, other], 0), place, axis=0)]
    ppermute x1, waiting for transfers between devices: 52 us -> 46.6 us  [gather_weights(): from_prev = lax.ppermute(pair, 'dp', to_next)]
    dot_general x3 -> x2, matrix products: 48.6 us -> 52.3 us  [body(): term = jnp.dot(part, augmented[lo:hi], preferred_element_type=jnp.float32)]
    unnamed x29 -> x37, local copies, waits for them, and re-layouts: 12.6 us -> 12.7 us
  transfers between devices with their start and end apart: 10 -> 11, of which waited for: 6 -> 7; matrix products, arithmetic and copies ran while one was open for 27% -> 36% of each run, Pallas kernels for 0% -> 0%
where the time goes in v2:
time: 403 us; the launch traced here: 397 us
  waiting for transfers between devices  147 us (36%)
  matrix products  84.9 us (21%)
  local copies, waits for them, and re-layouts  83.7 us (21%)
  other arithmetic  36.3 us (9%)
  starting transfers between devices  29.6 us (7%)
  between operations  15 us (4%)
    dot_general x2, matrix products, body(): term = jnp.dot(part, augmented[lo:hi], preferred_element_type=jnp.float32)  52.3 us
    ppermute x1, waiting for transfers between devices, gather_weights(): from_prev = lax.ppermute(pair, 'dp', to_next)  46.6 us
    ppermute x1, waiting for transfers between devices, gather_weights(): pair = jnp.stack([weight_shard, lax.ppermute(weight_shard, 'dp', to_yh)])  33.4 us
    all_to_all x1, waiting for transfers between devices, body(): lax.all_to_all(taken, 'dp', split_axis=0, concat_axis=0, tiled=True)  28.1 us
    select_n x2, other arithmetic, body(): gathered = jnp.take(jnp.concatenate([mine, other], 0), place, axis=0)  18.1 us
    ppermute x1, waiting for transfers between devices, gather_weights(): lax.ppermute(from_prev[0], 'dp', to_next)  17.9 us
    gather x1, local copies, waits for them, and re-layouts, body(): gathered = jnp.take(jnp.concatenate([mine, other], 0), place, axis=0)  15.5 us
    unnamed x37, local copies, waits for them, and re-layouts  12.7 us
  transfers between devices with their start and end apart: 11, of which 7 were waited for; matrix products, arithmetic and copies ran while one was open for 36% of the time, Pallas kernels for 0%

profile of v2, /device:TPU:1, one launch (start us, length us, event | category | flops | bytes accessed | tf_op | source)
XLA Modules:
  0.0 397.0 jit_solution(2680700329590757513)
XLA Ops:
  7.2 3.7 concatenate.21
  10.9 3.7 collective-permute-start
  14.6 1.9 fusion.10
  16.6 2.0 fusion.12
  18.5 1.3 fusion.65
  20.0 33.4 %collective-permute-done = bf16[448,1344]{1,0:T(8,128)(2,1)} collective-permute-done((bf16[448,1344]{1,0:T(8,128)(2,1)}, bf16[448,1344]{1,0:T(8,128)(2,1)}, u32[]{:S(2)}, u32[]{:S(2)}) %collective-permute-start) | collective-permute-done | bytes 1204256 | tf_op jit(solution)/shard_map/ppermute | solution.py:62
  53.3 2.0 pad_maximum_fusion.2
  55.3 1.1 collective-permute-start.1
  56.5 1.6 collective-permute-start.2
  58.1 1.7 constant_dynamic-update-slice_fusion.3
  59.8 2.9 constant_dynamic-update-slice_fusion.2
  62.7 46.6 %collective-permute-done.1 = bf16[2,448,1344]{2,1,0:T(8,128)(2,1)S(1)} collective-permute-done((bf16[2,448,1344]{2,1,0:T(8,128)(2,1)S(1)}, bf16[2,448,1344]{2,1,0:T(8,128)(2,1)S(1)}, u32[]{:S(2)}, u32[]{:S(2)}) %collective-permute-start.1) | collective-permute-done | bytes 2408480 | tf_op jit(solution)/shard_map/ppermute | solution.py:63
  109.6 2.7 collective-permute-start.4
  112.3 2.7 constant_dynamic-update-slice_fusion.1
  114.9 2.6 constant_dynamic-update-slice_fusion
  117.6 17.9 %collective-permute-done.3 = bf16[448,1344]{1,0:T(8,128)(2,1)S(1)} collective-permute-done((bf16[448,1344]{1,0:T(8,128)(2,1)S(1)}, bf16[448,1344]{1,0:T(8,128)(2,1)S(1)}, u32[]{:S(2)}, u32[]{:S(2)}) %collective-permute-start.3) | collective-permute-done | bytes 1204256 | tf_op jit(solution)/shard_map/ppermute | solution.py:66
  135.5 1.7 bitcast_dynamic-update-slice_fusion.3
  137.2 1.6 bitcast_dynamic-update-slice_fusion.1
  138.8 5.4 %collective-permute-start.5 = (bf16[8,448,1344]{2,1,0:T(8,128)(2,1)}, bf16[8,448,1344]{2,1,0:T(8,128)(2,1)}, u32[]{:S(2)}, u32[]{:S(2)}) collective-permute-start(bf16[8,448,1344]{2,1,0:T(8,128)(2,1)} %get-tuple-element.8), channel_id=1, source_target_pairs={{0,8},{8,0},{16,24},{24,16},{32,40},{40,32},{48,56},{56,48},{64,72... | collective-permute-start | bytes 28901384 | tf_op jit(solution)/shard_map/ppermute | solution.py:69
  144.4 1.1 scatter_custom_fusion
  145.6 0.1 broadcast_in_dim.120
  146.5 0.6 broadcast_compare_fusion.1
  147.1 2.1 fusion.22
  149.2 10.6 %collective-permute-done.5 = bf16[8,448,1344]{2,1,0:T(8,128)(2,1)} collective-permute-done((bf16[8,448,1344]{2,1,0:T(8,128)(2,1)}, bf16[8,448,1344]{2,1,0:T(8,128)(2,1)}, u32[]{:S(2)}, u32[]{:S(2)}) %collective-permute-start.5) | collective-permute-done | bytes 9633824 | tf_op jit(solution)/shard_map/ppermute | solution.py:69
  159.8 8.4 %constant_dynamic-update-slice_fusion.4 = bf16[16,448,1344]{2,1,0:T(8,128)(2,1)} fusion(bf16[16,448,1344]{2,1,0:T(8,128)(2,1)} %get-tuple-element.9, bf16[8,448,1344]{2,1,0:T(8,128)(2,1)} %collective-permute-done.5), kind=kLoop, calls=%fused_computation.85 | loop fusion | bytes 20185088 | tf_op jit(solution)/shard_map/concatenate | solution.py:102
  168.2 15.5 %gather_fusion = bf16[16,448,1344]{2,1,0:T(8,128)(2,1)} fusion(bf16[16,448,1344]{2,1,0:T(8,128)(2,1)} %constant_dynamic-update-slice_fusion.4, s32[1024]{0:T(1024)S(1)} %pad_clamp_fusion), kind=kCustom, calls=%fused_computation | custom fusion | bytes 38535232 | tf_op jit(solution)/shard_map/jit(_take)/gather | solution.py:102
  183.6 18.1 %bitcast_select_fusion = bf16[7168,1344]{1,0:T(8,128)(2,1)} fusion(bf16[16,448,1344]{2,1,0:T(8,128)(2,1)} %gather_fusion, pred[7168]{0:T(1024)(128)(4,1)S(1)} %broadcast_in_dim.120), kind=kLoop, calls=%fused_computation.7 | loop fusion | flops 9633792 | bytes 38542336 | tf_op jit(solution)/shard_map/jit(_take)/select_n | solution.py:102
  201.7 25.4 %fusion.5 = f32[1024,1728]{0,1:T(8,128)} fusion(bf16[1024,3584]{1,0:T(8,128)(2,1)} %all-gather.5.cloned.1.call-done, bf16[7168,384]{1,0:T(8,128)(2,1)} %param.21, bf16[7168,1344]{1,0:T(8,128)(2,1)} %bitcast_select_fusion), kind=kOutput, calls=%fused_computation.12 | convolution fusion | flops 12708347904 | bytes 39190528 | tf_op jit(solution)/shard_map/dot_general | solution.py:111
  227.2 1.7 all-gather.3.cloned.1.call-done
  228.9 26.8 %fusion.68 = (bf16[1024,1728]{0,1:T(8,128)(2,1)}, f32[1024,1728]{0,1:T(8,128)}) fusion(f32[1024,1728]{0,1:T(8,128)} %fusion.5, bf16[1024,3584]{1,0:T(8,128)(2,1)} %all-gather.3.cloned.1.call-done, bf16[7168,1344]{1,0:T(8,128)(2,1)} %bitcast_select_fusion, bf16[7168,384]{1,0:T(8,128)(2,1)} %param.21), kind=kOutput, calls=%fused_computation.127 | convolution fusion | flops 12711886848 | bytes 49807360 | tf_op jit(solution)/shard_map/dot_general | solution.py:111
  255.7 2.9 fusion.27
  258.6 3.0 fusion.29
  261.6 2.0 fusion.28
  263.6 1.0 fusion.66
  264.6 5.2 %fusion.70 = (f32[2,512]{1,0:T(2,128)S(1)}, f32[2,512,1024]{2,1,0:T(8,128)}) fusion(pred[512,1024]{1,0:T(8,128)(4,1)} %get-tuple-element.20, bf16[512,2,224]{0,2,1:T(8,128)(2,1)} %bitcast.74, bf16[1024,2,224]{0,2,1:T(8,128)(2,1)} %bitcast.67), kind=kOutput, calls=%fused_computation.129 | convolution fusion | flops 473957376 | bytes 6098944 | tf_op jit(solution)/shard_map/sub | solution.py:37
  269.8 5.2 %fusion.69 = (f32[2,512]{1,0:T(2,128)S(1)}, f32[2,512,1024]{2,1,0:T(8,128)}) fusion(pred[512,1024]{1,0:T(8,128)(4,1)} %get-tuple-element.21, bf16[512,2,224]{0,2,1:T(8,128)(2,1)} %bitcast.73, bf16[1024,2,224]{0,2,1:T(8,128)(2,1)} %bitcast.68), kind=kOutput, calls=%fused_computation.128 | convolution fusion | flops 473957376 | bytes 6098944 | tf_op jit(solution)/shard_map/sub | solution.py:37
  275.0 3.5 fusion.33
  278.6 0.4 copy-done.15
  279.0 0.9 fusion.31
  280.0 6.3 %convolution_convert_fusion.1 = bf16[1024,3584]{1,0:T(8,128)(2,1)} fusion(bf16[448,3584]{1,0:T(8,128)(2,1)S(1)} %copy-done, bf16[512,448]{0,1:T(8,128)(2,1)S(1)} %bitcast.78, bf16[512,448]{0,1:T(8,128)(2,1)S(1)} %bitcast.77), kind=kOutput, calls=%fused_computation.14 | convolution fusion | flops 3293839360 | bytes 11468800 | tf_op jit(solution)/shard_map/dot_general | solution.py:173
  286.3 0.6 copy-done.9
  286.9 0.6 broadcast_in_dim.129
  287.5 7.3 %all-to-all-start = ((s32[16,1,4]{2,1,0:T(1,128)}), s32[16,1,4]{2,1,0:T(1,128)S(1)}, u32[]{:S(2)}, u32[]{:S(2)}) async-start(s32[16,1,4]{2,1,0:T(1,128)} %broadcast_in_dim.129), calls=%async_computation.1 | async-start | bytes 16384 | tf_op jit(solution)/shard_map/all_to_all | solution.py:153
  294.8 0.1 convert_reduce_fusion
  294.9 0.2 reduce-window.8
  295.3 0.1 min.22
  295.4 0.1 compare_and_fusion
  295.5 1.2 broadcast_in_dim.130
  296.7 4.0 broadcast_in_dim.131
  300.7 1.2 broadcast_in_dim.132
  301.9 3.9 broadcast_in_dim.133
  305.9 2.9 pad_maximum_fusion.4
  308.8 3.8 copy.20
  312.6 7.5 %gather_fusion.1 = bf16[1024,896]{1,0:T(8,128)(2,1)} fusion(bf16[1024,896]{1,0:T(8,128)(2,1)} %copy.20, s32[1024]{0:T(1024)S(1)} %broadcast_clamp_fusion), kind=kCustom, calls=%fused_computation.1 | custom fusion | bytes 3674112 | tf_op jit(solution)/shard_map/jit(_take)/gather | solution.py:147
  320.1 4.4 %gather.15 = bf16[16,4,14336]{2,1,0:T(4,128)(2,1)} reshape(bf16[1024,896]{1,0:T(8,128)(2,1)} %gather_fusion.1) | data formatting | bytes 3670016 | tf_op jit(solution)/shard_map/jit(_take)/gather | solution.py:147
  324.5 5.6 %select_select_fusion = bf16[16,4,14336]{2,1,0:T(4,128)(2,1)} fusion(pred[16,4,14336]{2,1,0:T(4,128)(4,1)} %broadcast_in_dim.131, pred[16,4,14336]{2,1,0:T(4,128)(4,1)} %broadcast_in_dim.133, bf16[16,4,14336]{2,1,0:T(4,128)(2,1)} %gather.15), kind=kLoop, calls=%fused_computation.52 | loop fusion | flops 1835008 | bytes 5505024 | tf_op jit(solution)/shard_map/jit(_where)/select_n | solution.py:148
  330.0 7.6 %all-to-all-start.1 = ((bf16[16,4,14336]{2,1,0:T(4,128)(2,1)}), bf16[16,4,14336]{2,1,0:T(4,128)(2,1)}, u32[]{:S(2)}, u32[]{:S(2)}) async-start(bf16[16,4,14336]{2,1,0:T(4,128)(2,1)} %select_select_fusion), calls=%async_computation.2 | async-start | bytes 3670016 | tf_op jit(solution)/shard_map/all_to_all | solution.py:152
  337.6 0.5 broadcast.259
  338.1 0.6 reduce.3
  338.8 28.1 %all-to-all-done.1 = bf16[16,4,14336]{2,1,0:T(4,128)(2,1)} async-done(((bf16[16,4,14336]{2,1,0:T(4,128)(2,1)}), bf16[16,4,14336]{2,1,0:T(4,128)(2,1)}, u32[]{:S(2)}, u32[]{:S(2)}) %all-to-all-start.1) | async-done | bytes 1835040 | tf_op jit(solution)/shard_map/all_to_all | solution.py:152
  366.9 3.8 reshape.316
  370.8 3.6 convolution_convert_fusion
  374.3 6.8 %reshape.317 = bf16[64,16,2,448]{3,2,1,0:T(2,128)(2,1)} reshape(bf16[64,14336]{1,0:T(8,128)(2,1)} %convolution_convert_fusion) | data formatting | bytes 3670016 | tf_op jit(solution)/shard_map/reshape | solution.py:163
  381.1 9.1 %reduce-scatter.2.cloned.1.call-done = bf16[128,3584]{1,0:T(8,128)(2,1)} async-done(((bf16[1024,3584]{1,0:T(8,128)(2,1)}), bf16[128,3584]{1,0:T(8,128)(2,1)}) %reduce-scatter.2.cloned.1.call-update) | async-done | bytes 917520 | tf_op jit(solution)/shard_map/reduce_scatter | solution.py:172
  (63 shorter events, 0.9 us)
Async XLA Ops:
  7.2 272.8 %copy-start = (bf16[448,3584]{1,0:T(8,128)(2,1)S(1)}, bf16[448,3584]{1,0:T(8,128)(2,1)}, u32[]{:S(2)}) copy-start(bf16[448,3584]{1,0:T(8,128)(2,1)} %param.23) | copy-start | bytes 9633796
  7.2 9.4 %copy-start.6 = (f32[7168]{0:T(1024)S(1)}, f32[7168]{0:T(1024)}, u32[]{:S(2)}) copy-start(f32[7168]{0:T(1024)} %param.17) | copy-start | bytes 86020
  7.2 194.5 %all-gather.5.cloned.1.call-start = ((), (), s32[]{:S(2)}) async-start(), calls=%async_computation.4 | async-start | bytes 8257536 | tf_op jit(solution)/shard_map/all_gather | solution.py:110
  10.9 42.4 %collective-permute-start = (bf16[448,1344]{1,0:T(8,128)(2,1)}, bf16[448,1344]{1,0:T(8,128)(2,1)}, u32[]{:S(2)}, u32[]{:S(2)}) collective-permute-start(bf16[448,1344]{1,0:T(8,128)(2,1)} %concatenate.21), channel_id=1, source_target_pairs={{0,16},{8,24},{16,0},{24,8},{32,48},{40,56},{48,32},{56,40},{64,80... | collective-permute-start | bytes 3612680 | tf_op jit(solution)/shard_map/ppermute | solution.py:62
  19.9 209.0 %all-gather.3.cloned.1.call-start = ((), (), s32[]{:S(2)}) async-start(), calls=%async_computation.3 | async-start | bytes 8257536 | tf_op jit(solution)/shard_map/all_gather | solution.py:110
  19.9 38.1 %copy-start.1 = (bf16[448,1344]{1,0:T(8,128)(2,1)S(1)}, bf16[448,1344]{1,0:T(8,128)(2,1)}, u32[]{:S(2)}) copy-start(bf16[448,1344]{1,0:T(8,128)(2,1)} %concatenate.21) | copy-start | bytes 3612676
  55.3 53.9 %collective-permute-start.1 = (bf16[2,448,1344]{2,1,0:T(8,128)(2,1)S(1)}, bf16[2,448,1344]{2,1,0:T(8,128)(2,1)S(1)}, u32[]{:S(2)}, u32[]{:S(2)}) collective-permute-start(bf16[2,448,1344]{2,1,0:T(8,128)(2,1)S(1)} %pad_maximum_fusion.2), channel_id=1, source_target_pairs={{0,32},{8,40},{16,48},{24,56},{32,64},{40,72},{48,80},{56,88},{64,... | collective-permute-start | bytes 7225352 | tf_op jit(solution)/shard_map/ppermute | solution.py:63
  56.5 53.0 %collective-permute-start.2 = (bf16[2,448,1344]{2,1,0:T(8,128)(2,1)S(1)}, bf16[2,448,1344]{2,1,0:T(8,128)(2,1)S(1)}, u32[]{:S(2)}, u32[]{:S(2)}) collective-permute-start(bf16[2,448,1344]{2,1,0:T(8,128)(2,1)S(1)} %pad_maximum_fusion.2), channel_id=1, source_target_pairs={{0,96},{8,104},{16,112},{24,120},{32,0},{40,8},{48,16},{56,24},{64... | collective-permute-start | bytes 7225352 | tf_op jit(solution)/shard_map/ppermute | solution.py:64
  109.4 26.1 %collective-permute-start.3 = (bf16[448,1344]{1,0:T(8,128)(2,1)S(1)}, bf16[448,1344]{1,0:T(8,128)(2,1)S(1)}, u32[]{:S(2)}, u32[]{:S(2)}) collective-permute-start(bf16[448,1344]{1,0:T(8,128)(2,1)S(1)} %slice_bitcast_fusion.1), channel_id=1, source_target_pairs={{0,32},{8,40},{16,48},{24,56},{32,64},{40,72},{48,80},{56,88},{64,... | collective-permute-start | bytes 3612680 | tf_op jit(solution)/shard_map/ppermute | solution.py:66
  109.6 27.6 %collective-permute-start.4 = (bf16[448,1344]{1,0:T(8,128)(2,1)S(1)}, bf16[448,1344]{1,0:T(8,128)(2,1)S(1)}, u32[]{:S(2)}, u32[]{:S(2)}) collective-permute-start(bf16[448,1344]{1,0:T(8,128)(2,1)S(1)} %slice_bitcast_fusion), channel_id=1, source_target_pairs={{0,96},{8,104},{16,112},{24,120},{32,0},{40,8},{48,16},{56,24},{64... | collective-permute-start | bytes 3612680 | tf_op jit(solution)/shard_map/ppermute | solution.py:66
  135.5 8.9 %copy-start.10 = (s32[16]{0:T(128)S(1)}, s32[16]{0:T(128)}, u32[]{:S(2)}) copy-start(s32[16]{0:T(128)} %constant.118.clone) | copy-start | bytes 196
  135.5 8.9 %copy-start.11 = (s32[16]{0:T(128)S(1)}, s32[16]{0:T(128)}, u32[]{:S(2)}) copy-start(s32[16]{0:T(128)} %constant.119.clone) | copy-start | bytes 196
  135.5 8.9 %copy-start.12 = (s32[16]{0:T(128)S(1)}, s32[16]{0:T(128)}, u32[]{:S(2)}) copy-start(s32[16]{0:T(128)} %constant.120.clone) | copy-start | bytes 196
  135.5 11.0 %copy-start.4 = (s32[1024]{0:T(1024)S(1)}, s32[1024]{0:T(1024)}, u32[]{:S(2)}) copy-start(s32[1024]{0:T(1024)} %param.24) | copy-start | bytes 12292
  138.8 20.9 %collective-permute-start.5 = (bf16[8,448,1344]{2,1,0:T(8,128)(2,1)}, bf16[8,448,1344]{2,1,0:T(8,128)(2,1)}, u32[]{:S(2)}, u32[]{:S(2)}) collective-permute-start(bf16[8,448,1344]{2,1,0:T(8,128)(2,1)} %get-tuple-element.8), channel_id=1, source_target_pairs={{0,8},{8,0},{16,24},{24,16},{32,40},{40,32},{48,56},{56,48},{64,72... | collective-permute-start | bytes 28901384 | tf_op jit(solution)/shard_map/ppermute | solution.py:69
  144.2 246.0 %reduce-scatter.2.cloned.1.call-start = ((), (), s32[]{:S(2)}) async-start(), calls=%async_computation.5 | async-start | bytes 8257536 | tf_op jit(solution)/shard_map/reduce_scatter | solution.py:172
  146.4 2.8 copy-start.7
  227.2 28.5 %copy-start.3 = (bf16[3,128,448]{1,2,0:T(8,128)(2,1)S(1)}, bf16[3,128,448]{1,2,0:T(8,128)(2,1)}, u32[]{:S(2)}) copy-start(bf16[3,128,448]{1,2,0:T(8,128)(2,1)} %param.22) | copy-start | bytes 1032196
  269.8 5.2 %copy-start.14 = (pred[512]{0:T(512)(128)(4,1)S(1)}, pred[512]{0:T(512)(128)(4,1)}, u32[]{:S(2)}) copy-start(pred[512]{0:T(512)(128)(4,1)} %get-tuple-element.31) | copy-start | bytes 1540
  275.0 3.6 copy-start.2
  275.0 3.6 copy-start.13
  275.0 4.0 %copy-start.15 = (f32[2,512,1024]{2,1,0:T(8,128)S(1)}, f32[2,512,1024]{2,1,0:T(8,128)}, u32[]{:S(2)}) copy-start(f32[2,512,1024]{2,1,0:T(8,128)} %get-tuple-element.27) | copy-start | bytes 12582916
  286.3 0.7 copy-start.9
  286.3 8.5 %copy-start.5 = (s32[1024]{0:T(1024)S(1)}, s32[1024]{0:T(1024)}, u32[]{:S(2)}) copy-start(s32[1024]{0:T(1024)} %param.24) | copy-start | bytes 12292
  286.3 8.5 %copy-start.8 = (pred[1024]{0:T(1024)(128)(4,1)S(1)}, pred[1024]{0:T(1024)(128)(4,1)}, u32[]{:S(2)}) copy-start(pred[1024]{0:T(1024)(128)(4,1)} %copy-done.7) | copy-start | bytes 3076
  287.5 42.5 %all-to-all-start = ((s32[16,1,4]{2,1,0:T(1,128)}), s32[16,1,4]{2,1,0:T(1,128)S(1)}, u32[]{:S(2)}, u32[]{:S(2)}) async-start(s32[16,1,4]{2,1,0:T(1,128)} %broadcast_in_dim.129), calls=%async_computation.1 | async-start | bytes 16384 | tf_op jit(solution)/shard_map/all_to_all | solution.py:153
  330.0 36.9 %all-to-all-start.1 = ((bf16[16,4,14336]{2,1,0:T(4,128)(2,1)}), bf16[16,4,14336]{2,1,0:T(4,128)(2,1)}, u32[]{:S(2)}, u32[]{:S(2)}) async-start(bf16[16,4,14336]{2,1,0:T(4,128)(2,1)} %select_select_fusion), calls=%async_computation.2 | async-start | bytes 3670016 | tf_op jit(solution)/shard_map/all_to_all | solution.py:152
Sparse Core Ops, SparseCore 0:
  20.0 96.1 all-gather.4
  144.4 84.4 all-gather.2
  286.4 103.6 reduce-scatter.1

commit v3 on v2

--- a/solution.py
+++ b/solution.py
@@ -18,17 +18,19 @@
     return (combined * factor * input_norm_gain).astype(jnp.bfloat16)
 
 
-def attend_block(query, keys, values, segment, position, live, first, count, key_end):
+def attend_rows(query, keys, values, segment, live, query_at):
     heads = query.shape[1] // HD
-    block_query = query[first : first + count].reshape(count, heads, HD)
+    count = query_at.shape[0]
+    key_end = keys.shape[0]
+    position = jnp.arange(key_end, dtype=jnp.int32)
+    block_query = jnp.take(query, query_at, axis=0).reshape(count, heads, HD)
     block_keys = keys.reshape(key_end, heads, HD)
     block_values = values.reshape(key_end, heads, HD)
     scores = jnp.einsum(
         "qhd,khd->hqk", block_query, block_keys, preferred_element_type=jnp.float32
     ) / math.sqrt(HD)
-    query_at = position[first : first + count]
     allowed = (
-        (segment[first : first + count, None] == segment[None, :key_end])
+        (jnp.take(segment, query_at)[:, None] == segment[None, :])
         & (position[None, :] <= query_at[:, None])
         & (position[None, :] < live)
     )
@@ -98,19 +100,25 @@
         [query_projection_weight, key_projection_weight, value_projection_weight], 1
     )
     mine, other, order = gather_weights(weight_shard)
-    place = jnp.zeros_like(order).at[order].set(jnp.arange(order.shape[0], dtype=jnp.int32))
-    gathered = jnp.take(jnp.concatenate([mine, other], 0), place, axis=0)
-    full_rows = gathered.shape[0] * block_rows
-    augmented = jnp.concatenate(
-        [gathered.reshape(full_rows, 3 * head_cols), adapter_down_maps], 1
-    )
-    split = hidden_state_input.shape[1]
+    local = normalized_hidden.shape[0]
+    in_order = jnp.take(
+        normalized_hidden.reshape(local, order.shape[0], block_rows), order, axis=1
+    ).reshape(local, -1)
+    down_in_order = jnp.take(
+        adapter_down_maps.reshape(order.shape[0], block_rows, -1), order, axis=0
+    ).reshape(order.shape[0] * block_rows, -1)
+    split = mine.shape[0] * block_rows
     folded_all = None
-    for lo, hi in ((0, split), (split, full_rows)):
-        part = lax.all_gather(normalized_hidden[:, lo:hi], "tensor", axis=0, tiled=True)
-        term = jnp.dot(part, augmented[lo:hi], preferred_element_type=jnp.float32)
+    low_all = None
+    for lo, hi, weight_part in ((0, split, mine), (split, 2 * split, other)):
+        part = lax.all_gather(in_order[:, lo:hi], "tensor", axis=0, tiled=True)
+        term = jnp.dot(
+            part, weight_part.reshape(split, 3 * head_cols), preferred_element_type=jnp.float32
+        )
+        low = jnp.dot(part, down_in_order[lo:hi], preferred_element_type=jnp.float32)
         folded_all = term if folded_all is None else folded_all + term
-    adapter_update = folded_all[:, 3 * head_cols :].astype(jnp.bfloat16)
+        low_all = low if low_all is None else low_all + low
+    adapter_update = low_all.astype(jnp.bfloat16)
     folded = [folded_all[:, k * head_cols : (k + 1) * head_cols] for k in range(3)]
     projected = []
     for adapter_selector in range(3):
@@ -161,22 +169,23 @@
         placing, flat_received, (((0,), (0,)), ((), ())), preferred_element_type=jnp.float32
     )
     kv_cache = cache_rows.astype(jnp.bfloat16).reshape(total_reqs, piece_len, 2, head_cols)
-    block = min(512, stream)
-    attended_parts = []
-    for block_index in range(stream // block):
-        first = block_index * block
-        attended_parts.append(
-            attend_block(query, keys, values, segment, position, live, first, block, stream)
+    shards = lax.axis_size("tensor")
+    rows = stream // shards
+    halves = []
+    for h in range(2):
+        query_at = (
+            jnp.arange(shards, dtype=jnp.int32)[:, None] * rows
+            + h * (rows // 2)
+            + jnp.arange(rows // 2, dtype=jnp.int32)[None, :]
+        ).reshape(-1)
+        attended = attend_rows(query, keys, values, segment, live, query_at)
+        partial_value = jnp.dot(
+            attended, output_projection_weight, preferred_element_type=jnp.float32
+        ).astype(jnp.bfloat16)
+        halves.append(
+            lax.psum_scatter(partial_value, "tensor", scatter_dimension=0, tiled=True)
         )
-    attended = jnp.concatenate(attended_parts, 0)
-    block_out = lax.psum_scatter(
-        jnp.dot(attended, output_projection_weight, preferred_element_type=jnp.float32).astype(
-            jnp.bfloat16
-        ),
-        "tensor",
-        scatter_dimension=0,
-        tiled=True,
-    )
+    block_out = jnp.concatenate(halves, 0)
     return (block_out, kv_cache)
 
 

time: 403 us -> 440 us (1.092)
  waiting for transfers between devices: 147 us -> 163 us
  local copies, waits for them, and re-layouts: 83.7 us -> 96.9 us
    all_gather x2, waiting for transfers between devices: 1.72 us -> 25.8 us  [body(): part = lax.all_gather(in_order[:, lo:hi], 'tensor', axis=0, tiled=True)]
    ppermute x1, waiting for transfers between devices: 10.6 us -> 0.01 us  [gather_weights(): other = lax.ppermute(mine, 'dp', to_core)]
    ppermute x1, waiting for transfers between devices: 33.4 us -> 43.2 us  [gather_weights(): pair = jnp.stack([weight_shard, lax.ppermute(weight_shard, 'dp', to_yh)])]
    concatenate x1 -> x0, local copies, waits for them, and re-layouts: 8.4 us -> none  [body(): gathered = jnp.take(jnp.concatenate([mine, other], 0), place, axis=0)]
    gather x1 -> x6, local copies, waits for them, and re-layouts: 15.5 us -> 22.6 us  [the longest x2 8.23 us: attend_rows(): block_query = jnp.take(query, query_at, axis=0).reshape(count, heads, HD)]
    reduce_scatter x1 -> x2, waiting for transfers between devices: 9.11 us -> 3.34 us  [body(): lax.psum_scatter(partial_value, 'tensor', scatter_dimension=0, tiled=True)]
    select_n x3 -> x8, other arithmetic: 18.1 us -> 12.4 us  [the longest x1 5.16 us: body(): jnp.take(normalized_hidden.reshape(local, order.shape[0], block_rows), or...]
    unnamed x37 -> x29, local copies, waits for them, and re-layouts: 12.7 us -> 18 us
  transfers between devices with their start and end apart: 11 -> 12, of which waited for: 7 -> 6; matrix products, arithmetic and copies ran while one was open for 36% -> 30% of each run, Pallas kernels for 0% -> 0%
where the time goes in v3:
time: 440 us; the launch traced here: 432 us
  waiting for transfers between devices  163 us (37%)
  local copies, waits for them, and re-layouts  96.9 us (22%)
  matrix products  88.6 us (20%)
  other arithmetic  35 us (8%)
  starting transfers between devices  33.3 us (8%)
  between operations  15.2 us (3%)
    ppermute x1, waiting for transfers between devices, gather_weights(): from_prev = lax.ppermute(pair, 'dp', to_next)  48.7 us
    ppermute x1, waiting for transfers between devices, gather_weights(): pair = jnp.stack([weight_shard, lax.ppermute(weight_shard, 'dp', to_yh)])  43.2 us
    dot_general x2, matrix products, body(): jnp.dot(part, weight_part.reshape(split, 3 * head_cols), preferred_elemen...  34 us
    all_to_all x1, waiting for transfers between devices, body(): lax.all_to_all(taken, 'dp', split_axis=0, concat_axis=0, tiled=True)  28 us
    all_gather x2, waiting for transfers between devices, body(): part = lax.all_gather(in_order[:, lo:hi], 'tensor', axis=0, tiled=True)  25.8 us
    unnamed x29, local copies, waits for them, and re-layouts  18 us
    dot_general x2, matrix products, body(): jnp.dot(part, down_in_order[lo:hi], preferred_element_type=jnp.float32)  17.5 us
    ppermute x1, waiting for transfers between devices, gather_weights(): lax.ppermute(from_prev[0], 'dp', to_next)  14 us
  transfers between devices with their start and end apart: 12, of which 6 were waited for; matrix products, arithmetic and copies ran while one was open for 30% of the time, Pallas kernels for 0%

profile of v3, /device:TPU:1, one launch (start us, length us, event | category | flops | bytes accessed | tf_op | source)
XLA Modules:
  0.0 432.0 jit_solution(1216221184367094869)
XLA Ops:
  7.3 2.4 copy.37
  9.6 2.2 copy.36
  11.9 1.9 multiply_reduce_fusion
  15.4 3.2 multiply_convert_fusion
  18.6 3.6 gather_fusion
  22.2 5.2 %bitcast_select_fusion = bf16[128,7168]{0,1:T(8,128)(2,1)S(1)} fusion(bf16[16,128,448]{1,2,0:T(8,128)(2,1)} %gather_fusion, pred[7168]{0:T(1024)(128)(4,1)S(1)} %broadcast_in_dim.143), kind=kLoop, calls=%fused_computation.46 | loop fusion | flops 917504 | bytes 3677184 | tf_op jit(solution)/shard_map/jit(_take)/select_n | solution.py:104
  27.3 1.3 fusion.47
  28.8 3.5 concatenate.24
  32.3 3.7 collective-permute-start
  36.0 43.2 %collective-permute-done = bf16[448,1344]{1,0:T(8,128)(2,1)S(1)} collective-permute-done((bf16[448,1344]{1,0:T(8,128)(2,1)}, bf16[448,1344]{1,0:T(8,128)(2,1)S(1)}, u32[]{:S(2)}, u32[]{:S(2)}) %collective-permute-start) | collective-permute-done | bytes 1204256 | tf_op jit(solution)/shard_map/ppermute | solution.py:64
  80.4 3.1 pad_maximum_fusion
  83.4 1.2 collective-permute-start.1
  84.7 1.4 collective-permute-start.2
  86.2 2.6 constant_dynamic-update-slice_fusion.3
  88.8 48.7 %collective-permute-done.1 = bf16[2,448,1344]{2,1,0:T(8,128)(2,1)} collective-permute-done((bf16[2,448,1344]{2,1,0:T(8,128)(2,1)}, bf16[2,448,1344]{2,1,0:T(8,128)(2,1)}, u32[]{:S(2)}, u32[]{:S(2)}) %collective-permute-start.1) | collective-permute-done | bytes 2408480 | tf_op jit(solution)/shard_map/ppermute | solution.py:65
  137.5 1.4 slice_bitcast_fusion.1
  139.0 1.4 slice_bitcast_fusion
  140.4 2.7 collective-permute-start.4
  144.3 3.4 constant_dynamic-update-slice_fusion.1
  147.6 3.3 constant_dynamic-update-slice_fusion
  150.9 14.0 %collective-permute-done.3 = bf16[448,1344]{1,0:T(8,128)(2,1)S(1)} collective-permute-done((bf16[448,1344]{1,0:T(8,128)(2,1)S(1)}, bf16[448,1344]{1,0:T(8,128)(2,1)S(1)}, u32[]{:S(2)}, u32[]{:S(2)}) %collective-permute-start.3) | collective-permute-done | bytes 1204256 | tf_op jit(solution)/shard_map/ppermute | solution.py:68
  167.2 5.9 %collective-permute-start.5 = (bf16[8,448,1344]{2,1,0:T(8,128)(2,1)}, bf16[8,448,1344]{2,1,0:T(8,128)(2,1)}, u32[]{:S(2)}, u32[]{:S(2)}) collective-permute-start(bf16[8,448,1344]{2,1,0:T(8,128)(2,1)} %bitcast_dynamic-update-slice_fusion), channel_id=1, source_target_pairs={{0,8},{8,0},{16,24},{24,16},{32,40},{40,32},{48,56},{56,48},{64,72... | collective-permute-start | bytes 28901384 | tf_op jit(solution)/shard_map/ppermute | solution.py:71
  173.1 6.3 %gather_fusion.1 = bf16[16,448,384]{2,1,0:T(8,128)(2,1)} fusion(bf16[16,448,384]{2,1,0:T(8,128)(2,1)} %bitcast.83, s32[1024]{0:T(1024)S(1)} %get-tuple-element.24), kind=kCustom, calls=%fused_computation.5 | custom fusion | bytes 11010112 | tf_op jit(solution)/shard_map/jit(_take)/gather | solution.py:107
  179.7 2.3 gather_fusion.3
  182.0 2.3 gather_fusion.5
  184.3 2.2 fusion.11
  186.5 3.2 broadcast_select_fusion
  189.7 3.0 fusion.46
  192.7 9.0 %fusion.51 = f32[1024,384]{1,0:T(8,128)} fusion(bf16[1024,3584]{0,1:T(8,128)(2,1)} %all-gather.3.cloned.1.call-done, bf16[3584,384]{1,0:T(8,128)(2,1)} %bitcast.81), kind=kOutput, calls=%fused_computation.124 | convolution fusion | flops 2818572288 | bytes 11665408 | tf_op jit(solution)/shard_map/dot_general | solution.py:118
  201.7 25.8 %all-gather.5.cloned.1.call-done = bf16[1024,3584]{0,1:T(8,128)(2,1)} async-done(((bf16[128,3584]{0,1:T(8,128)(2,1)}), bf16[1024,3584]{0,1:T(8,128)(2,1)}) %all-gather.5.cloned.1.call-update) | async-done | bytes 7340048 | tf_op jit(solution)/shard_map/all_gather | solution.py:114
  227.6 8.5 %add_convert_fusion = bf16[1024,384]{1,0:T(8,128)(2,1)S(1)} fusion(f32[1024,384]{1,0:T(8,128)} %fusion.51, bf16[1024,3584]{0,1:T(8,128)(2,1)} %all-gather.5.cloned.1.call-done, bf16[3584,384]{1,0:T(8,128)(2,1)} %bitcast.80), kind=kOutput, calls=%fused_computation.48 | convolution fusion | flops 2819358720 | bytes 12451840 | tf_op jit(solution)/shard_map/dot_general | solution.py:118
  236.1 16.2 %fusion.50 = f32[1024,1344]{0,1:T(8,128)} fusion(bf16[1024,3584]{0,1:T(8,128)(2,1)S(1)} %copy-done.2, bf16[3584,1344]{1,0:T(8,128)(2,1)} %bitcast.12), kind=kOutput, calls=%fused_computation.123 | convolution fusion | flops 9865003008 | bytes 22478848 | tf_op jit(solution)/shard_map/dot_general | solution.py:115
  252.3 17.8 %convolution_add_fusion = f32[1024,1344]{0,1:T(8,128)} fusion(f32[1024,1344]{0,1:T(8,128)} %fusion.50, bf16[1024,3584]{0,1:T(8,128)(2,1)} %all-gather.3.cloned.1.call-done, bf16[3584,1344]{1,0:T(8,128)(2,1)} %bitcast.11), kind=kOutput, calls=%fused_computation.13 | convolution fusion | flops 9866379264 | bytes 27983872 | tf_op jit(solution)/shard_map/dot_general | solution.py:115
  270.1 2.8 fusion.18
  273.0 2.8 fusion.17
  275.8 2.9 fusion.16
  278.7 2.2 copy.38
  281.0 4.2 gather_fusion.6
  285.2 2.0 broadcast_select_fusion.1
  287.1 2.0 copy.41
  289.2 5.2 %fusion.48 = (f32[2,512]{1,0:T(2,128)S(1)}, f32[2,512,1024]{2,1,0:T(8,128)}) fusion(pred[512,1024]{1,0:T(8,128)(4,1)} %get-tuple-element.17, bf16[512,2,224]{0,2,1:T(8,128)(2,1)} %bitcast.96, bf16[1024,2,224]{0,2,1:T(8,128)(2,1)} %bitcast.88), kind=kOutput, calls=%fused_computation.121 | convolution fusion | flops 473957376 | bytes 6098944 | tf_op jit(solution)/shard_map/sub | solution.py:39
  294.3 3.4 fusion.20
  297.7 3.9 convolution_convert_fusion.1
  301.7 4.0 gather_fusion.4
  305.7 2.0 broadcast_select_fusion.2
  307.7 2.0 copy.39
  309.7 5.2 %fusion.49 = (f32[2,512]{1,0:T(2,128)S(1)}, f32[2,512,1024]{2,1,0:T(8,128)}) fusion(pred[512,1024]{1,0:T(8,128)(4,1)} %get-tuple-element.16, bf16[512,2,224]{0,2,1:T(8,128)(2,1)} %bitcast.95, bf16[1024,2,224]{0,2,1:T(8,128)(2,1)} %bitcast.89), kind=kOutput, calls=%fused_computation.122 | convolution fusion | flops 473957376 | bytes 6098944 | tf_op jit(solution)/shard_map/sub | solution.py:39
  314.9 3.4 fusion.22
  318.3 3.9 convolution_convert_fusion.2
  323.4 10.8 %all-to-all-start = ((s32[16,1,4]{2,1,0:T(1,128)}), s32[16,1,4]{2,1,0:T(1,128)S(1)}, u32[]{:S(2)}, u32[]{:S(2)}) async-start(s32[16,1,4]{2,1,0:T(1,128)} %broadcast_in_dim.154), calls=%async_computation.2 | async-start | bytes 16384 | tf_op jit(solution)/shard_map/all_to_all | solution.py:161
  335.6 3.9 broadcast_in_dim.156
  340.8 3.9 broadcast_in_dim.158
  344.7 2.9 pad_maximum_fusion.1
  347.5 3.8 copy.42
  351.4 7.5 %gather_fusion.2 = bf16[1024,896]{1,0:T(8,128)(2,1)} fusion(bf16[1024,896]{1,0:T(8,128)(2,1)} %copy.42, s32[1024]{0:T(1024)S(1)} %get-tuple-element.25), kind=kCustom, calls=%fused_computation.6 | custom fusion | bytes 3674112 | tf_op jit(solution)/shard_map/jit(_take)/gather | solution.py:155
  358.8 4.3 gather.26
  363.1 5.7 %select_select_fusion = bf16[16,4,14336]{2,1,0:T(4,128)(2,1)} fusion(pred[16,4,14336]{2,1,0:T(4,128)(4,1)} %broadcast_in_dim.156, pred[16,4,14336]{2,1,0:T(4,128)(4,1)} %broadcast_in_dim.158, bf16[16,4,14336]{2,1,0:T(4,128)(2,1)} %gather.26), kind=kLoop, calls=%fused_computation.47 | loop fusion | flops 1835008 | bytes 5505024 | tf_op jit(solution)/shard_map/jit(_where)/select_n | solution.py:156
  368.9 7.2 %all-to-all-start.1 = ((bf16[16,4,14336]{2,1,0:T(4,128)(2,1)}), bf16[16,4,14336]{2,1,0:T(4,128)(2,1)}, u32[]{:S(2)}, u32[]{:S(2)}) async-start(bf16[16,4,14336]{2,1,0:T(4,128)(2,1)} %select_select_fusion), calls=%async_computation.3 | async-start | bytes 3670016 | tf_op jit(solution)/shard_map/all_to_all | solution.py:160
  377.4 28.0 %all-to-all-done.1 = bf16[16,4,14336]{2,1,0:T(4,128)(2,1)} async-done(((bf16[16,4,14336]{2,1,0:T(4,128)(2,1)}), bf16[16,4,14336]{2,1,0:T(4,128)(2,1)}, u32[]{:S(2)}, u32[]{:S(2)}) %all-to-all-start.1) | async-done | bytes 1835040 | tf_op jit(solution)/shard_map/all_to_all | solution.py:160
  405.3 3.9 reshape.416
  409.2 3.6 convolution_convert_fusion
  412.8 6.8 %reshape.417 = bf16[64,16,2,448]{3,2,1,0:T(2,128)(2,1)} reshape(bf16[64,14336]{1,0:T(8,128)(2,1)} %convolution_convert_fusion) | data formatting | bytes 3670016 | tf_op jit(solution)/shard_map/reshape | solution.py:171
  419.6 3.3 reduce-scatter.3.cloned.1.call-done
  422.9 2.1 pad_maximum_fusion.2
  (74 shorter events, 11.3 us)
Async XLA Ops:
  7.2 290.6 %copy-start = (bf16[448,3584]{1,0:T(8,128)(2,1)S(1)}, bf16[448,3584]{1,0:T(8,128)(2,1)}, u32[]{:S(2)}) copy-start(bf16[448,3584]{1,0:T(8,128)(2,1)} %param.27) | copy-start | bytes 9633796
  7.2 8.0 %copy-start.8 = (s32[16]{0:T(128)S(1)}, s32[16]{0:T(128)}, u32[]{:S(2)}) copy-start(s32[16]{0:T(128)} %constant.154.clone) | copy-start | bytes 196
  7.2 8.0 %copy-start.9 = (s32[16]{0:T(128)S(1)}, s32[16]{0:T(128)}, u32[]{:S(2)}) copy-start(s32[16]{0:T(128)} %constant.153.clone) | copy-start | bytes 196
  7.2 8.0 %copy-start.10 = (s32[16]{0:T(128)S(1)}, s32[16]{0:T(128)}, u32[]{:S(2)}) copy-start(s32[16]{0:T(128)} %constant.152.clone) | copy-start | bytes 196
  7.2 6.6 %copy-start.6 = (f32[7168]{0:T(1024)S(1)}, f32[7168]{0:T(1024)}, u32[]{:S(2)}) copy-start(f32[7168]{0:T(1024)} %param.21) | copy-start | bytes 86020
  7.2 7.3 %copy-start.1 = (s32[1024]{0:T(1024)S(1)}, s32[1024]{0:T(1024)}, u32[]{:S(2)}) copy-start(s32[1024]{0:T(1024)} %param.28) | copy-start | bytes 12292
  7.2 185.5 %all-gather.3.cloned.1.call-start = ((), (), s32[]{:S(2)}) async-start(), calls=%async_computation.4 | async-start | bytes 8257536 | tf_op jit(solution)/shard_map/all_gather | solution.py:114
  28.7 198.8 %all-gather.5.cloned.1.call-start = ((), (), s32[]{:S(2)}) async-start(), calls=%async_computation.5 | async-start | bytes 8257536 | tf_op jit(solution)/shard_map/all_gather | solution.py:114
  32.3 46.9 %collective-permute-start = (bf16[448,1344]{1,0:T(8,128)(2,1)}, bf16[448,1344]{1,0:T(8,128)(2,1)S(1)}, u32[]{:S(2)}, u32[]{:S(2)}) collective-permute-start(bf16[448,1344]{1,0:T(8,128)(2,1)} %concatenate.24), channel_id=1, source_target_pairs={{0,16},{8,24},{16,0},{24,8},{32,48},{40,56},{48,32},{56,40},{64,80... | collective-permute-start | bytes 3612680 | tf_op jit(solution)/shard_map/ppermute | solution.py:64
  79.2 1.2 copy-start.3
  83.4 54.0 %collective-permute-start.1 = (bf16[2,448,1344]{2,1,0:T(8,128)(2,1)}, bf16[2,448,1344]{2,1,0:T(8,128)(2,1)}, u32[]{:S(2)}, u32[]{:S(2)}) collective-permute-start(bf16[2,448,1344]{2,1,0:T(8,128)(2,1)} %pad_maximum_fusion), channel_id=1, source_target_pairs={{0,32},{8,40},{16,48},{24,56},{32,64},{40,72},{48,80},{56,88},{64,... | collective-permute-start | bytes 7225352 | tf_op jit(solution)/shard_map/ppermute | solution.py:65
  84.7 54.3 %collective-permute-start.2 = (bf16[2,448,1344]{2,1,0:T(8,128)(2,1)}, bf16[2,448,1344]{2,1,0:T(8,128)(2,1)}, u32[]{:S(2)}, u32[]{:S(2)}) collective-permute-start(bf16[2,448,1344]{2,1,0:T(8,128)(2,1)} %pad_maximum_fusion), channel_id=1, source_target_pairs={{0,96},{8,104},{16,112},{24,120},{32,0},{40,8},{48,16},{56,24},{64... | collective-permute-start | bytes 7225352 | tf_op jit(solution)/shard_map/ppermute | solution.py:66
  86.1 333.4 %reduce-scatter.5.cloned.1.call-start = ((), (), s32[]{:S(2)}) async-start(), calls=%async_computation.7 | async-start | bytes 4128768 | tf_op jit(solution)/shard_map/reduce_scatter | solution.py:186
  86.2 56.9 %copy-start.4 = (bf16[448,1344]{1,0:T(8,128)(2,1)S(1)}, bf16[448,1344]{1,0:T(8,128)(2,1)}, u32[]{:S(2)}) copy-start(bf16[448,1344]{1,0:T(8,128)(2,1)} %copy-done.3) | copy-start | bytes 3612676
  138.9 26.0 %collective-permute-start.3 = (bf16[448,1344]{1,0:T(8,128)(2,1)S(1)}, bf16[448,1344]{1,0:T(8,128)(2,1)S(1)}, u32[]{:S(2)}, u32[]{:S(2)}) collective-permute-start(bf16[448,1344]{1,0:T(8,128)(2,1)S(1)} %slice_bitcast_fusion.1), channel_id=1, source_target_pairs={{0,32},{8,40},{16,48},{24,56},{32,64},{40,72},{48,80},{56,88},{64,... | collective-permute-start | bytes 3612680 | tf_op jit(solution)/shard_map/ppermute | solution.py:68
  140.4 25.7 %collective-permute-start.4 = (bf16[448,1344]{1,0:T(8,128)(2,1)S(1)}, bf16[448,1344]{1,0:T(8,128)(2,1)S(1)}, u32[]{:S(2)}, u32[]{:S(2)}) collective-permute-start(bf16[448,1344]{1,0:T(8,128)(2,1)S(1)} %slice_bitcast_fusion), channel_id=1, source_target_pairs={{0,96},{8,104},{16,112},{24,120},{32,0},{40,8},{48,16},{56,24},{64... | collective-permute-start | bytes 3612680 | tf_op jit(solution)/shard_map/ppermute | solution.py:68
  167.2 68.8 %collective-permute-start.5 = (bf16[8,448,1344]{2,1,0:T(8,128)(2,1)}, bf16[8,448,1344]{2,1,0:T(8,128)(2,1)}, u32[]{:S(2)}, u32[]{:S(2)}) collective-permute-start(bf16[8,448,1344]{2,1,0:T(8,128)(2,1)} %bitcast_dynamic-update-slice_fusion), channel_id=1, source_target_pairs={{0,8},{8,0},{16,24},{24,16},{32,40},{40,32},{48,56},{56,48},{64,72... | collective-permute-start | bytes 28901384 | tf_op jit(solution)/shard_map/ppermute | solution.py:71
  227.6 8.5 %copy-start.2 = (bf16[1024,3584]{0,1:T(8,128)(2,1)S(1)}, bf16[1024,3584]{0,1:T(8,128)(2,1)}, u32[]{:S(2)}) copy-start(bf16[1024,3584]{0,1:T(8,128)(2,1)} %all-gather.5.cloned.1.call-done) | copy-start | bytes 22020100
  252.3 17.8 %copy-start.5 = (bf16[3,128,448]{1,2,0:T(8,128)(2,1)S(1)}, bf16[3,128,448]{1,2,0:T(8,128)(2,1)}, u32[]{:S(2)}) copy-start(bf16[3,128,448]{1,2,0:T(8,128)(2,1)} %param.26) | copy-start | bytes 1032196
  301.6 121.3 %reduce-scatter.3.cloned.1.call-start = ((), (), s32[]{:S(2)}) async-start(), calls=%async_computation.6 | async-start | bytes 4128768 | tf_op jit(solution)/shard_map/reduce_scatter | solution.py:186
  322.2 0.7 copy-start.7
  323.4 45.5 %all-to-all-start = ((s32[16,1,4]{2,1,0:T(1,128)}), s32[16,1,4]{2,1,0:T(1,128)S(1)}, u32[]{:S(2)}, u32[]{:S(2)}) async-start(s32[16,1,4]{2,1,0:T(1,128)} %broadcast_in_dim.154), calls=%async_computation.2 | async-start | bytes 16384 | tf_op jit(solution)/shard_map/all_to_all | solution.py:161
  368.9 36.4 %all-to-all-start.1 = ((bf16[16,4,14336]{2,1,0:T(4,128)(2,1)}), bf16[16,4,14336]{2,1,0:T(4,128)(2,1)}, u32[]{:S(2)}, u32[]{:S(2)}) async-start(bf16[16,4,14336]{2,1,0:T(4,128)(2,1)} %select_select_fusion), calls=%async_computation.3 | async-start | bytes 3670016 | tf_op jit(solution)/shard_map/all_to_all | solution.py:160
Sparse Core Ops, SparseCore 0:
  28.8 112.7 all-gather.2
  143.2 84.3 all-gather.4
  301.8 50.0 reduce-scatter.4
  354.2 68.6 reduce-scatter.2

commit v4 on v2

--- a/solution.py
+++ b/solution.py
@@ -4,6 +4,7 @@
 import jax.numpy as jnp
 from jax import lax
 from jax.sharding import PartitionSpec as P
+from jax.experimental.layout import Layout, with_layout_constraint
 
 HD = 224
 
@@ -98,19 +99,31 @@
         [query_projection_weight, key_projection_weight, value_projection_weight], 1
     )
     mine, other, order = gather_weights(weight_shard)
-    place = jnp.zeros_like(order).at[order].set(jnp.arange(order.shape[0], dtype=jnp.int32))
-    gathered = jnp.take(jnp.concatenate([mine, other], 0), place, axis=0)
-    full_rows = gathered.shape[0] * block_rows
-    augmented = jnp.concatenate(
-        [gathered.reshape(full_rows, 3 * head_cols), adapter_down_maps], 1
-    )
-    split = hidden_state_input.shape[1]
-    folded_all = None
-    for lo, hi in ((0, split), (split, full_rows)):
-        part = lax.all_gather(normalized_hidden[:, lo:hi], "tensor", axis=0, tiled=True)
-        term = jnp.dot(part, augmented[lo:hi], preferred_element_type=jnp.float32)
-        folded_all = term if folded_all is None else folded_all + term
-    adapter_update = folded_all[:, 3 * head_cols :].astype(jnp.bfloat16)
+    local = normalized_hidden.shape[0]
+    in_order = jnp.take(
+        normalized_hidden.reshape(local, order.shape[0], block_rows), order, axis=1
+    ).reshape(local, -1)
+    split = mine.shape[0] * block_rows
+    low_local = jnp.dot(
+        normalized_hidden, adapter_down_maps, preferred_element_type=jnp.float32
+    ).astype(jnp.bfloat16)
+    row_major = Layout((0, 1))
+    low_part = with_layout_constraint(
+        lax.all_gather(in_order[:, :split], "tensor", axis=0, tiled=True), row_major
+    )
+    folded_all = jnp.dot(
+        low_part, mine.reshape(split, 3 * head_cols), preferred_element_type=jnp.float32
+    )
+    high_part = with_layout_constraint(
+        lax.all_gather(
+            jnp.concatenate([in_order[:, split:], low_local], 1), "tensor", axis=0, tiled=True
+        ),
+        row_major,
+    )
+    folded_all = folded_all + jnp.dot(
+        high_part[:, :split], other.reshape(split, 3 * head_cols), preferred_element_type=jnp.float32
+    )
+    adapter_update = high_part[:, split:]
     folded = [folded_all[:, k * head_cols : (k + 1) * head_cols] for k in range(3)]
     projected = []
     for adapter_selector in range(3):
@@ -141,11 +154,13 @@
         jnp.arange(groups, dtype=jnp.int32)[:, None] * piece_len
         + jnp.arange(piece_len, dtype=jnp.int32)[None, :]
     )
-    source_rows = jnp.minimum(starts[None, :, None] + offsets[:, None, :], stream - 1)
+    source_rows = starts[None, :, None] + offsets[:, None, :]
     alive_mask = offsets[:, None, :] < lengths[None, :, None]
+    picking = (
+        (source_rows.reshape(-1)[:, None] == position[None, :]) & alive_mask.reshape(-1)[:, None]
+    ).astype(jnp.bfloat16)
     stacked = jnp.stack([keys, values], 1).reshape(stream, 2 * head_cols)
-    taken = jnp.take(stacked, source_rows.reshape(-1), axis=0)
-    taken = jnp.where(alive_mask.reshape(-1)[:, None], taken, jnp.zeros((), jnp.bfloat16))
+    taken = jnp.dot(picking, stacked, preferred_element_type=jnp.float32).astype(jnp.bfloat16)
     taken = taken.reshape(groups, requests, piece_len * 2 * head_cols)
     row_send = jnp.broadcast_to(request_cache_row[None, :], (groups, requests))
     received, received_rows = (

time: 403 us -> 388 us (0.963); the launches traced: 397 us -> 387 us
  waiting for transfers between devices: 147 us -> 199 us
  local copies, waits for them, and re-layouts: 83.7 us -> 52 us
  other arithmetic: 36.3 us -> 15.7 us
  matrix products: 84.9 us -> 76 us
    reduce_scatter x1, waiting for transfers between devices: 9.11 us -> 31.7 us  [body(): lax.psum_scatter(jnp.dot(attended, output_projection_weight, preferred_el...]
    select_n x5 -> x1, other arithmetic: 23.6 us -> 1.7 us  [body(): jnp.take(normalized_hidden.reshape(local, order.shape[0], block_rows), or...]
    gather x3 -> x2, local copies, waits for them, and re-layouts: 27.3 us -> 7.41 us  [body(): jnp.take(normalized_hidden.reshape(local, order.shape[0], block_rows), or...]
    ppermute x1, waiting for transfers between devices: 33.4 us -> 48.6 us  [gather_weights(): pair = jnp.stack([weight_shard, lax.ppermute(weight_shard, 'dp', to_yh)])]
    all_gather x2, waiting for transfers between devices: 1.72 us -> 16 us  [the longest x1 16 us: body(): lax.all_gather(in_order[:, :split], 'tensor', axis=0, tiled=True)]
    broadcast_in_dim x6 -> x2, local copies, waits for them, and re-layouts: 10.5 us -> 0.17 us  [body(): jnp.take(normalized_hidden.reshape(local, order.shape[0], block_rows), or...]
    dot_general x2 -> x4, matrix products: 52.3 us -> 43.3 us  [the longest x1 17.9 us: body(): jnp.dot(low_part, mine.reshape(split, 3 * head_cols), preferred_element_t...]
    concatenate x1 -> x0, local copies, waits for them, and re-layouts: 8.4 us -> none  [body(): gathered = jnp.take(jnp.concatenate([mine, other], 0), place, axis=0)]
  transfers between devices with their start and end apart: 11 -> 11, of which waited for: 7 -> 7; matrix products, arithmetic and copies ran while one was open for 36% -> 18% of each run, Pallas kernels for 0% -> 0%
where the time goes in v4:
time: 388 us; the launch traced here: 387 us
  waiting for transfers between devices  199 us (51%)
  matrix products  76 us (20%)
  local copies, waits for them, and re-layouts  52 us (13%)
  starting transfers between devices  29.2 us (8%)
  other arithmetic  15.7 us (4%)
  between operations  14.7 us (4%)
    ppermute x1, waiting for transfers between devices, gather_weights(): from_prev = lax.ppermute(pair, 'dp', to_next)  48.7 us
    ppermute x1, waiting for transfers between devices, gather_weights(): pair = jnp.stack([weight_shard, lax.ppermute(weight_shard, 'dp', to_yh)])  48.6 us
    reduce_scatter x1, waiting for transfers between devices, body(): lax.psum_scatter(jnp.dot(attended, output_projection_weight, preferred_el...  31.7 us
    all_to_all x1, waiting for transfers between devices, body(): lax.all_to_all(taken, 'dp', split_axis=0, concat_axis=0, tiled=True)  28.1 us
    unnamed x45, local copies, waits for them, and re-layouts  18.5 us
    dot_general x1, matrix products, body(): jnp.dot(low_part, mine.reshape(split, 3 * head_cols), preferred_element_t...  17.9 us
    dot_general x1, matrix products, body(): jnp.dot(high_part[:, :split], other.reshape(split, 3 * head_cols), prefer...  17.2 us
    all_gather x1, waiting for transfers between devices, body(): lax.all_gather(in_order[:, :split], 'tensor', axis=0, tiled=True)  16 us
  transfers between devices with their start and end apart: 11, of which 7 were waited for; matrix products, arithmetic and copies ran while one was open for 18% of the time, Pallas kernels for 0%

profile of v4, /device:TPU:1, one launch (start us, length us, event | category | flops | bytes accessed | tf_op | source)
XLA Modules:
  0.0 386.8 jit_solution(5788911664608993963)
XLA Ops:
  7.3 2.4 copy.24
  9.6 1.9 fusion.7
  11.5 2.2 copy.23
  13.9 4.4 %fusion.40 = bf16[128,384]{1,0:T(8,128)(2,1)S(1)} fusion(bf16[7168,384]{1,0:T(8,128)(2,1)} %param.21, f32[7168]{0:T(1024)S(1)} %copy-done.9, f32[128]{0:T(128)S(1)} %add_rsqrt_fusion, bf16[128,3584]{1,0:T(8,128)(2,1)} %param.16, bf16[128,3584]{1,0:T(8,128)(2,1)} %param.15), kind=kOutput, calls=%fused_computation.63 | convolution fusion | flops 711114752 | bytes 7467520 | tf_op jit(solution)/shard_map/dot_general | solution.py:107
  18.4 2.5 multiply_convert_fusion
  20.8 3.5 gather_fusion
  24.4 3.9 %copy.25 = bf16[128,7168]{1,0:T(8,128)(2,1)} copy(bf16[128,7168]{0,1:T(8,128)(2,1)} %bitcast.65) | data formatting | bytes 3670016 | tf_op jit(solution)/shard_map/jit(_take)/gather | solution.py:103
  28.3 0.1 broadcast_in_dim.56
  28.4 1.7 broadcast_select_fusion
  30.1 1.0 fusion.71
  31.1 1.0 pad_maximum_fusion.4
  32.2 3.5 concatenate.27
  35.8 3.7 collective-permute-start
  39.5 48.6 %collective-permute-done = bf16[448,1344]{1,0:T(8,128)(2,1)S(1)} collective-permute-done((bf16[448,1344]{1,0:T(8,128)(2,1)}, bf16[448,1344]{1,0:T(8,128)(2,1)S(1)}, u32[]{:S(2)}, u32[]{:S(2)}) %collective-permute-start) | collective-permute-done | bytes 1204256 | tf_op jit(solution)/shard_map/ppermute | solution.py:63
  88.1 1.1 copy-done.1
  89.2 3.1 pad_maximum_fusion
  92.3 1.1 collective-permute-start.1
  93.4 1.6 collective-permute-start.2
  95.1 2.5 constant_dynamic-update-slice_fusion.3
  97.6 48.7 %collective-permute-done.1 = bf16[2,448,1344]{2,1,0:T(8,128)(2,1)} collective-permute-done((bf16[2,448,1344]{2,1,0:T(8,128)(2,1)}, bf16[2,448,1344]{2,1,0:T(8,128)(2,1)}, u32[]{:S(2)}, u32[]{:S(2)}) %collective-permute-start.1) | collective-permute-done | bytes 2408480 | tf_op jit(solution)/shard_map/ppermute | solution.py:64
  146.3 1.4 slice_bitcast_fusion.1
  147.8 1.4 slice_bitcast_fusion
  149.2 2.7 collective-permute-start.4
  152.0 1.2 constant_dynamic-update-slice_fusion.2
  153.1 3.3 constant_dynamic-update-slice_fusion.1
  156.4 3.6 constant_dynamic-update-slice_fusion
  160.0 13.7 %collective-permute-done.3 = bf16[448,1344]{1,0:T(8,128)(2,1)S(1)} collective-permute-done((bf16[448,1344]{1,0:T(8,128)(2,1)S(1)}, bf16[448,1344]{1,0:T(8,128)(2,1)S(1)}, u32[]{:S(2)}, u32[]{:S(2)}) %collective-permute-start.3) | collective-permute-done | bytes 1204256 | tf_op jit(solution)/shard_map/ppermute | solution.py:67
  173.7 1.1 bitcast_dynamic-update-slice_fusion.1
  174.9 1.2 bitcast_dynamic-update-slice_fusion
  176.1 5.4 %collective-permute-start.5 = (bf16[8,448,1344]{2,1,0:T(8,128)(2,1)}, bf16[8,448,1344]{2,1,0:T(8,128)(2,1)}, u32[]{:S(2)}, u32[]{:S(2)}) collective-permute-start(bf16[8,448,1344]{2,1,0:T(8,128)(2,1)} %bitcast_dynamic-update-slice_fusion), channel_id=1, source_target_pairs={{0,8},{8,0},{16,24},{24,16},{32,40},{40,32},{48,56},{56,48},{64,72... | collective-permute-start | bytes 28901384 | tf_op jit(solution)/shard_map/ppermute | solution.py:70
  182.2 0.5 broadcast_compare_fusion.1
  182.8 2.1 fusion.21
  184.9 12.1 %collective-permute-done.5 = bf16[8,448,1344]{2,1,0:T(8,128)(2,1)} collective-permute-done((bf16[8,448,1344]{2,1,0:T(8,128)(2,1)}, bf16[8,448,1344]{2,1,0:T(8,128)(2,1)}, u32[]{:S(2)}, u32[]{:S(2)}) %collective-permute-start.5) | collective-permute-done | bytes 9633824 | tf_op jit(solution)/shard_map/ppermute | solution.py:70
  197.0 17.2 %fusion.2 = f32[1024,1344]{0,1:T(8,128)} fusion(bf16[3584,1344]{1,0:T(8,128)(2,1)} %bitcast.12, bf16[1024,3968]{1,0:T(8,128)(2,1)} %all-gather.5.cloned.1.call-done), kind=kOutput, calls=%fused_computation.5 | convolution fusion | flops 9865003008 | bytes 22937600 | tf_op jit(solution)/shard_map/dot_general | solution.py:123
  214.2 16.0 %all-gather.3.cloned.1.call-done = bf16[1024,3584]{1,0:T(8,128)(2,1)} async-done(((bf16[128,3584]{1,0:T(8,128)(2,1)}), bf16[1024,3584]{1,0:T(8,128)(2,1)}) %all-gather.3.cloned.1.call-update) | async-done | bytes 7340048 | tf_op jit(solution)/shard_map/all_gather | solution.py:112
  230.2 17.9 %convolution_add_fusion = f32[1024,1344]{0,1:T(8,128)} fusion(f32[1024,1344]{0,1:T(8,128)} %fusion.2, bf16[1024,3584]{1,0:T(8,128)(2,1)} %all-gather.3.cloned.1.call-done, bf16[3584,1344]{1,0:T(8,128)(2,1)} %bitcast.11), kind=kOutput, calls=%fused_computation.9 | convolution fusion | flops 9866379264 | bytes 27983872 | tf_op jit(solution)/shard_map/dot_general | solution.py:114
  248.2 2.0 fusion.29
  250.2 1.0 fusion.72
  251.2 2.9 fusion.28
  254.1 5.8 %fusion.74 = (f32[2,512]{1,0:T(2,128)}, f32[2,512,1024]{2,1,0:T(8,128)}) fusion(pred[512,1024]{1,0:T(8,128)(4,1)} %get-tuple-element.9, bf16[512,2,224]{0,2,1:T(8,128)(2,1)} %bitcast.77, bf16[1024,2,224]{0,2,1:T(8,128)(2,1)} %bitcast.67), kind=kOutput, calls=%fused_computation.116 | convolution fusion | flops 473957376 | bytes 6098944 | tf_op jit(solution)/shard_map/sub | solution.py:38
  260.0 5.7 %fusion.75 = (f32[2,512]{1,0:T(2,128)}, f32[2,512,1024]{2,1,0:T(8,128)}) fusion(pred[512,1024]{1,0:T(8,128)(4,1)} %get-tuple-element.8, bf16[512,2,224]{0,2,1:T(8,128)(2,1)} %bitcast.76, bf16[1024,2,224]{0,2,1:T(8,128)(2,1)} %bitcast.68), kind=kOutput, calls=%fused_computation.117 | convolution fusion | flops 473957376 | bytes 6098944 | tf_op jit(solution)/shard_map/sub | solution.py:38
  265.7 2.0 fusion.30
  267.8 3.5 fusion.37
  271.3 0.3 copy-done.17
  271.5 0.9 fusion.39
  272.5 6.1 %convolution_convert_fusion.1 = bf16[1024,3584]{1,0:T(8,128)(2,1)} fusion(bf16[448,3584]{1,0:T(8,128)(2,1)S(1)} %copy-done, bf16[512,448]{0,1:T(8,128)(2,1)S(1)} %bitcast.79, bf16[512,448]{0,1:T(8,128)(2,1)S(1)} %bitcast.80), kind=kOutput, calls=%fused_computation.4 | convolution fusion | flops 3293839360 | bytes 11468800 | tf_op jit(solution)/shard_map/dot_general | solution.py:188
  278.6 0.6 copy-done.12
  279.3 0.6 broadcast_in_dim.100
  279.9 7.3 %all-to-all-start = ((s32[16,1,4]{2,1,0:T(1,128)}), s32[16,1,4]{2,1,0:T(1,128)S(1)}, u32[]{:S(2)}, u32[]{:S(2)}) async-start(s32[16,1,4]{2,1,0:T(1,128)} %broadcast_in_dim.100), calls=%async_computation.1 | async-start | bytes 16384 | tf_op jit(solution)/shard_map/all_to_all | solution.py:168
  287.1 0.1 convert_reduce_fusion
  287.3 0.2 reduce-window.8
  287.6 0.1 add.121
  287.8 0.1 lt.78
  287.9 1.6 pad_maximum_fusion.2
  289.5 3.8 fusion.33
  293.3 4.4 %reshape.307 = bf16[16,4,14336]{2,1,0:T(4,128)(2,1)} reshape(bf16[1024,896]{1,0:T(8,128)(2,1)} %fusion.33) | data formatting | bytes 3670016 | tf_op jit(solution)/shard_map/reshape | solution.py:164
  297.7 7.2 %all-to-all-start.1 = ((bf16[16,4,14336]{2,1,0:T(4,128)(2,1)}), bf16[16,4,14336]{2,1,0:T(4,128)(2,1)}, u32[]{:S(2)}, u32[]{:S(2)}) async-start(bf16[16,4,14336]{2,1,0:T(4,128)(2,1)} %reshape.307), calls=%async_computation.2 | async-start | bytes 3670016 | tf_op jit(solution)/shard_map/all_to_all | solution.py:167
  304.9 0.5 broadcast.202
  305.4 0.7 reduce.3
  306.2 28.1 %all-to-all-done.1 = bf16[16,4,14336]{2,1,0:T(4,128)(2,1)} async-done(((bf16[16,4,14336]{2,1,0:T(4,128)(2,1)}), bf16[16,4,14336]{2,1,0:T(4,128)(2,1)}, u32[]{:S(2)}, u32[]{:S(2)}) %all-to-all-start.1) | async-done | bytes 1835040 | tf_op jit(solution)/shard_map/all_to_all | solution.py:167
  334.3 3.9 reshape.308
  338.2 3.6 convolution_convert_fusion
  341.8 6.8 %reshape.309 = bf16[64,16,2,448]{3,2,1,0:T(2,128)(2,1)} reshape(bf16[64,14336]{1,0:T(8,128)(2,1)} %convolution_convert_fusion) | data formatting | bytes 3670016 | tf_op jit(solution)/shard_map/reshape | solution.py:178
  348.6 31.7 %reduce-scatter.2.cloned.1.call-done = bf16[128,3584]{1,0:T(8,128)(2,1)} async-done(((bf16[1024,3584]{1,0:T(8,128)(2,1)}), bf16[128,3584]{1,0:T(8,128)(2,1)}) %reduce-scatter.2.cloned.1.call-update) | async-done | bytes 917520 | tf_op jit(solution)/shard_map/reduce_scatter | solution.py:187
  (63 shorter events, 0.9 us)
Async XLA Ops:
  7.2 265.3 %copy-start = (bf16[448,3584]{1,0:T(8,128)(2,1)S(1)}, bf16[448,3584]{1,0:T(8,128)(2,1)}, u32[]{:S(2)}) copy-start(bf16[448,3584]{1,0:T(8,128)(2,1)} %param.23) | copy-start | bytes 9633796
  7.2 6.7 %copy-start.13 = (s32[16]{0:T(128)S(1)}, s32[16]{0:T(128)}, u32[]{:S(2)}) copy-start(s32[16]{0:T(128)} %constant.101.clone) | copy-start | bytes 196
  7.2 6.6 %copy-start.14 = (s32[16]{0:T(128)S(1)}, s32[16]{0:T(128)}, u32[]{:S(2)}) copy-start(s32[16]{0:T(128)} %constant.100.clone) | copy-start | bytes 196
  7.2 6.6 %copy-start.15 = (s32[16]{0:T(128)S(1)}, s32[16]{0:T(128)}, u32[]{:S(2)}) copy-start(s32[16]{0:T(128)} %constant.99.clone) | copy-start | bytes 196
  7.2 6.5 %copy-start.9 = (f32[7168]{0:T(1024)S(1)}, f32[7168]{0:T(1024)}, u32[]{:S(2)}) copy-start(f32[7168]{0:T(1024)} %param.17) | copy-start | bytes 86020
  7.2 177.7 %all-gather.5.cloned.1.call-start = ((), (), s32[]{:S(2)}) async-start(), calls=%async_computation.4 | async-start | bytes 9142272 | tf_op jit(solution)/shard_map/all_gather | solution.py:118
  13.9 4.5 %copy-start.4 = (bf16[128,3584]{0,1:T(8,128)(2,1)S(1)}, bf16[128,3584]{0,1:T(8,128)(2,1)}, u32[]{:S(2)}) copy-start(bf16[128,3584]{0,1:T(8,128)(2,1)} %copy.24) | copy-start | bytes 2752516
  13.9 4.5 %copy-start.5 = (bf16[128,3584]{0,1:T(8,128)(2,1)S(1)}, bf16[128,3584]{0,1:T(8,128)(2,1)}, u32[]{:S(2)}) copy-start(bf16[128,3584]{0,1:T(8,128)(2,1)} %copy.23) | copy-start | bytes 2752516
  32.2 198.0 %all-gather.3.cloned.1.call-start = ((), (), s32[]{:S(2)}) async-start(), calls=%async_computation.3 | async-start | bytes 8257536 | tf_op jit(solution)/shard_map/all_gather | solution.py:112
  35.8 52.3 %collective-permute-start = (bf16[448,1344]{1,0:T(8,128)(2,1)}, bf16[448,1344]{1,0:T(8,128)(2,1)S(1)}, u32[]{:S(2)}, u32[]{:S(2)}) collective-permute-start(bf16[448,1344]{1,0:T(8,128)(2,1)} %concatenate.27), channel_id=1, source_target_pairs={{0,16},{8,24},{16,0},{24,8},{32,48},{40,56},{48,32},{56,40},{64,80... | collective-permute-start | bytes 3612680 | tf_op jit(solution)/shard_map/ppermute | solution.py:63
  88.1 1.1 copy-start.1
  92.3 54.0 %collective-permute-start.1 = (bf16[2,448,1344]{2,1,0:T(8,128)(2,1)}, bf16[2,448,1344]{2,1,0:T(8,128)(2,1)}, u32[]{:S(2)}, u32[]{:S(2)}) collective-permute-start(bf16[2,448,1344]{2,1,0:T(8,128)(2,1)} %pad_maximum_fusion), channel_id=1, source_target_pairs={{0,32},{8,40},{16,48},{24,56},{32,64},{40,72},{48,80},{56,88},{64,... | collective-permute-start | bytes 7225352 | tf_op jit(solution)/shard_map/ppermute | solution.py:64
  93.4 54.5 %collective-permute-start.2 = (bf16[2,448,1344]{2,1,0:T(8,128)(2,1)}, bf16[2,448,1344]{2,1,0:T(8,128)(2,1)}, u32[]{:S(2)}, u32[]{:S(2)}) collective-permute-start(bf16[2,448,1344]{2,1,0:T(8,128)(2,1)} %pad_maximum_fusion), channel_id=1, source_target_pairs={{0,96},{8,104},{16,112},{24,120},{32,0},{40,8},{48,16},{56,24},{64... | collective-permute-start | bytes 7225352 | tf_op jit(solution)/shard_map/ppermute | solution.py:65
  95.0 285.3 %reduce-scatter.2.cloned.1.call-start = ((), (), s32[]{:S(2)}) async-start(), calls=%async_computation.5 | async-start | bytes 8257536 | tf_op jit(solution)/shard_map/reduce_scatter | solution.py:187
  95.1 56.9 %copy-start.2 = (bf16[448,1344]{1,0:T(8,128)(2,1)S(1)}, bf16[448,1344]{1,0:T(8,128)(2,1)}, u32[]{:S(2)}) copy-start(bf16[448,1344]{1,0:T(8,128)(2,1)} %copy-done.1) | copy-start | bytes 3612676
  147.7 26.0 %collective-permute-start.3 = (bf16[448,1344]{1,0:T(8,128)(2,1)S(1)}, bf16[448,1344]{1,0:T(8,128)(2,1)S(1)}, u32[]{:S(2)}, u32[]{:S(2)}) collective-permute-start(bf16[448,1344]{1,0:T(8,128)(2,1)S(1)} %slice_bitcast_fusion.1), channel_id=1, source_target_pairs={{0,32},{8,40},{16,48},{24,56},{32,64},{40,72},{48,80},{56,88},{64,... | collective-permute-start | bytes 3612680 | tf_op jit(solution)/shard_map/ppermute | solution.py:67
  149.2 25.7 %collective-permute-start.4 = (bf16[448,1344]{1,0:T(8,128)(2,1)S(1)}, bf16[448,1344]{1,0:T(8,128)(2,1)S(1)}, u32[]{:S(2)}, u32[]{:S(2)}) collective-permute-start(bf16[448,1344]{1,0:T(8,128)(2,1)S(1)} %slice_bitcast_fusion), channel_id=1, source_target_pairs={{0,96},{8,104},{16,112},{24,120},{32,0},{40,8},{48,16},{56,24},{64... | collective-permute-start | bytes 3612680 | tf_op jit(solution)/shard_map/ppermute | solution.py:67
  160.0 22.2 %copy-start.7 = (s32[1024]{0:T(1024)S(1)}, s32[1024]{0:T(1024)}, u32[]{:S(2)}) copy-start(s32[1024]{0:T(1024)} %param.24) | copy-start | bytes 12292
  176.1 21.0 %collective-permute-start.5 = (bf16[8,448,1344]{2,1,0:T(8,128)(2,1)}, bf16[8,448,1344]{2,1,0:T(8,128)(2,1)}, u32[]{:S(2)}, u32[]{:S(2)}) collective-permute-start(bf16[8,448,1344]{2,1,0:T(8,128)(2,1)} %bitcast_dynamic-update-slice_fusion), channel_id=1, source_target_pairs={{0,8},{8,0},{16,24},{24,16},{32,40},{40,32},{48,56},{56,48},{64,72... | collective-permute-start | bytes 28901384 | tf_op jit(solution)/shard_map/ppermute | solution.py:70
  182.2 0.6 copy-start.10
  230.2 17.9 %copy-start.6 = (bf16[3,128,448]{1,2,0:T(8,128)(2,1)S(1)}, bf16[3,128,448]{1,2,0:T(8,128)(2,1)}, u32[]{:S(2)}) copy-start(bf16[3,128,448]{1,2,0:T(8,128)(2,1)} %param.22) | copy-start | bytes 1032196
  267.7 3.5 copy-start.3
  267.7 3.5 copy-start.16
  267.7 3.8 copy-start.17
  267.7 3.8 copy-start.18
  278.6 0.7 copy-start.12
  278.6 8.5 %copy-start.8 = (s32[1024]{0:T(1024)S(1)}, s32[1024]{0:T(1024)}, u32[]{:S(2)}) copy-start(s32[1024]{0:T(1024)} %param.24) | copy-start | bytes 12292
  278.6 8.5 %copy-start.11 = (pred[1024]{0:T(1024)(128)(4,1)S(1)}, pred[1024]{0:T(1024)(128)(4,1)}, u32[]{:S(2)}) copy-start(pred[1024]{0:T(1024)(128)(4,1)} %copy-done.10) | copy-start | bytes 3076
  279.9 17.9 %all-to-all-start = ((s32[16,1,4]{2,1,0:T(1,128)}), s32[16,1,4]{2,1,0:T(1,128)S(1)}, u32[]{:S(2)}, u32[]{:S(2)}) async-start(s32[16,1,4]{2,1,0:T(1,128)} %broadcast_in_dim.100), calls=%async_computation.1 | async-start | bytes 16384 | tf_op jit(solution)/shard_map/all_to_all | solution.py:168
  297.7 36.6 %all-to-all-start.1 = ((bf16[16,4,14336]{2,1,0:T(4,128)(2,1)}), bf16[16,4,14336]{2,1,0:T(4,128)(2,1)}, u32[]{:S(2)}, u32[]{:S(2)}) async-start(bf16[16,4,14336]{2,1,0:T(4,128)(2,1)} %reshape.307), calls=%async_computation.2 | async-start | bytes 3670016 | tf_op jit(solution)/shard_map/all_to_all | solution.py:167
Sparse Core Ops, SparseCore 0:
  32.3 116.1 all-gather.4
  150.7 79.4 all-gather.2
  278.7 101.4 reduce-scatter.1

commit v5 on v4

--- a/solution.py
+++ b/solution.py
@@ -75,6 +75,32 @@
     c_flip = jnp.array([0] * 8 + [1] * 8, jnp.int32)
     order = ((x + x_off) % 4) * 4 + (yh ^ y_flip) * 2 + (c ^ c_flip)
     return mine, other, order
+
+
+def tensor_perm(move):
+    return [(yl * 4 + z, move(yl, z)) for yl in range(2) for z in range(4)]
+
+
+def ring_scatter(partial_value):
+    t = lax.axis_index("tensor")
+    yl, z = t // 4, t % 4
+    blocks = partial_value.reshape(2, 4, -1, partial_value.shape[1])
+    send = lax.dynamic_index_in_dim(blocks, 1 - yl, 0, keepdims=False)
+    mine = lax.dynamic_index_in_dim(blocks, yl, 0, keepdims=False)
+    got = lax.ppermute(send, "tensor", tensor_perm(lambda a, b: (1 - a) * 4 + b))
+    summed = mine.astype(jnp.float32) + got.astype(jnp.float32)
+    half = summed.shape[2] // 2
+    outs = []
+    for direction, cols in ((1, slice(0, half)), (-1, slice(half, None))):
+        perm = tensor_perm(lambda a, b, d=direction: a * 4 + (b + d) % 4)
+        part = summed[:, :, cols]
+        acc = lax.dynamic_index_in_dim(part, (z - direction) % 4, 0, keepdims=False)
+        for k in range(3):
+            got = lax.ppermute(acc.astype(jnp.bfloat16), "tensor", perm)
+            own = lax.dynamic_index_in_dim(part, (z - direction * (k + 2)) % 4, 0, keepdims=False)
+            acc = got.astype(jnp.float32) + own
+        outs.append(acc)
+    return jnp.concatenate(outs, 1).astype(jnp.bfloat16)
 
 
 def body(
@@ -184,14 +210,14 @@
             attend_block(query, keys, values, segment, position, live, first, block, stream)
         )
     attended = jnp.concatenate(attended_parts, 0)
-    block_out = lax.psum_scatter(
-        jnp.dot(attended, output_projection_weight, preferred_element_type=jnp.float32).astype(
-            jnp.bfloat16
-        ),
-        "tensor",
-        scatter_dimension=0,
-        tiled=True,
-    )
+    partial_value = jnp.dot(
+        attended, output_projection_weight, preferred_element_type=jnp.float32
+    ).astype(jnp.bfloat16)
+    cols = partial_value.shape[1] // 2
+    on_sparse = lax.psum_scatter(
+        partial_value[:, :cols], "tensor", scatter_dimension=0, tiled=True
+    )
+    block_out = jnp.concatenate([on_sparse, ring_scatter(partial_value[:, cols:])], 1)
     return (block_out, kv_cache)
 
 

time: 388 us -> 450 us (1.16); the launches traced: 387 us -> 441 us
  waiting for transfers between devices: 199 us -> 226 us
  local copies, waits for them, and re-layouts: 52 us -> 62.9 us
  other arithmetic: 15.7 us -> 26 us
  starting transfers between devices: 29.2 us -> 38.5 us
    all_to_all x1, waiting for transfers between devices: 28.1 us -> 74.7 us  [body(): lax.all_to_all(taken, 'dp', split_axis=0, concat_axis=0, tiled=True)]
    reduce_scatter x1, waiting for transfers between devices: 31.7 us -> 0.01 us  [body(): lax.psum_scatter(partial_value[:, :cols], 'tensor', scatter_dimension=0,...]
    ppermute x0 -> x7, waiting for transfers between devices: none -> 11.9 us  [the longest x6 11.9 us: ring_scatter(): got = lax.ppermute(acc.astype(jnp.bfloat16), 'tensor', perm)]
    ppermute x0 -> x7, starting transfers between devices: none -> 7.6 us  [the longest x6 7.6 us: ring_scatter(): got = lax.ppermute(acc.astype(jnp.bfloat16), 'tensor', perm)]
    slice x0 -> x2, local copies, waits for them, and re-layouts: none -> 4.89 us  [the longest x1 3.39 us: body(): partial_value[:, :cols]]
    unnamed x45 -> x53, local copies, waits for them, and re-layouts: 18.5 us -> 19.7 us
  transfers between devices with their start and end apart: 11 -> 18, of which waited for: 7 -> 9; matrix products, arithmetic and copies ran while one was open for 18% -> 19% of each run, Pallas kernels for 0% -> 0%
where the time goes in v5:
time: 450 us; the launch traced here: 441 us
  waiting for transfers between devices  226 us (50%)
  matrix products  72.7 us (16%)
  local copies, waits for them, and re-layouts  62.9 us (14%)
  starting transfers between devices  38.5 us (9%)
  other arithmetic  26 us (6%)
  between operations  15.3 us (3%)
    all_to_all x1, waiting for transfers between devices, body(): lax.all_to_all(taken, 'dp', split_axis=0, concat_axis=0, tiled=True)  74.7 us
    ppermute x1, waiting for transfers between devices, gather_weights(): from_prev = lax.ppermute(pair, 'dp', to_next)  48.7 us
    ppermute x1, waiting for transfers between devices, gather_weights(): pair = jnp.stack([weight_shard, lax.ppermute(weight_shard, 'dp', to_yh)])  48.6 us
    unnamed x53, local copies, waits for them, and re-layouts  19.7 us
    dot_general x1, matrix products, body(): jnp.dot(low_part, mine.reshape(split, 3 * head_cols), preferred_element_t...  18 us
    dot_general x1, matrix products, body(): jnp.dot(high_part[:, :split], other.reshape(split, 3 * head_cols), prefer...  17.1 us
    all_gather x1, waiting for transfers between devices, body(): lax.all_gather(in_order[:, :split], 'tensor', axis=0, tiled=True)  15.7 us
    ppermute x1, waiting for transfers between devices, gather_weights(): lax.ppermute(from_prev[0], 'dp', to_next)  13.7 us
  transfers between devices with their start and end apart: 18, of which 9 were waited for; matrix products, arithmetic and copies ran while one was open for 19% of the time, Pallas kernels for 0%

profile of v5, /device:TPU:1, one launch (start us, length us, event | category | flops | bytes accessed | tf_op | source)
XLA Modules:
  0.0 440.7 jit_solution(6628828395986777358)
XLA Ops:
  7.3 2.4 copy.24
  9.6 1.9 fusion.7
  11.5 2.2 copy.23
  13.9 4.4 %fusion.40 = bf16[128,384]{1,0:T(8,128)(2,1)S(1)} fusion(bf16[7168,384]{1,0:T(8,128)(2,1)} %param.21, f32[7168]{0:T(1024)S(1)} %copy-done.13, f32[128]{0:T(128)S(1)} %add_rsqrt_fusion, bf16[128,3584]{1,0:T(8,128)(2,1)} %param.16, bf16[128,3584]{1,0:T(8,128)(2,1)} %param.15), kind=kOutput, calls=%fused_computation.65 | convolution fusion | flops 711114752 | bytes 7467520 | tf_op jit(solution)/shard_map/dot_general | solution.py:133
  18.4 2.5 multiply_convert_fusion
  20.8 3.5 gather_fusion
  24.4 3.9 copy.25
  28.4 1.7 broadcast_select_fusion
  32.3 3.5 concatenate.33
  35.8 3.7 collective-permute-start
  39.5 48.6 %collective-permute-done = bf16[448,1344]{1,0:T(8,128)(2,1)S(1)} collective-permute-done((bf16[448,1344]{1,0:T(8,128)(2,1)}, bf16[448,1344]{1,0:T(8,128)(2,1)S(1)}, u32[]{:S(2)}, u32[]{:S(2)}) %collective-permute-start) | collective-permute-done | bytes 1204256 | tf_op jit(solution)/shard_map/ppermute | solution.py:63
  88.1 1.1 copy-done.3
  89.3 3.0 pad_maximum_fusion
  93.3 1.6 collective-permute-start.2
  95.0 2.5 constant_dynamic-update-slice_fusion.3
  97.6 48.7 %collective-permute-done.1 = bf16[2,448,1344]{2,1,0:T(8,128)(2,1)} collective-permute-done((bf16[2,448,1344]{2,1,0:T(8,128)(2,1)}, bf16[2,448,1344]{2,1,0:T(8,128)(2,1)}, u32[]{:S(2)}, u32[]{:S(2)}) %collective-permute-start.1) | collective-permute-done | bytes 2408480 | tf_op jit(solution)/shard_map/ppermute | solution.py:64
  146.3 1.4 slice_bitcast_fusion.1
  147.8 1.4 slice_bitcast_fusion
  149.2 2.7 collective-permute-start.4
  151.9 1.2 constant_dynamic-update-slice_fusion.2
  153.1 3.3 constant_dynamic-update-slice_fusion.1
  156.5 3.6 constant_dynamic-update-slice_fusion
  160.1 13.7 %collective-permute-done.3 = bf16[448,1344]{1,0:T(8,128)(2,1)S(1)} collective-permute-done((bf16[448,1344]{1,0:T(8,128)(2,1)S(1)}, bf16[448,1344]{1,0:T(8,128)(2,1)S(1)}, u32[]{:S(2)}, u32[]{:S(2)}) %collective-permute-start.3) | collective-permute-done | bytes 1204256 | tf_op jit(solution)/shard_map/ppermute | solution.py:67
  173.7 1.1 bitcast_dynamic-update-slice_fusion.1
  174.9 1.2 bitcast_dynamic-update-slice_fusion
  176.0 5.9 %collective-permute-start.5 = (bf16[8,448,1344]{2,1,0:T(8,128)(2,1)}, bf16[8,448,1344]{2,1,0:T(8,128)(2,1)}, u32[]{:S(2)}, u32[]{:S(2)}) collective-permute-start(bf16[8,448,1344]{2,1,0:T(8,128)(2,1)} %bitcast_dynamic-update-slice_fusion), channel_id=1, source_target_pairs={{0,8},{8,0},{16,24},{24,16},{32,40},{40,32},{48,56},{56,48},{64,72... | collective-permute-start | bytes 28901384 | tf_op jit(solution)/shard_map/ppermute | solution.py:70
  183.2 2.1 fusion.21
  185.3 12.1 %collective-permute-done.5 = bf16[8,448,1344]{2,1,0:T(8,128)(2,1)} collective-permute-done((bf16[8,448,1344]{2,1,0:T(8,128)(2,1)}, bf16[8,448,1344]{2,1,0:T(8,128)(2,1)}, u32[]{:S(2)}, u32[]{:S(2)}) %collective-permute-start.5) | collective-permute-done | bytes 9633824 | tf_op jit(solution)/shard_map/ppermute | solution.py:70
  197.4 17.1 %fusion.2 = f32[1024,1344]{0,1:T(8,128)} fusion(bf16[3584,1344]{1,0:T(8,128)(2,1)} %bitcast.12, bf16[1024,3968]{1,0:T(8,128)(2,1)} %all-gather.5.cloned.1.call-done), kind=kOutput, calls=%fused_computation.5 | convolution fusion | flops 9865003008 | bytes 22937600 | tf_op jit(solution)/shard_map/dot_general | solution.py:149
  214.6 15.7 %all-gather.3.cloned.1.call-done = bf16[1024,3584]{1,0:T(8,128)(2,1)} async-done(((bf16[128,3584]{1,0:T(8,128)(2,1)}), bf16[1024,3584]{1,0:T(8,128)(2,1)}) %all-gather.3.cloned.1.call-update) | async-done | bytes 7340048 | tf_op jit(solution)/shard_map/all_gather | solution.py:138
  230.3 18.0 %convolution_add_fusion = f32[1024,1344]{0,1:T(8,128)} fusion(f32[1024,1344]{0,1:T(8,128)} %fusion.2, bf16[1024,3584]{1,0:T(8,128)(2,1)} %all-gather.3.cloned.1.call-done, bf16[3584,1344]{1,0:T(8,128)(2,1)} %bitcast.11), kind=kOutput, calls=%fused_computation.9 | convolution fusion | flops 9866379264 | bytes 27983872 | tf_op jit(solution)/shard_map/dot_general | solution.py:140
  248.3 2.0 fusion.29
  251.3 2.9 fusion.28
  254.2 5.8 %fusion.84 = (f32[2,512]{1,0:T(2,128)}, f32[2,512,1024]{2,1,0:T(8,128)}) fusion(pred[512,1024]{1,0:T(8,128)(4,1)} %get-tuple-element.13, bf16[512,2,224]{0,2,1:T(8,128)(2,1)} %bitcast.113, bf16[1024,2,224]{0,2,1:T(8,128)(2,1)} %bitcast.103), kind=kOutput, calls=%fused_computation.137 | convolution fusion | flops 473957376 | bytes 6098944 | tf_op jit(solution)/shard_map/sub | solution.py:38
  260.0 5.8 %fusion.85 = (f32[2,512]{1,0:T(2,128)}, f32[2,512,1024]{2,1,0:T(8,128)}) fusion(pred[512,1024]{1,0:T(8,128)(4,1)} %get-tuple-element.12, bf16[512,2,224]{0,2,1:T(8,128)(2,1)} %bitcast.112, bf16[1024,2,224]{0,2,1:T(8,128)(2,1)} %bitcast.104), kind=kOutput, calls=%fused_computation.138 | convolution fusion | flops 473957376 | bytes 6098944 | tf_op jit(solution)/shard_map/sub | solution.py:38
  265.8 2.0 fusion.30
  267.8 3.5 fusion.37
  272.5 4.3 convolution_convert_fusion.1
  276.8 3.4 fusion.79
  281.5 7.3 %all-to-all-start = ((s32[16,1,4]{2,1,0:T(1,128)}), s32[16,1,4]{2,1,0:T(1,128)S(1)}, u32[]{:S(2)}, u32[]{:S(2)}) async-start(s32[16,1,4]{2,1,0:T(1,128)} %broadcast_in_dim.100), calls=%async_computation.1 | async-start | bytes 16384 | tf_op jit(solution)/shard_map/all_to_all | solution.py:194
  289.5 3.0 dynamic-slice_bitcast_fusion
  292.7 3.9 fusion.33
  296.6 4.3 reshape.315
  300.9 8.4 %all-to-all-start.1 = ((bf16[16,4,14336]{2,1,0:T(4,128)(2,1)}), bf16[16,4,14336]{2,1,0:T(4,128)(2,1)}, u32[]{:S(2)}, u32[]{:S(2)}) async-start(bf16[16,4,14336]{2,1,0:T(4,128)(2,1)} %reshape.315), calls=%async_computation.2 | async-start | bytes 3670016 | tf_op jit(solution)/shard_map/all_to_all | solution.py:193
  310.7 74.7 %all-to-all-done.1 = bf16[16,4,14336]{2,1,0:T(4,128)(2,1)} async-done(((bf16[16,4,14336]{2,1,0:T(4,128)(2,1)}), bf16[16,4,14336]{2,1,0:T(4,128)(2,1)}, u32[]{:S(2)}, u32[]{:S(2)}) %all-to-all-start.1) | async-done | bytes 1835040 | tf_op jit(solution)/shard_map/all_to_all | solution.py:193
  385.5 3.9 reshape.316
  389.4 2.4 convert_add_fusion
  391.8 1.5 fusion.80
  393.3 1.2 copy-done.2
  395.3 1.9 collective-permute-start.10
  397.2 2.1 convolution_convert_fusion
  399.3 6.8 %reshape.317 = bf16[64,16,2,448]{3,2,1,0:T(2,128)(2,1)} reshape(bf16[64,14336]{1,0:T(8,128)(2,1)} %convolution_convert_fusion) | data formatting | bytes 3670016 | tf_op jit(solution)/shard_map/reshape | solution.py:204
  407.2 1.1 fusion.48
  408.3 2.7 collective-permute-start.11
  411.0 3.9 collective-permute-done.7
  414.9 1.1 fusion.51
  416.0 1.1 fusion.47
  417.1 2.7 collective-permute-start.12
  419.8 3.0 collective-permute-done.8
  422.8 1.1 fusion.50
  424.0 1.1 fusion.46
  425.1 5.0 %collective-permute-done.9 = bf16[128,896]{1,0:T(8,128)(2,1)S(1)} collective-permute-done((bf16[128,896]{1,0:T(8,128)(2,1)S(1)}, bf16[128,896]{1,0:T(8,128)(2,1)S(1)}, u32[]{:S(2)}, u32[]{:S(2)}) %collective-permute-start.9) | collective-permute-done | bytes 229408 | tf_op jit(solution)/shard_map/ppermute | solution.py:99
  430.1 1.8 fusion.49
  431.8 2.1 pad_maximum_fusion.5
  (98 shorter events, 12.0 us)
Async XLA Ops:
  7.2 265.4 %copy-start = (bf16[448,3584]{1,0:T(8,128)(2,1)S(1)}, bf16[448,3584]{1,0:T(8,128)(2,1)}, u32[]{:S(2)}) copy-start(bf16[448,3584]{1,0:T(8,128)(2,1)} %param.23) | copy-start | bytes 9633796
  7.2 6.7 %copy-start.17 = (s32[16]{0:T(128)S(1)}, s32[16]{0:T(128)}, u32[]{:S(2)}) copy-start(s32[16]{0:T(128)} %constant.189.clone) | copy-start | bytes 196
  7.2 6.6 %copy-start.18 = (s32[16]{0:T(128)S(1)}, s32[16]{0:T(128)}, u32[]{:S(2)}) copy-start(s32[16]{0:T(128)} %constant.188.clone) | copy-start | bytes 196
  7.2 6.6 %copy-start.19 = (s32[16]{0:T(128)S(1)}, s32[16]{0:T(128)}, u32[]{:S(2)}) copy-start(s32[16]{0:T(128)} %constant.187.clone) | copy-start | bytes 196
  7.2 6.5 %copy-start.13 = (f32[7168]{0:T(1024)S(1)}, f32[7168]{0:T(1024)}, u32[]{:S(2)}) copy-start(f32[7168]{0:T(1024)} %param.17) | copy-start | bytes 86020
  7.2 178.1 %all-gather.5.cloned.1.call-start = ((), (), s32[]{:S(2)}) async-start(), calls=%async_computation.4 | async-start | bytes 9142272 | tf_op jit(solution)/shard_map/all_gather | solution.py:144
  13.9 4.5 %copy-start.8 = (bf16[128,3584]{0,1:T(8,128)(2,1)S(1)}, bf16[128,3584]{0,1:T(8,128)(2,1)}, u32[]{:S(2)}) copy-start(bf16[128,3584]{0,1:T(8,128)(2,1)} %copy.24) | copy-start | bytes 2752516
  13.9 4.5 %copy-start.9 = (bf16[128,3584]{0,1:T(8,128)(2,1)S(1)}, bf16[128,3584]{0,1:T(8,128)(2,1)}, u32[]{:S(2)}) copy-start(bf16[128,3584]{0,1:T(8,128)(2,1)} %copy.23) | copy-start | bytes 2752516
  32.2 198.0 %all-gather.3.cloned.1.call-start = ((), (), s32[]{:S(2)}) async-start(), calls=%async_computation.3 | async-start | bytes 8257536 | tf_op jit(solution)/shard_map/all_gather | solution.py:138
  35.8 52.3 %collective-permute-start = (bf16[448,1344]{1,0:T(8,128)(2,1)}, bf16[448,1344]{1,0:T(8,128)(2,1)S(1)}, u32[]{:S(2)}, u32[]{:S(2)}) collective-permute-start(bf16[448,1344]{1,0:T(8,128)(2,1)} %concatenate.33), channel_id=1, source_target_pairs={{0,16},{8,24},{16,0},{24,8},{32,48},{40,56},{48,32},{56,40},{64,80... | collective-permute-start | bytes 3612680 | tf_op jit(solution)/shard_map/ppermute | solution.py:63
  88.1 1.1 copy-start.3
  92.3 54.0 %collective-permute-start.1 = (bf16[2,448,1344]{2,1,0:T(8,128)(2,1)}, bf16[2,448,1344]{2,1,0:T(8,128)(2,1)}, u32[]{:S(2)}, u32[]{:S(2)}) collective-permute-start(bf16[2,448,1344]{2,1,0:T(8,128)(2,1)} %pad_maximum_fusion), channel_id=1, source_target_pairs={{0,32},{8,40},{16,48},{24,56},{32,64},{40,72},{48,80},{56,88},{64,... | collective-permute-start | bytes 7225352 | tf_op jit(solution)/shard_map/ppermute | solution.py:64
  93.3 54.5 %collective-permute-start.2 = (bf16[2,448,1344]{2,1,0:T(8,128)(2,1)}, bf16[2,448,1344]{2,1,0:T(8,128)(2,1)}, u32[]{:S(2)}, u32[]{:S(2)}) collective-permute-start(bf16[2,448,1344]{2,1,0:T(8,128)(2,1)} %pad_maximum_fusion), channel_id=1, source_target_pairs={{0,96},{8,104},{16,112},{24,120},{32,0},{40,8},{48,16},{56,24},{64... | collective-permute-start | bytes 7225352 | tf_op jit(solution)/shard_map/ppermute | solution.py:65
  95.0 336.9 %reduce-scatter.2.cloned.1.call-start = ((), (), s32[]{:S(2)}) async-start(), calls=%async_computation.5 | async-start | bytes 4128768 | tf_op jit(solution)/shard_map/reduce_scatter | solution.py:217
  95.0 56.9 %copy-start.4 = (bf16[448,1344]{1,0:T(8,128)(2,1)S(1)}, bf16[448,1344]{1,0:T(8,128)(2,1)}, u32[]{:S(2)}) copy-start(bf16[448,1344]{1,0:T(8,128)(2,1)} %copy-done.3) | copy-start | bytes 3612676
  147.7 26.0 %collective-permute-start.3 = (bf16[448,1344]{1,0:T(8,128)(2,1)S(1)}, bf16[448,1344]{1,0:T(8,128)(2,1)S(1)}, u32[]{:S(2)}, u32[]{:S(2)}) collective-permute-start(bf16[448,1344]{1,0:T(8,128)(2,1)S(1)} %slice_bitcast_fusion.1), channel_id=1, source_target_pairs={{0,32},{8,40},{16,48},{24,56},{32,64},{40,72},{48,80},{56,88},{64,... | collective-permute-start | bytes 3612680 | tf_op jit(solution)/shard_map/ppermute | solution.py:67
  149.2 25.6 %collective-permute-start.4 = (bf16[448,1344]{1,0:T(8,128)(2,1)S(1)}, bf16[448,1344]{1,0:T(8,128)(2,1)S(1)}, u32[]{:S(2)}, u32[]{:S(2)}) collective-permute-start(bf16[448,1344]{1,0:T(8,128)(2,1)S(1)} %slice_bitcast_fusion), channel_id=1, source_target_pairs={{0,96},{8,104},{16,112},{24,120},{32,0},{40,8},{48,16},{56,24},{64... | collective-permute-start | bytes 3612680 | tf_op jit(solution)/shard_map/ppermute | solution.py:67
  160.1 22.5 %copy-start.11 = (s32[1024]{0:T(1024)S(1)}, s32[1024]{0:T(1024)}, u32[]{:S(2)}) copy-start(s32[1024]{0:T(1024)} %param.24) | copy-start | bytes 12292
  176.0 21.4 %collective-permute-start.5 = (bf16[8,448,1344]{2,1,0:T(8,128)(2,1)}, bf16[8,448,1344]{2,1,0:T(8,128)(2,1)}, u32[]{:S(2)}, u32[]{:S(2)}) collective-permute-start(bf16[8,448,1344]{2,1,0:T(8,128)(2,1)} %bitcast_dynamic-update-slice_fusion), channel_id=1, source_target_pairs={{0,8},{8,0},{16,24},{24,16},{32,40},{40,32},{48,56},{56,48},{64,72... | collective-permute-start | bytes 28901384 | tf_op jit(solution)/shard_map/ppermute | solution.py:70
  182.6 0.6 copy-start.14
  230.3 18.0 %copy-start.10 = (bf16[3,128,448]{1,2,0:T(8,128)(2,1)S(1)}, bf16[3,128,448]{1,2,0:T(8,128)(2,1)}, u32[]{:S(2)}) copy-start(bf16[3,128,448]{1,2,0:T(8,128)(2,1)} %param.22) | copy-start | bytes 1032196
  267.8 3.5 copy-start.6
  267.8 3.5 copy-start.20
  267.8 3.8 copy-start.21
  267.8 3.8 copy-start.22
  280.2 0.7 copy-start.16
  280.2 8.5 %copy-start.12 = (s32[1024]{0:T(1024)S(1)}, s32[1024]{0:T(1024)}, u32[]{:S(2)}) copy-start(s32[1024]{0:T(1024)} %param.24) | copy-start | bytes 12292
  280.2 8.5 %copy-start.15 = (pred[1024]{0:T(1024)(128)(4,1)S(1)}, pred[1024]{0:T(1024)(128)(4,1)}, u32[]{:S(2)}) copy-start(pred[1024]{0:T(1024)(128)(4,1)} %copy-done.14) | copy-start | bytes 3076
  281.5 19.4 %all-to-all-start = ((s32[16,1,4]{2,1,0:T(1,128)}), s32[16,1,4]{2,1,0:T(1,128)S(1)}, u32[]{:S(2)}, u32[]{:S(2)}) async-start(s32[16,1,4]{2,1,0:T(1,128)} %broadcast_in_dim.100), calls=%async_computation.1 | async-start | bytes 16384 | tf_op jit(solution)/shard_map/all_to_all | solution.py:194
  289.5 3.0 copy-start.5
  289.5 3.0 copy-start.7
  292.5 96.9 %collective-permute-start.6 = (bf16[4,128,1792]{2,1,0:T(8,128)(2,1)}, bf16[4,128,1792]{2,1,0:T(8,128)(2,1)}, u32[]{:S(2)}, u32[]{:S(2)}) collective-permute-start(bf16[4,128,1792]{2,1,0:T(8,128)(2,1)} %dynamic-slice_bitcast_fusion), channel_id=1, source_target_pairs={{0,4},{1,5},{2,6},{3,7},{4,0},{5,1},{6,2},{7,3},{8,12},{9,13},{10,... | collective-permute-start | bytes 5505032 | tf_op jit(solution)/shard_map/ppermute | solution.py:90
  300.9 84.6 %all-to-all-start.1 = ((bf16[16,4,14336]{2,1,0:T(4,128)(2,1)}), bf16[16,4,14336]{2,1,0:T(4,128)(2,1)}, u32[]{:S(2)}, u32[]{:S(2)}) async-start(bf16[16,4,14336]{2,1,0:T(4,128)(2,1)} %reshape.315), calls=%async_computation.2 | async-start | bytes 3670016 | tf_op jit(solution)/shard_map/all_to_all | solution.py:193
  391.8 5.4 %copy-start.1 = (bf16[64,14336]{1,0:T(8,128)(2,1)S(1)}, bf16[64,14336]{1,0:T(8,128)(2,1)}, u32[]{:S(2)}) copy-start(bf16[64,14336]{1,0:T(8,128)(2,1)} %reshape.316) | copy-start | bytes 5505028
  393.3 1.2 copy-start.2
  395.3 11.9 %collective-permute-start.10 = (bf16[128,896]{1,0:T(8,128)(2,1)}, bf16[128,896]{1,0:T(8,128)(2,1)S(1)}, u32[]{:S(2)}, u32[]{:S(2)}) collective-permute-start(bf16[128,896]{1,0:T(8,128)(2,1)} %fusion.56), channel_id=1, source_target_pairs={{0,3},{1,0},{2,1},{3,2},{4,7},{5,4},{6,5},{7,6},{8,11},{9,8},{10,9... | collective-permute-start | bytes 688136 | tf_op jit(solution)/shard_map/ppermute | solution.py:99
  407.1 7.8 %collective-permute-start.7 = (bf16[128,896]{1,0:T(8,128)(2,1)S(1)}, bf16[128,896]{1,0:T(8,128)(2,1)S(1)}, u32[]{:S(2)}, u32[]{:S(2)}) collective-permute-start(bf16[128,896]{1,0:T(8,128)(2,1)S(1)} %fusion.55), channel_id=1, source_target_pairs={{0,1},{1,2},{2,3},{3,0},{4,5},{5,6},{6,7},{7,4},{8,9},{9,10},{10,1... | collective-permute-start | bytes 688136 | tf_op jit(solution)/shard_map/ppermute | solution.py:99
  408.3 7.8 %collective-permute-start.11 = (bf16[128,896]{1,0:T(8,128)(2,1)S(1)}, bf16[128,896]{1,0:T(8,128)(2,1)S(1)}, u32[]{:S(2)}, u32[]{:S(2)}) collective-permute-start(bf16[128,896]{1,0:T(8,128)(2,1)S(1)} %fusion.48), channel_id=1, source_target_pairs={{0,3},{1,0},{2,1},{3,2},{4,7},{5,4},{6,5},{7,6},{8,11},{9,8},{10,9... | collective-permute-start | bytes 688136 | tf_op jit(solution)/shard_map/ppermute | solution.py:99
  415.9 6.9 %collective-permute-start.8 = (bf16[128,896]{1,0:T(8,128)(2,1)S(1)}, bf16[128,896]{1,0:T(8,128)(2,1)S(1)}, u32[]{:S(2)}, u32[]{:S(2)}) collective-permute-start(bf16[128,896]{1,0:T(8,128)(2,1)S(1)} %fusion.51), channel_id=1, source_target_pairs={{0,1},{1,2},{2,3},{3,0},{4,5},{5,6},{6,7},{7,4},{8,9},{9,10},{10,1... | collective-permute-start | bytes 688136 | tf_op jit(solution)/shard_map/ppermute | solution.py:99
  417.1 6.9 %collective-permute-start.12 = (bf16[128,896]{1,0:T(8,128)(2,1)S(1)}, bf16[128,896]{1,0:T(8,128)(2,1)S(1)}, u32[]{:S(2)}, u32[]{:S(2)}) collective-permute-start(bf16[128,896]{1,0:T(8,128)(2,1)S(1)} %fusion.47), channel_id=1, source_target_pairs={{0,3},{1,0},{2,1},{3,2},{4,7},{5,4},{6,5},{7,6},{8,11},{9,8},{10,9... | collective-permute-start | bytes 688136 | tf_op jit(solution)/shard_map/ppermute | solution.py:99
  423.9 6.2 %collective-permute-start.9 = (bf16[128,896]{1,0:T(8,128)(2,1)S(1)}, bf16[128,896]{1,0:T(8,128)(2,1)S(1)}, u32[]{:S(2)}, u32[]{:S(2)}) collective-permute-start(bf16[128,896]{1,0:T(8,128)(2,1)S(1)} %fusion.50), channel_id=1, source_target_pairs={{0,1},{1,2},{2,3},{3,0},{4,5},{5,6},{6,7},{7,4},{8,9},{9,10},{10,1... | collective-permute-start | bytes 688136 | tf_op jit(solution)/shard_map/ppermute | solution.py:99
Sparse Core Ops, SparseCore 0:
  32.3 116.1 all-gather.4
  150.7 79.4 all-gather.2
  280.4 92.9 reduce-scatter.1

commit v6 on v4

--- a/solution.py
+++ b/solution.py
@@ -3,8 +3,8 @@
 import jax
 import jax.numpy as jnp
 from jax import lax
-from jax.sharding import PartitionSpec as P
-from jax.experimental.layout import Layout, with_layout_constraint
+from jax.sharding import Mesh, PartitionSpec as P
+
 
 HD = 224
 
@@ -42,39 +42,53 @@
     return mixed.astype(jnp.bfloat16).reshape(count, heads * HD)
 
 
-def dp_index(x, yh, c):
-    return x * 4 + yh * 2 + c
-
-
-def dp_perm(move):
-    return [
-        (dp_index(x, yh, c), dp_index(*move(x, yh, c)))
-        for x in range(4)
-        for yh in range(2)
-        for c in range(2)
-    ]
-
-
 def gather_weights(weight_shard):
-    to_yh = dp_perm(lambda x, yh, c: (x, 1 - yh, c))
-    to_next = dp_perm(lambda x, yh, c: ((x + 1) % 4, yh, c))
-    to_prev = dp_perm(lambda x, yh, c: ((x - 1) % 4, yh, c))
-    to_core = dp_perm(lambda x, yh, c: (x, yh, 1 - c))
-    pair = jnp.stack([weight_shard, lax.ppermute(weight_shard, "dp", to_yh)])
-    from_prev = lax.ppermute(pair, "dp", to_next)
-    from_next = lax.ppermute(pair, "dp", to_prev)
-    far = jnp.stack(
-        [lax.ppermute(from_prev[0], "dp", to_next), lax.ppermute(from_next[1], "dp", to_prev)]
-    )
-    mine = jnp.concatenate([pair, from_prev, from_next, far], 0)
-    other = lax.ppermute(mine, "dp", to_core)
-    d = lax.axis_index("dp")
-    x, yh, c = d // 4, (d // 2) % 2, d % 2
-    x_off = jnp.array([0, 0, -1, -1, 1, 1, 2, 2] * 2, jnp.int32)
-    y_flip = jnp.array([0, 1] * 8, jnp.int32)
-    c_flip = jnp.array([0] * 8 + [1] * 8, jnp.int32)
-    order = ((x + x_off) % 4) * 4 + (yh ^ y_flip) * 2 + (c ^ c_flip)
+    mine = lax.all_gather(weight_shard, "dpo", axis=0, tiled=False)
+    other = lax.ppermute(mine, "core", [(0, 1), (1, 0)])
+    c = lax.axis_index("core")
+    chips = mine.shape[0]
+    k = jnp.arange(chips, dtype=jnp.int32)
+    order = jnp.concatenate([2 * k + c, 2 * k + 1 - c])
     return mine, other, order
+
+
+def tensor_perm(move):
+    return [(yl * 4 + z, move(yl, z)) for yl in range(2) for z in range(4)]
+
+
+def gather_rows(local):
+    to_next = tensor_perm(lambda yl, z: yl * 4 + (z + 1) % 4)
+    to_prev = tensor_perm(lambda yl, z: yl * 4 + (z - 1) % 4)
+    to_pair = tensor_perm(lambda yl, z: (1 - yl) * 4 + z)
+    from_prev = lax.ppermute(local, "tensor", to_next)
+    from_next = lax.ppermute(local, "tensor", to_prev)
+    from_pair = lax.ppermute(local, "tensor", to_pair)
+    pair_next = lax.ppermute(from_next, "tensor", to_pair)
+    next_next = lax.ppermute(from_next, "tensor", to_prev)
+    pair_prev = lax.ppermute(from_pair, "tensor", to_next)
+    cut = (local.shape[1] // 256) * 128
+    pair_far = jnp.concatenate(
+        [
+            lax.ppermute(pair_next[:, :cut], "tensor", to_prev),
+            lax.ppermute(pair_prev[:, cut:], "tensor", to_next),
+        ],
+        1,
+    )
+    t = lax.axis_index("tensor")
+    yl, z = t // 4, t % 4
+    at = lambda a, b: a * 4 + b % 4
+    row_blocks = jnp.stack(
+        [
+            at(yl, z), at(yl, z - 1), at(yl, z + 1), at(1 - yl, z),
+            at(1 - yl, z + 1), at(yl, z + 2), at(1 - yl, z - 1), at(1 - yl, z + 2),
+        ]
+    ).astype(jnp.int32)
+    groups_in = (
+        jnp.concatenate([local, from_prev, from_next, from_pair], 0),
+        jnp.concatenate([pair_next, next_next, pair_prev], 0),
+        pair_far,
+    )
+    return groups_in, row_blocks
 
 
 def body(
@@ -107,23 +121,23 @@
     low_local = jnp.dot(
         normalized_hidden, adapter_down_maps, preferred_element_type=jnp.float32
     ).astype(jnp.bfloat16)
-    row_major = Layout((0, 1))
-    low_part = with_layout_constraint(
-        lax.all_gather(in_order[:, :split], "tensor", axis=0, tiled=True), row_major
-    )
-    folded_all = jnp.dot(
-        low_part, mine.reshape(split, 3 * head_cols), preferred_element_type=jnp.float32
-    )
-    high_part = with_layout_constraint(
-        lax.all_gather(
-            jnp.concatenate([in_order[:, split:], low_local], 1), "tensor", axis=0, tiled=True
-        ),
-        row_major,
-    )
-    folded_all = folded_all + jnp.dot(
-        high_part[:, :split], other.reshape(split, 3 * head_cols), preferred_element_type=jnp.float32
-    )
-    adapter_update = high_part[:, split:]
+    low_local = jnp.dot(
+        normalized_hidden, adapter_down_maps, preferred_element_type=jnp.float32
+    ).astype(jnp.bfloat16)
+    groups_in, row_blocks = gather_rows(jnp.concatenate([in_order, low_local], 1))
+    split = mine.shape[0] * block_rows
+    pieces = []
+    for rows_in in groups_in:
+        term = jnp.dot(
+            rows_in[:, :split], mine.reshape(split, 3 * head_cols),
+            preferred_element_type=jnp.float32,
+        ) + jnp.dot(
+            rows_in[:, split : 2 * split], other.reshape(split, 3 * head_cols),
+            preferred_element_type=jnp.float32,
+        )
+        pieces.append((term, rows_in[:, 2 * split :]))
+    folded_all = jnp.concatenate([p[0] for p in pieces], 0)
+    adapter_update = jnp.concatenate([p[1] for p in pieces], 0)
     folded = [folded_all[:, k * head_cols : (k + 1) * head_cols] for k in range(3)]
     projected = []
     for adapter_selector in range(3):
@@ -138,14 +152,17 @@
         projected.append((folded[adapter_selector] + adapter).astype(jnp.bfloat16))
     query, keys, values = projected
     stream = query.shape[0]
-    position = jnp.arange(stream, dtype=jnp.int32)
+    rows = stream // row_blocks.shape[0]
+    position = (row_blocks[:, None] * rows + jnp.arange(rows, dtype=jnp.int32)[None, :]).reshape(-1)
+    segment_at = jnp.take(segment, position)
     live = live_token_length[0]
     requests = request_cache_row.shape[0]
     longest = stream // requests
-    groups = lax.axis_size("dp")
+    groups = lax.axis_size("dpo") * lax.axis_size("core")
     piece_len = longest // groups
     numbers = jnp.arange(requests, dtype=jnp.int32)
-    membership = ((segment[:, None] == numbers[None, :]) & (position < live)[:, None]).astype(
+    absolute = jnp.arange(stream, dtype=jnp.int32)
+    membership = ((segment[:, None] == numbers[None, :]) & (absolute < live)[:, None]).astype(
         jnp.int32
     )
     lengths = jnp.sum(membership, axis=0)
@@ -164,8 +181,8 @@
     taken = taken.reshape(groups, requests, piece_len * 2 * head_cols)
     row_send = jnp.broadcast_to(request_cache_row[None, :], (groups, requests))
     received, received_rows = (
-        lax.all_to_all(taken, "dp", split_axis=0, concat_axis=0, tiled=True),
-        lax.all_to_all(row_send, "dp", split_axis=0, concat_axis=0, tiled=True),
+        lax.all_to_all(taken, ("dpo", "core"), split_axis=0, concat_axis=0, tiled=True),
+        lax.all_to_all(row_send, ("dpo", "core"), split_axis=0, concat_axis=0, tiled=True),
     )
     total_reqs = groups * requests
     placing = (
@@ -181,9 +198,10 @@
     for block_index in range(stream // block):
         first = block_index * block
         attended_parts.append(
-            attend_block(query, keys, values, segment, position, live, first, block, stream)
+            attend_block(query, keys, values, segment_at, position, live, first, block, stream)
         )
-    attended = jnp.concatenate(attended_parts, 0)
+    arrival = jnp.zeros_like(position).at[position].set(absolute)
+    attended = jnp.take(jnp.concatenate(attended_parts, 0), arrival, axis=0)
     block_out = lax.psum_scatter(
         jnp.dot(attended, output_projection_weight, preferred_element_type=jnp.float32).astype(
             jnp.bfloat16
@@ -196,23 +214,27 @@
 
 
 def solution(mesh):
+    dp, tensor = mesh.devices.shape
+    split_mesh = Mesh(mesh.devices.reshape(dp // 2, 2, tensor), ("dpo", "core", "tensor"))
+    rows = ("dpo", "core", "tensor")
+    streams = ("dpo", "core")
     return jax.shard_map(
         body,
-        mesh=mesh,
+        mesh=split_mesh,
         in_specs=(
-            P(("dp", "tensor"), None),
-            P(("dp", "tensor"), None),
+            P(rows, None),
+            P(rows, None),
             P(),
-            P("dp", "tensor"),
-            P("dp", "tensor"),
-            P("dp", "tensor"),
+            P(streams, "tensor"),
+            P(streams, "tensor"),
+            P(streams, "tensor"),
             P(),
             P(None, None, "tensor"),
             P("tensor", None),
-            P("dp"),
-            P("dp"),
-            P("dp"),
+            P(streams),
+            P(streams),
+            P(streams),
         ),
-        out_specs=(P(("dp", "tensor"), None), P(None, "dp", None, "tensor")),
+        out_specs=(P(rows, None), P(None, streams, None, "tensor")),
         check_vma=False,
     )

time: 388 us -> 493 us (1.27); the launches traced: 387 us -> 484 us
  waiting for transfers between devices: 199 us -> 242 us
  matrix products: 76 us -> 110 us
  other arithmetic: 15.7 us -> 32 us
  local copies, waits for them, and re-layouts: 52 us -> 58.7 us
    all_gather x2 -> x1, waiting for transfers between devices: 16 us -> 109 us  [gather_weights(): mine = lax.all_gather(weight_shard, 'dpo', axis=0, tiled=False)]
    ppermute x6 -> x9, waiting for transfers between devices: 123 us -> 74.2 us  [the longest x1 35.8 us: gather_rows(): from_pair = lax.ppermute(local, 'tensor', to_pair)]
    dot_general x2 -> x6, matrix products: 35.1 us -> 68.9 us  [the longest x3 36 us: body(): jnp.dot(rows_in[:, :split], mine.reshape(split, 3 * head_cols), preferred...]
    concatenate x1 -> x6, other arithmetic: 1.02 us -> 16.6 us  [the longest x1 8.74 us: gather_rows(): jnp.concatenate([local, from_prev, from_next, from_pair], 0)]
    gather x0 -> x2, local copies, waits for them, and re-layouts: none -> 11 us  [the longest x1 6.49 us: body(): attended = jnp.take(jnp.concatenate(attended_parts, 0), arrival, axis=0)]
    unnamed x45 -> x28, local copies, waits for them, and re-layouts: 18.5 us -> 8.65 us
    ppermute x6 -> x9, starting transfers between devices: 14.6 us -> 12.4 us  [the longest x1 3.41 us: gather_rows(): next_next = lax.ppermute(from_next, 'tensor', to_prev)]
  transfers between devices with their start and end apart: 11 -> 13, of which waited for: 7 -> 6; matrix products, arithmetic and copies ran while one was open for 18% -> 22% of each run, Pallas kernels for 0% -> 0%
where the time goes in v6:
time: 493 us; the launch traced here: 484 us
  waiting for transfers between devices  242 us (49%)
  matrix products  110 us (22%)
  local copies, waits for them, and re-layouts  58.7 us (12%)
  other arithmetic  32 us (6%)
  starting transfers between devices  25.9 us (5%)
  between operations  15.4 us (3%)
    all_gather x1, waiting for transfers between devices, gather_weights(): mine = lax.all_gather(weight_shard, 'dpo', axis=0, tiled=False)  109 us
    dot_general x3, matrix products, body(): jnp.dot(rows_in[:, :split], mine.reshape(split, 3 * head_cols), preferred...  36 us
    ppermute x1, waiting for transfers between devices, gather_rows(): from_pair = lax.ppermute(local, 'tensor', to_pair)  35.8 us
    dot_general x3, matrix products, body(): jnp.dot(rows_in[:, split:2 * split], other.reshape(split, 3 * head_cols),...  32.9 us
    reduce_scatter x1, waiting for transfers between devices, body(): lax.psum_scatter(jnp.dot(attended, output_projection_weight, preferred_el...  31.4 us
    all_to_all x1, waiting for transfers between devices, body(): lax.all_to_all(taken, ('dpo', 'core'), split_axis=0, concat_axis=0, tiled...  28.1 us
    ppermute x1, waiting for transfers between devices, gather_rows(): pair_prev = lax.ppermute(from_pair, 'tensor', to_next)  24.8 us
    ppermute x1, waiting for transfers between devices, gather_rows(): lax.ppermute(pair_prev[:, cut:], 'tensor', to_next)  13.6 us
  transfers between devices with their start and end apart: 13, of which 6 were waited for; matrix products, arithmetic and copies ran while one was open for 22% of the time, Pallas kernels for 0%

profile of v6, /device:TPU:1, one launch (start us, length us, event | category | flops | bytes accessed | tf_op | source)
XLA Modules:
  0.0 484.4 jit_solution(4154289597873180537)
XLA Ops:
  7.2 3.7 concatenate.78
  11.3 2.2 copy.26
  13.6 2.2 copy.27
  15.8 1.9 fusion.5
  17.7 4.3 fusion.45
  22.2 3.2 multiply_convert_fusion
  25.4 3.6 gather_fusion
  29.1 108.5 %all-gather.3.cloned.1.call-done = bf16[3584,1344]{1,0:T(8,128)(2,1)} async-done(((bf16[448,1344]{1,0:T(8,128)(2,1)}), bf16[3584,1344]{1,0:T(8,128)(2,1)}) %all-gather.3.cloned.1.call-update) | async-done | bytes 9633808 | tf_op jit(solution)/shard_map/all_gather | solution.py:46
  137.6 1.4 collective-permute-start.3
  139.0 5.2 %bitcast_select_fusion = bf16[128,7168]{0,1:T(8,128)(2,1)S(1)} fusion(bf16[16,128,448]{1,2,0:T(8,128)(2,1)} %gather_fusion, pred[7168]{0:T(1024)(128)(4,1)S(1)} %broadcast_in_dim.106), kind=kLoop, calls=%fused_computation.60 | loop fusion | flops 917504 | bytes 3677184 | tf_op jit(solution)/shard_map/jit(_take)/select_n | solution.py:117
  144.1 1.2 copy-done.2
  145.4 1.4 pad_maximum_fusion.2
  147.1 2.7 collective-permute-start.1
  150.6 4.3 scatter_custom_fusion
  154.9 35.8 %collective-permute-done.2 = bf16[128,7552]{0,1:T(8,128)(2,1)} collective-permute-done((bf16[128,7552]{0,1:T(8,128)(2,1)}, bf16[128,7552]{0,1:T(8,128)(2,1)}, u32[]{:S(2)}, u32[]{:S(2)}) %collective-permute-start.2) | collective-permute-done | bytes 1933344 | tf_op jit(solution)/shard_map/ppermute | solution.py:65
  190.7 1.3 collective-permute-start.6
  192.0 0.4 collective-permute-start.4
  192.5 4.5 gather_fusion.1
  197.1 1.9 and_and_fusion.1
  199.0 3.4 collective-permute-start.5
  202.4 8.7 %pad_maximum_fusion = bf16[512,7552]{0,1:T(8,128)(2,1)} fusion(bf16[128,7552]{0,1:T(8,128)(2,1)} %collective-permute-done.2, bf16[128,7552]{0,1:T(8,128)(2,1)} %collective-permute-done.1, bf16[128,7552]{0,1:T(8,128)(2,1)} %collective-permute-done, bf16[128,384]{0,1:T(8,128)(2,1)S(1)} %copy.28, bf16[128,7168]{0,1:T(8,128)(2,1)} %copy-done.2), kind=kLoop, calls=%fused_computation.7 | loop fusion | flops 38666240 | bytes 15466496 | tf_op jit(solution)/shard_map/concatenate | solution.py:87
  211.1 24.8 %collective-permute-done.6 = bf16[128,7552]{0,1:T(8,128)(2,1)} collective-permute-done((bf16[128,7552]{0,1:T(8,128)(2,1)}, bf16[128,7552]{0,1:T(8,128)(2,1)}, u32[]{:S(2)}, u32[]{:S(2)}) %collective-permute-start.6) | collective-permute-done | bytes 1933344 | tf_op jit(solution)/shard_map/ppermute | solution.py:68
  235.9 1.3 slice.124
  237.3 2.2 slice.122
  239.5 2.9 collective-permute-start.7
  242.4 1.9 constant_dynamic-update-slice_fusion.2
  244.3 0.5 constant_dynamic-update-slice_fusion.1
  244.8 2.1 constant_dynamic-update-slice_fusion
  246.9 13.6 %collective-permute-done.8 = bf16[128,3840]{0,1:T(8,128)(2,1)S(1)} collective-permute-done((bf16[128,3840]{0,1:T(8,128)(2,1)S(1)}, bf16[128,3840]{0,1:T(8,128)(2,1)S(1)}, u32[]{:S(2)}, u32[]{:S(2)}) %collective-permute-start.8) | collective-permute-done | bytes 983072 | tf_op jit(solution)/shard_map/ppermute | solution.py:73
  260.5 1.1 fusion.54
  261.6 13.7 %fusion.8 = f32[512,1344]{0,1:T(8,128)} fusion(bf16[3584,1344]{1,0:T(8,128)(2,1)} %bitcast.20, bf16[512,7552]{0,1:T(8,128)(2,1)} %pad_maximum_fusion), kind=kOutput, calls=%fused_computation.24 | convolution fusion | flops 4932501504 | bytes 16515072 | tf_op jit(solution)/shard_map/dot_general | solution.py:134
  275.3 11.3 %fusion.17 = f32[384,1344]{0,1:T(8,128)} fusion(bf16[3584,1344]{1,0:T(8,128)(2,1)} %bitcast.20, bf16[384,7552]{0,1:T(8,128)(2,1)} %copy-done.5), kind=kOutput, calls=%fused_computation.33 | convolution fusion | flops 3699376128 | bytes 14909440 | tf_op jit(solution)/shard_map/dot_general | solution.py:134
  286.6 7.9 %fusion.50 = f32[128,1344]{0,1:T(8,128)S(1)} fusion(bf16[3584,1344]{1,0:T(8,128)(2,1)} %bitcast.20, bf16[128,3840]{0,1:T(8,128)(2,1)S(1)} %collective-permute-done.8, bf16[128,3712]{0,1:T(8,128)(2,1)S(1)} %collective-permute-done.7), kind=kOutput, calls=%fused_computation.73 | convolution fusion | flops 1234960384 | bytes 12255232 | tf_op jit(solution)/shard_map/dot_general | solution.py:134
  294.5 15.6 %convolution_add_fusion.1 = f32[128,1344]{0,1:T(8,128)} fusion(f32[128,1344]{0,1:T(8,128)S(1)} %fusion.50, bf16[3584,1344]{1,0:T(8,128)(2,1)S(1)} %bitcast.89, bf16[128,3712]{0,1:T(8,128)(2,1)S(1)} %collective-permute-done.7), kind=kOutput, calls=%fused_computation.36 | convolution fusion | flops 1233297408 | bytes 12386304 | tf_op jit(solution)/shard_map/dot_general | solution.py:131
  310.1 11.2 %fusion.12 = f32[512,1344]{0,1:T(8,128)} fusion(f32[512,1344]{0,1:T(8,128)} %fusion.8, bf16[3584,1344]{1,0:T(8,128)(2,1)S(1)} %bitcast.89, bf16[512,7552]{0,1:T(8,128)(2,1)} %pad_maximum_fusion), kind=kOutput, calls=%fused_computation.29 | convolution fusion | flops 4933189632 | bytes 18808832 | tf_op jit(solution)/shard_map/dot_general | solution.py:131
  321.4 9.2 %convolution_add_fusion = f32[384,1344]{0,1:T(8,128)} fusion(f32[384,1344]{0,1:T(8,128)} %fusion.17, bf16[3584,1344]{1,0:T(8,128)(2,1)S(1)} %bitcast.89, bf16[384,7552]{0,1:T(8,128)(2,1)} %copy-done.5), kind=kOutput, calls=%fused_computation.32 | convolution fusion | flops 3699892224 | bytes 16515072 | tf_op jit(solution)/shard_map/dot_general | solution.py:131
  330.6 3.0 pad_maximum_fusion.1
  333.6 1.3 fusion.33
  334.9 1.4 fusion.35
  336.3 0.4 fusion.34
  336.7 1.0 fusion.86
  337.7 5.2 %fusion.88 = (f32[2,512]{1,0:T(2,128)S(1)}, f32[2,512,1024]{2,1,0:T(8,128)}) fusion(pred[512,1024]{1,0:T(8,128)(4,1)} %get-tuple-element.5, bf16[512,2,224]{0,2,1:T(8,128)(2,1)} %bitcast.100, bf16[1024,2,224]{0,2,1:T(8,128)(2,1)} %bitcast.90), kind=kOutput, calls=%fused_computation.145 | convolution fusion | flops 473957376 | bytes 6098944 | tf_op jit(solution)/shard_map/sub | solution.py:38
  342.9 4.2 fusion.42
  347.1 2.0 copy.30
  349.1 5.2 %fusion.89 = (f32[2,512]{1,0:T(2,128)S(1)}, f32[2,512,1024]{2,1,0:T(8,128)}) fusion(pred[512,1024]{1,0:T(8,128)(4,1)} %get-tuple-element.4, bf16[512,2,224]{0,2,1:T(8,128)(2,1)} %bitcast.99, bf16[1024,2,224]{0,2,1:T(8,128)(2,1)} %bitcast.91), kind=kOutput, calls=%fused_computation.146 | convolution fusion | flops 473957376 | bytes 6098944 | tf_op jit(solution)/shard_map/sub | solution.py:38
  354.3 4.4 fusion.44
  358.6 2.0 copy.29
  360.6 2.3 pad_maximum_fusion.6
  362.9 6.5 %gather_fusion.2 = bf16[1024,448]{1,0:T(8,128)(2,1)} fusion(bf16[1024,448]{1,0:T(8,128)(2,1)} %pad_maximum_fusion.6, s32[1024]{0:T(1024)S(1)} %get-tuple-element.22), kind=kCustom, calls=%fused_computation.2 | custom fusion | bytes 1839104 | tf_op jit(solution)/shard_map/jit(_take)/gather | solution.py:204
  369.4 7.4 %convolution_convert_fusion.1 = bf16[1024,3584]{1,0:T(8,128)(2,1)} fusion(bf16[448,3584]{1,0:T(8,128)(2,1)S(1)} %copy-done, bf16[1024,448]{1,0:T(8,128)(2,1)} %gather_fusion.2, pred[1024]{0:T(1024)(128)(4,1)S(1)} %compare_and_fusion), kind=kOutput, calls=%fused_computation.8 | convolution fusion | flops 3292463104 | bytes 11469824 | tf_op jit(solution)/shard_map/dot_general | solution.py:206
  376.8 0.6 copy-done.8
  377.4 0.6 broadcast_in_dim.117
  378.0 6.2 %all-to-all-start = ((s32[16,1,4]{2,1,0:T(1,128)}), s32[16,1,4]{2,1,0:T(1,128)S(1)}, u32[]{:S(2)}, u32[]{:S(2)}) async-start(s32[16,1,4]{2,1,0:T(1,128)} %broadcast_in_dim.117), calls=%async_computation.1 | async-start | bytes 16384 | tf_op jit(solution)/shard_map/all_to_all | solution.py:185
  385.0 1.6 pad_maximum_fusion.4
  386.7 3.9 fusion.38
  390.5 4.4 reshape.547
  394.9 7.2 %all-to-all-start.1 = ((bf16[16,4,14336]{2,1,0:T(4,128)(2,1)}), bf16[16,4,14336]{2,1,0:T(4,128)(2,1)}, u32[]{:S(2)}, u32[]{:S(2)}) async-start(bf16[16,4,14336]{2,1,0:T(4,128)(2,1)} %reshape.547), calls=%async_computation.2 | async-start | bytes 3670016 | tf_op jit(solution)/shard_map/all_to_all | solution.py:184
  402.1 0.5 broadcast.391
  402.6 0.7 reduce.3
  403.4 28.1 %all-to-all-done.1 = bf16[16,4,14336]{2,1,0:T(4,128)(2,1)} async-done(((bf16[16,4,14336]{2,1,0:T(4,128)(2,1)}), bf16[16,4,14336]{2,1,0:T(4,128)(2,1)}, u32[]{:S(2)}, u32[]{:S(2)}) %all-to-all-start.1) | async-done | bytes 1835040 | tf_op jit(solution)/shard_map/all_to_all | solution.py:184
  431.5 3.8 reshape.548
  435.4 3.6 convolution_convert_fusion
  438.9 6.8 %reshape.549 = bf16[64,16,2,448]{3,2,1,0:T(2,128)(2,1)} reshape(bf16[64,14336]{1,0:T(8,128)(2,1)} %convolution_convert_fusion) | data formatting | bytes 3670016 | tf_op jit(solution)/shard_map/reshape | solution.py:195
  445.7 31.4 %reduce-scatter.2.cloned.1.call-done = bf16[128,3584]{1,0:T(8,128)(2,1)} async-done(((bf16[1024,3584]{1,0:T(8,128)(2,1)}), bf16[128,3584]{1,0:T(8,128)(2,1)}) %reduce-scatter.2.cloned.1.call-update) | async-done | bytes 917520 | tf_op jit(solution)/shard_map/reduce_scatter | solution.py:205
  (71 shorter events, 2.3 us)
Async XLA Ops:
  7.2 362.3 %copy-start = (bf16[448,3584]{1,0:T(8,128)(2,1)S(1)}, bf16[448,3584]{1,0:T(8,128)(2,1)}, u32[]{:S(2)}) copy-start(bf16[448,3584]{1,0:T(8,128)(2,1)} %param.20) | copy-start | bytes 9633796
  7.2 4.1 copy-start.7
  7.2 130.4 %all-gather.3.cloned.1.call-start = ((), (), s32[]{:S(2)}) async-start(), calls=%async_computation.4 | async-start | bytes 11354112 | tf_op jit(solution)/shard_map/all_gather | solution.py:46
  10.9 466.2 %reduce-scatter.2.cloned.1.call-start = ((), (), s32[]{:S(2)}) async-start(), calls=%async_computation.3 | async-start | bytes 8257536 | tf_op jit(solution)/shard_map/reduce_scatter | solution.py:205
  137.6 54.9 %copy-start.1 = (s32[1024]{0:T(1024)S(1)}, s32[1024]{0:T(1024)}, u32[]{:S(2)}) copy-start(s32[1024]{0:T(1024)} %param.21) | copy-start | bytes 12292
  137.6 124.0 %collective-permute-start.3 = (bf16[8,448,1344]{2,1,0:T(8,128)(2,1)}, bf16[8,448,1344]{2,1,0:T(8,128)(2,1)}, u32[]{:S(2)}, u32[]{:S(2)}) collective-permute-start(bf16[8,448,1344]{2,1,0:T(8,128)(2,1)} %bitcast.87), channel_id=1, source_target_pairs={{0,8},{8,0},{1,9},{9,1},{2,10},{10,2},{3,11},{11,3},{4,12},{12,4},... | collective-permute-start | bytes 28901384 | tf_op jit(solution)/shard_map/ppermute | solution.py:47
  144.1 1.2 copy-start.2
  146.7 44.0 %collective-permute-start.2 = (bf16[128,7552]{0,1:T(8,128)(2,1)}, bf16[128,7552]{0,1:T(8,128)(2,1)}, u32[]{:S(2)}, u32[]{:S(2)}) collective-permute-start(bf16[128,7552]{0,1:T(8,128)(2,1)} %pad_maximum_fusion.2), channel_id=1, source_target_pairs={{0,4},{1,5},{2,6},{3,7},{4,0},{5,1},{6,2},{7,3},{8,12},{9,13},{10,... | collective-permute-start | bytes 5799944 | tf_op jit(solution)/shard_map/ppermute | solution.py:65
  147.1 44.9 %collective-permute-start.1 = (bf16[128,7552]{0,1:T(8,128)(2,1)}, bf16[128,7552]{0,1:T(8,128)(2,1)}, u32[]{:S(2)}, u32[]{:S(2)}) collective-permute-start(bf16[128,7552]{0,1:T(8,128)(2,1)} %pad_maximum_fusion.2), channel_id=1, source_target_pairs={{0,3},{1,0},{2,1},{3,2},{4,7},{5,4},{6,5},{7,6},{8,11},{9,8},{10,9... | collective-permute-start | bytes 5799944 | tf_op jit(solution)/shard_map/ppermute | solution.py:64
  149.7 52.7 %collective-permute-start = (bf16[128,7552]{0,1:T(8,128)(2,1)}, bf16[128,7552]{0,1:T(8,128)(2,1)}, u32[]{:S(2)}, u32[]{:S(2)}) collective-permute-start(bf16[128,7552]{0,1:T(8,128)(2,1)} %pad_maximum_fusion.2), channel_id=1, source_target_pairs={{0,1},{1,2},{2,3},{3,0},{4,5},{5,6},{6,7},{7,4},{8,9},{9,10},{10,1... | collective-permute-start | bytes 5799944 | tf_op jit(solution)/shard_map/ppermute | solution.py:63
  190.7 45.2 %collective-permute-start.6 = (bf16[128,7552]{0,1:T(8,128)(2,1)}, bf16[128,7552]{0,1:T(8,128)(2,1)}, u32[]{:S(2)}, u32[]{:S(2)}) collective-permute-start(bf16[128,7552]{0,1:T(8,128)(2,1)} %collective-permute-done.2), channel_id=1, source_target_pairs={{0,1},{1,2},{2,3},{3,0},{4,5},{5,6},{6,7},{7,4},{8,9},{9,10},{10,1... | collective-permute-start | bytes 5799944 | tf_op jit(solution)/shard_map/ppermute | solution.py:68
  192.0 45.3 %collective-permute-start.4 = (bf16[128,7552]{0,1:T(8,128)(2,1)}, bf16[128,7552]{0,1:T(8,128)(2,1)}, u32[]{:S(2)}, u32[]{:S(2)}) collective-permute-start(bf16[128,7552]{0,1:T(8,128)(2,1)} %collective-permute-done.1), channel_id=1, source_target_pairs={{0,4},{1,5},{2,6},{3,7},{4,0},{5,1},{6,2},{7,3},{8,12},{9,13},{10,... | collective-permute-start | bytes 5799944 | tf_op jit(solution)/shard_map/ppermute | solution.py:66
  199.0 45.3 %collective-permute-start.5 = (bf16[128,7552]{0,1:T(8,128)(2,1)}, bf16[128,7552]{0,1:T(8,128)(2,1)S(1)}, u32[]{:S(2)}, u32[]{:S(2)}) collective-permute-start(bf16[128,7552]{0,1:T(8,128)(2,1)} %collective-permute-done.1), channel_id=1, source_target_pairs={{0,3},{1,0},{2,1},{3,2},{4,7},{5,4},{6,5},{7,6},{8,11},{9,8},{10,9... | collective-permute-start | bytes 5799944 | tf_op jit(solution)/shard_map/ppermute | solution.py:67
  237.2 23.3 %collective-permute-start.8 = (bf16[128,3840]{0,1:T(8,128)(2,1)S(1)}, bf16[128,3840]{0,1:T(8,128)(2,1)S(1)}, u32[]{:S(2)}, u32[]{:S(2)}) collective-permute-start(bf16[128,3840]{0,1:T(8,128)(2,1)S(1)} %slice.124), channel_id=1, source_target_pairs={{0,1},{1,2},{2,3},{3,0},{4,5},{5,6},{6,7},{7,4},{8,9},{9,10},{10,1... | collective-permute-start | bytes 2949128 | tf_op jit(solution)/shard_map/ppermute | solution.py:73
  239.5 47.1 %collective-permute-start.7 = (bf16[128,3712]{0,1:T(8,128)(2,1)}, bf16[128,3712]{0,1:T(8,128)(2,1)S(1)}, u32[]{:S(2)}, u32[]{:S(2)}) collective-permute-start(bf16[128,3712]{0,1:T(8,128)(2,1)} %slice.122), channel_id=1, source_target_pairs={{0,3},{1,0},{2,1},{3,2},{4,7},{5,4},{6,5},{7,6},{8,11},{9,8},{10,9... | collective-permute-start | bytes 2850824 | tf_op jit(solution)/shard_map/ppermute | solution.py:72
  244.3 16.2 %copy-start.3 = (bf16[128,7168]{0,1:T(8,128)(2,1)S(1)}, bf16[128,7168]{0,1:T(8,128)(2,1)}, u32[]{:S(2)}) copy-start(bf16[128,7168]{0,1:T(8,128)(2,1)} %copy-done.2) | copy-start | bytes 5505028
  246.8 14.8 %copy-start.5 = (bf16[384,7552]{0,1:T(8,128)(2,1)}, bf16[384,7552]{0,1:T(8,128)(2,1)S(1)}, u32[]{:S(2)}) copy-start(bf16[384,7552]{0,1:T(8,128)(2,1)S(1)} %constant_dynamic-update-slice_fusion) | copy-start | bytes 17399812
  261.6 32.9 %slice-start = ((s8[10092544]{0:T(1024)(128)(4,1)}), s8[4194304]{0:T(1024)(128)(4,1)S(1)}, s32[]{:S(2)}) async-start(s8[10092544]{0:T(1024)(128)(4,1)} %bitcast.88), calls=%async_computation.5 | async-start | bytes 8388608
  261.6 32.9 %slice-start.1 = ((s8[10092544]{0:T(1024)(128)(4,1)}), s8[4194304]{0:T(1024)(128)(4,1)S(1)}, s32[]{:S(2)}) async-start(s8[10092544]{0:T(1024)(128)(4,1)} %bitcast.88), calls=%async_computation.6 | async-start | bytes 8388608
  275.3 19.2 %slice-start.2 = ((s8[10092544]{0:T(1024)(128)(4,1)}), s8[1703936]{0:T(1024)(128)(4,1)S(1)}, s32[]{:S(2)}) async-start(s8[10092544]{0:T(1024)(128)(4,1)} %bitcast.88), calls=%async_computation.7 | async-start | bytes 3407872
  321.4 9.2 %copy-start.4 = (f32[128,1344]{0,1:T(8,128)S(1)}, f32[128,1344]{0,1:T(8,128)}, u32[]{:S(2)}) copy-start(f32[128,1344]{0,1:T(8,128)} %convolution_add_fusion.1) | copy-start | bytes 2064388
  330.6 3.0 copy-start.6
  376.8 0.7 copy-start.8
  378.0 16.9 %all-to-all-start = ((s32[16,1,4]{2,1,0:T(1,128)}), s32[16,1,4]{2,1,0:T(1,128)S(1)}, u32[]{:S(2)}, u32[]{:S(2)}) async-start(s32[16,1,4]{2,1,0:T(1,128)} %broadcast_in_dim.117), calls=%async_computation.1 | async-start | bytes 16384 | tf_op jit(solution)/shard_map/all_to_all | solution.py:185
  394.9 36.6 %all-to-all-start.1 = ((bf16[16,4,14336]{2,1,0:T(4,128)(2,1)}), bf16[16,4,14336]{2,1,0:T(4,128)(2,1)}, u32[]{:S(2)}, u32[]{:S(2)}) async-start(bf16[16,4,14336]{2,1,0:T(4,128)(2,1)} %reshape.547), calls=%async_computation.2 | async-start | bytes 3670016 | tf_op jit(solution)/shard_map/all_to_all | solution.py:184
Sparse Core Ops, SparseCore 0:
  11.0 126.4 all-gather.2
  376.9 100.1 reduce-scatter.1

commit v7 on v4

--- a/solution.py
+++ b/solution.py
@@ -19,19 +19,20 @@
     return (combined * factor * input_norm_gain).astype(jnp.bfloat16)
 
 
-def attend_block(query, keys, values, segment, position, live, first, count, key_end):
+def attend_block(query, keys, values, segment, position, live, first, count, key_start, key_end):
     heads = query.shape[1] // HD
+    span = key_end - key_start
     block_query = query[first : first + count].reshape(count, heads, HD)
-    block_keys = keys.reshape(key_end, heads, HD)
-    block_values = values.reshape(key_end, heads, HD)
+    block_keys = keys[key_start:key_end].reshape(span, heads, HD)
+    block_values = values[key_start:key_end].reshape(span, heads, HD)
     scores = jnp.einsum(
         "qhd,khd->hqk", block_query, block_keys, preferred_element_type=jnp.float32
     ) / math.sqrt(HD)
     query_at = position[first : first + count]
     allowed = (
-        (segment[first : first + count, None] == segment[None, :key_end])
-        & (position[None, :] <= query_at[:, None])
-        & (position[None, :] < live)
+        (segment[first : first + count, None] == segment[None, key_start:key_end])
+        & (position[None, key_start:key_end] <= query_at[:, None])
+        & (position[None, key_start:key_end] < live)
     )
     scores = jnp.where(allowed[None], scores, negative)
     top = jnp.max(scores, axis=-1, keepdims=True)
@@ -178,10 +179,14 @@
     kv_cache = cache_rows.astype(jnp.bfloat16).reshape(total_reqs, piece_len, 2, head_cols)
     block = min(512, stream)
     attended_parts = []
+    longest_request = stream // request_cache_row.shape[0]
     for block_index in range(stream // block):
         first = block_index * block
+        key_start = max(0, first - longest_request)
         attended_parts.append(
-            attend_block(query, keys, values, segment, position, live, first, block, stream)
+            attend_block(
+                query, keys, values, segment, position, live, first, block, key_start, first + block
+            )
         )
     attended = jnp.concatenate(attended_parts, 0)
     block_out = lax.psum_scatter(

time: 388 us -> 385 us (level)
  matrix products: 76 us -> 70 us
    unnamed x45 -> x47, local copies, waits for them, and re-layouts: 18.5 us -> 16.8 us
where the time goes in v7:
time: 385 us; the launch traced here: 384 us
  waiting for transfers between devices  200 us (52%)
  matrix products  70 us (18%)
  local copies, waits for them, and re-layouts  53.6 us (14%)
  starting transfers between devices  29.2 us (8%)
  other arithmetic  16.2 us (4%)
  between operations  14.7 us (4%)
    ppermute x1, waiting for transfers between devices, gather_weights(): from_prev = lax.ppermute(pair, 'dp', to_next)  48.9 us
    ppermute x1, waiting for transfers between devices, gather_weights(): pair = jnp.stack([weight_shard, lax.ppermute(weight_shard, 'dp', to_yh)])  48.6 us
    reduce_scatter x1, waiting for transfers between devices, body(): lax.psum_scatter(jnp.dot(attended, output_projection_weight, preferred_el...  31.7 us
    all_to_all x1, waiting for transfers between devices, body(): lax.all_to_all(taken, 'dp', split_axis=0, concat_axis=0, tiled=True)  28.1 us
    dot_general x1, matrix products, body(): jnp.dot(low_part, mine.reshape(split, 3 * head_cols), preferred_element_t...  17.9 us
    dot_general x1, matrix products, body(): jnp.dot(high_part[:, :split], other.reshape(split, 3 * head_cols), prefer...  17.2 us
    unnamed x47, local copies, waits for them, and re-layouts  16.8 us
    all_gather x1, waiting for transfers between devices, body(): lax.all_gather(in_order[:, :split], 'tensor', axis=0, tiled=True)  16.7 us
  transfers between devices with their start and end apart: 11, of which 7 were waited for; matrix products, arithmetic and copies ran while one was open for 18% of the time, Pallas kernels for 0%

profile of v7, /device:TPU:1, one launch (start us, length us, event | category | flops | bytes accessed | tf_op | source)
XLA Modules:
  0.0 383.7 jit_solution(6556377599574601337)
XLA Ops:
  7.3 2.4 copy.27
  9.6 1.9 fusion.7
  11.5 2.2 copy.26
  13.9 4.4 %fusion.31 = bf16[128,384]{1,0:T(8,128)(2,1)S(1)} fusion(bf16[7168,384]{1,0:T(8,128)(2,1)} %param.21, f32[7168]{0:T(1024)S(1)} %copy-done.11, f32[128]{0:T(128)S(1)} %add_rsqrt_fusion, bf16[128,3584]{1,0:T(8,128)(2,1)} %param.16, bf16[128,3584]{1,0:T(8,128)(2,1)} %param.15), kind=kOutput, calls=%fused_computation.54 | convolution fusion | flops 711114752 | bytes 7467520 | tf_op jit(solution)/shard_map/dot_general | solution.py:108
  18.4 2.5 multiply_convert_fusion
  20.8 3.5 gather_fusion
  24.4 3.9 %copy.28 = bf16[128,7168]{1,0:T(8,128)(2,1)} copy(bf16[128,7168]{0,1:T(8,128)(2,1)} %bitcast.69) | data formatting | bytes 3670016 | tf_op jit(solution)/shard_map/jit(_take)/gather | solution.py:104
  28.4 1.7 broadcast_select_fusion
  30.1 1.0 fusion.65
  31.2 1.0 pad_maximum_fusion.4
  32.3 3.5 concatenate.27
  35.8 3.7 collective-permute-start
  39.5 48.6 %collective-permute-done = bf16[448,1344]{1,0:T(8,128)(2,1)S(1)} collective-permute-done((bf16[448,1344]{1,0:T(8,128)(2,1)}, bf16[448,1344]{1,0:T(8,128)(2,1)S(1)}, u32[]{:S(2)}, u32[]{:S(2)}) %collective-permute-start) | collective-permute-done | bytes 1204256 | tf_op jit(solution)/shard_map/ppermute | solution.py:64
  88.1 3.5 pad_maximum_fusion
  91.6 1.1 collective-permute-start.1
  92.7 1.6 collective-permute-start.2
  94.4 2.4 constant_dynamic-update-slice_fusion.3
  96.8 48.9 %collective-permute-done.1 = bf16[2,448,1344]{2,1,0:T(8,128)(2,1)} collective-permute-done((bf16[2,448,1344]{2,1,0:T(8,128)(2,1)}, bf16[2,448,1344]{2,1,0:T(8,128)(2,1)}, u32[]{:S(2)}, u32[]{:S(2)}) %collective-permute-start.1) | collective-permute-done | bytes 2408480 | tf_op jit(solution)/shard_map/ppermute | solution.py:65
  145.7 1.4 slice_bitcast_fusion.1
  147.2 1.4 slice_bitcast_fusion
  148.6 2.7 collective-permute-start.4
  151.3 1.2 constant_dynamic-update-slice_fusion.2
  152.5 3.3 constant_dynamic-update-slice_fusion.1
  155.8 3.4 constant_dynamic-update-slice_fusion
  159.2 13.9 %collective-permute-done.3 = bf16[448,1344]{1,0:T(8,128)(2,1)S(1)} collective-permute-done((bf16[448,1344]{1,0:T(8,128)(2,1)S(1)}, bf16[448,1344]{1,0:T(8,128)(2,1)S(1)}, u32[]{:S(2)}, u32[]{:S(2)}) %collective-permute-start.3) | collective-permute-done | bytes 1204256 | tf_op jit(solution)/shard_map/ppermute | solution.py:68
  173.1 1.2 bitcast_dynamic-update-slice_fusion.1
  174.3 1.2 bitcast_dynamic-update-slice_fusion
  175.5 5.4 %collective-permute-start.5 = (bf16[8,448,1344]{2,1,0:T(8,128)(2,1)}, bf16[8,448,1344]{2,1,0:T(8,128)(2,1)}, u32[]{:S(2)}, u32[]{:S(2)}) collective-permute-start(bf16[8,448,1344]{2,1,0:T(8,128)(2,1)} %bitcast_dynamic-update-slice_fusion), channel_id=1, source_target_pairs={{0,8},{8,0},{16,24},{24,16},{32,40},{40,32},{48,56},{56,48},{64,72... | collective-permute-start | bytes 28901384 | tf_op jit(solution)/shard_map/ppermute | solution.py:71
  181.6 0.5 broadcast_compare_fusion.2
  182.2 1.0 and_and_fusion.1
  183.2 1.2 and_and_fusion
  184.3 12.1 %collective-permute-done.5 = bf16[8,448,1344]{2,1,0:T(8,128)(2,1)} collective-permute-done((bf16[8,448,1344]{2,1,0:T(8,128)(2,1)}, bf16[8,448,1344]{2,1,0:T(8,128)(2,1)}, u32[]{:S(2)}, u32[]{:S(2)}) %collective-permute-start.5) | collective-permute-done | bytes 9633824 | tf_op jit(solution)/shard_map/ppermute | solution.py:71
  196.4 17.2 %fusion.2 = f32[1024,1344]{0,1:T(8,128)} fusion(bf16[3584,1344]{1,0:T(8,128)(2,1)} %bitcast.12, bf16[1024,3968]{1,0:T(8,128)(2,1)} %all-gather.5.cloned.1.call-done), kind=kOutput, calls=%fused_computation.5 | convolution fusion | flops 9865003008 | bytes 22937600 | tf_op jit(solution)/shard_map/dot_general | solution.py:124
  213.6 16.7 %all-gather.3.cloned.1.call-done = bf16[1024,3584]{1,0:T(8,128)(2,1)} async-done(((bf16[128,3584]{1,0:T(8,128)(2,1)}), bf16[1024,3584]{1,0:T(8,128)(2,1)}) %all-gather.3.cloned.1.call-update) | async-done | bytes 7340048 | tf_op jit(solution)/shard_map/all_gather | solution.py:113
  230.3 17.9 %convolution_add_fusion = f32[1024,1344]{0,1:T(8,128)} fusion(f32[1024,1344]{0,1:T(8,128)} %fusion.2, bf16[1024,3584]{1,0:T(8,128)(2,1)} %all-gather.3.cloned.1.call-done, bf16[3584,1344]{1,0:T(8,128)(2,1)} %bitcast.11), kind=kOutput, calls=%fused_computation.9 | convolution fusion | flops 9866379264 | bytes 27983872 | tf_op jit(solution)/shard_map/dot_general | solution.py:115
  248.2 2.0 fusion.18
  250.2 0.8 slice.127
  251.0 2.0 fusion.16
  253.1 1.0 slice.136
  254.1 0.8 slice.133
  254.9 2.0 fusion.17
  256.9 1.0 fusion.66
  257.9 4.5 %fusion.68 = (f32[2,512]{1,0:T(2,128)S(1)}, f32[2,512,768]{2,1,0:T(8,128)}) fusion(pred[512,768]{1,0:T(8,128)(4,1)} %and_and_fusion, bf16[512,2,224]{0,2,1:T(8,128)(2,1)} %bitcast.76, bf16[768,2,224]{0,2,1:T(8,128)(2,1)} %bitcast.74), kind=kOutput, calls=%fused_computation.112 | convolution fusion | flops 355468032 | bytes 4689920 | tf_op jit(solution)/shard_map/sub | solution.py:39
  262.3 3.5 fusion.69
  265.8 2.3 fusion.28
  268.1 0.5 slice-done
  268.6 0.8 fusion.30
  269.4 6.1 %convolution_convert_fusion.1 = bf16[1024,3584]{1,0:T(8,128)(2,1)} fusion(bf16[448,3584]{1,0:T(8,128)(2,1)S(1)} %copy-done, bf16[512,448]{0,1:T(8,128)(2,1)S(1)} %bitcast.81, bf16[512,448]{0,1:T(8,128)(2,1)S(1)} %bitcast.80), kind=kOutput, calls=%fused_computation.4 | convolution fusion | flops 3293839360 | bytes 11468800 | tf_op jit(solution)/shard_map/dot_general | solution.py:193
  275.6 0.6 copy-done.14
  276.2 0.6 broadcast_in_dim.107
  276.8 7.3 %all-to-all-start = ((s32[16,1,4]{2,1,0:T(1,128)}), s32[16,1,4]{2,1,0:T(1,128)S(1)}, u32[]{:S(2)}, u32[]{:S(2)}) async-start(s32[16,1,4]{2,1,0:T(1,128)} %broadcast_in_dim.107), calls=%async_computation.1 | async-start | bytes 16384 | tf_op jit(solution)/shard_map/all_to_all | solution.py:169
  284.1 0.1 convert_reduce_fusion
  284.2 0.2 reduce-window.8
  284.8 1.6 pad_maximum_fusion.2
  286.4 3.8 fusion.21
  290.3 4.4 %reshape.332 = bf16[16,4,14336]{2,1,0:T(4,128)(2,1)} reshape(bf16[1024,896]{1,0:T(8,128)(2,1)} %fusion.21) | data formatting | bytes 3670016 | tf_op jit(solution)/shard_map/reshape | solution.py:165
  294.6 7.2 %all-to-all-start.1 = ((bf16[16,4,14336]{2,1,0:T(4,128)(2,1)}), bf16[16,4,14336]{2,1,0:T(4,128)(2,1)}, u32[]{:S(2)}, u32[]{:S(2)}) async-start(bf16[16,4,14336]{2,1,0:T(4,128)(2,1)} %reshape.332), calls=%async_computation.2 | async-start | bytes 3670016 | tf_op jit(solution)/shard_map/all_to_all | solution.py:168
  301.9 0.5 broadcast.205
  302.4 0.7 reduce.3
  303.1 28.1 %all-to-all-done.1 = bf16[16,4,14336]{2,1,0:T(4,128)(2,1)} async-done(((bf16[16,4,14336]{2,1,0:T(4,128)(2,1)}), bf16[16,4,14336]{2,1,0:T(4,128)(2,1)}, u32[]{:S(2)}, u32[]{:S(2)}) %all-to-all-start.1) | async-done | bytes 1835040 | tf_op jit(solution)/shard_map/all_to_all | solution.py:168
  331.3 3.9 %reshape.333 = bf16[64,14336]{1,0:T(8,128)(2,1)} reshape(bf16[16,4,14336]{2,1,0:T(4,128)(2,1)} %all-to-all-done.1) | data formatting | bytes 3670016 | tf_op jit(solution)/shard_map/reshape | solution.py:175
  335.1 3.6 convolution_convert_fusion
  338.7 6.8 %reshape.334 = bf16[64,16,2,448]{3,2,1,0:T(2,128)(2,1)} reshape(bf16[64,14336]{1,0:T(8,128)(2,1)} %convolution_convert_fusion) | data formatting | bytes 3670016 | tf_op jit(solution)/shard_map/reshape | solution.py:179
  345.5 31.7 %reduce-scatter.2.cloned.1.call-done = bf16[128,3584]{1,0:T(8,128)(2,1)} async-done(((bf16[1024,3584]{1,0:T(8,128)(2,1)}), bf16[128,3584]{1,0:T(8,128)(2,1)}) %reduce-scatter.2.cloned.1.call-update) | async-done | bytes 917520 | tf_op jit(solution)/shard_map/reduce_scatter | solution.py:192
  (75 shorter events, 1.2 us)
Async XLA Ops:
  7.2 262.2 %copy-start = (bf16[448,3584]{1,0:T(8,128)(2,1)S(1)}, bf16[448,3584]{1,0:T(8,128)(2,1)}, u32[]{:S(2)}) copy-start(bf16[448,3584]{1,0:T(8,128)(2,1)} %param.23) | copy-start | bytes 9633796
  7.2 6.7 %copy-start.15 = (s32[16]{0:T(128)S(1)}, s32[16]{0:T(128)}, u32[]{:S(2)}) copy-start(s32[16]{0:T(128)} %constant.102.clone) | copy-start | bytes 196
  7.2 6.6 %copy-start.16 = (s32[16]{0:T(128)S(1)}, s32[16]{0:T(128)}, u32[]{:S(2)}) copy-start(s32[16]{0:T(128)} %constant.101.clone) | copy-start | bytes 196
  7.2 6.6 %copy-start.17 = (s32[16]{0:T(128)S(1)}, s32[16]{0:T(128)}, u32[]{:S(2)}) copy-start(s32[16]{0:T(128)} %constant.100.clone) | copy-start | bytes 196
  7.2 6.5 %copy-start.11 = (f32[7168]{0:T(1024)S(1)}, f32[7168]{0:T(1024)}, u32[]{:S(2)}) copy-start(f32[7168]{0:T(1024)} %param.17) | copy-start | bytes 86020
  7.2 177.1 %all-gather.5.cloned.1.call-start = ((), (), s32[]{:S(2)}) async-start(), calls=%async_computation.4 | async-start | bytes 9142272 | tf_op jit(solution)/shard_map/all_gather | solution.py:119
  13.9 4.5 %copy-start.5 = (bf16[128,3584]{0,1:T(8,128)(2,1)S(1)}, bf16[128,3584]{0,1:T(8,128)(2,1)}, u32[]{:S(2)}) copy-start(bf16[128,3584]{0,1:T(8,128)(2,1)} %copy.27) | copy-start | bytes 2752516
  13.9 4.5 %copy-start.6 = (bf16[128,3584]{0,1:T(8,128)(2,1)S(1)}, bf16[128,3584]{0,1:T(8,128)(2,1)}, u32[]{:S(2)}) copy-start(bf16[128,3584]{0,1:T(8,128)(2,1)} %copy.26) | copy-start | bytes 2752516
  32.2 198.0 %all-gather.3.cloned.1.call-start = ((), (), s32[]{:S(2)}) async-start(), calls=%async_computation.3 | async-start | bytes 8257536 | tf_op jit(solution)/shard_map/all_gather | solution.py:113
  35.8 52.3 %collective-permute-start = (bf16[448,1344]{1,0:T(8,128)(2,1)}, bf16[448,1344]{1,0:T(8,128)(2,1)S(1)}, u32[]{:S(2)}, u32[]{:S(2)}) collective-permute-start(bf16[448,1344]{1,0:T(8,128)(2,1)} %concatenate.27), channel_id=1, source_target_pairs={{0,16},{8,24},{16,0},{24,8},{32,48},{40,56},{48,32},{56,40},{64,80... | collective-permute-start | bytes 3612680 | tf_op jit(solution)/shard_map/ppermute | solution.py:64
  88.1 3.5 copy-start.3
  91.6 54.1 %collective-permute-start.1 = (bf16[2,448,1344]{2,1,0:T(8,128)(2,1)}, bf16[2,448,1344]{2,1,0:T(8,128)(2,1)}, u32[]{:S(2)}, u32[]{:S(2)}) collective-permute-start(bf16[2,448,1344]{2,1,0:T(8,128)(2,1)} %pad_maximum_fusion), channel_id=1, source_target_pairs={{0,32},{8,40},{16,48},{24,56},{32,64},{40,72},{48,80},{56,88},{64,... | collective-permute-start | bytes 7225352 | tf_op jit(solution)/shard_map/ppermute | solution.py:65
  92.7 54.5 %collective-permute-start.2 = (bf16[2,448,1344]{2,1,0:T(8,128)(2,1)}, bf16[2,448,1344]{2,1,0:T(8,128)(2,1)}, u32[]{:S(2)}, u32[]{:S(2)}) collective-permute-start(bf16[2,448,1344]{2,1,0:T(8,128)(2,1)} %pad_maximum_fusion), channel_id=1, source_target_pairs={{0,96},{8,104},{16,112},{24,120},{32,0},{40,8},{48,16},{56,24},{64... | collective-permute-start | bytes 7225352 | tf_op jit(solution)/shard_map/ppermute | solution.py:66
  94.3 282.9 %reduce-scatter.2.cloned.1.call-start = ((), (), s32[]{:S(2)}) async-start(), calls=%async_computation.5 | async-start | bytes 8257536 | tf_op jit(solution)/shard_map/reduce_scatter | solution.py:192
  96.8 54.5 %copy-start.4 = (bf16[448,1344]{1,0:T(8,128)(2,1)S(1)}, bf16[448,1344]{1,0:T(8,128)(2,1)}, u32[]{:S(2)}) copy-start(bf16[448,1344]{1,0:T(8,128)(2,1)} %copy-done.3) | copy-start | bytes 3612676
  147.1 26.0 %collective-permute-start.3 = (bf16[448,1344]{1,0:T(8,128)(2,1)S(1)}, bf16[448,1344]{1,0:T(8,128)(2,1)S(1)}, u32[]{:S(2)}, u32[]{:S(2)}) collective-permute-start(bf16[448,1344]{1,0:T(8,128)(2,1)S(1)} %slice_bitcast_fusion.1), channel_id=1, source_target_pairs={{0,32},{8,40},{16,48},{24,56},{32,64},{40,72},{48,80},{56,88},{64,... | collective-permute-start | bytes 3612680 | tf_op jit(solution)/shard_map/ppermute | solution.py:68
  148.6 25.7 %collective-permute-start.4 = (bf16[448,1344]{1,0:T(8,128)(2,1)S(1)}, bf16[448,1344]{1,0:T(8,128)(2,1)S(1)}, u32[]{:S(2)}, u32[]{:S(2)}) collective-permute-start(bf16[448,1344]{1,0:T(8,128)(2,1)S(1)} %slice_bitcast_fusion), channel_id=1, source_target_pairs={{0,96},{8,104},{16,112},{24,120},{32,0},{40,8},{48,16},{56,24},{64... | collective-permute-start | bytes 3612680 | tf_op jit(solution)/shard_map/ppermute | solution.py:68
  159.2 21.6 %copy-start.9 = (s32[1024]{0:T(1024)S(1)}, s32[1024]{0:T(1024)}, u32[]{:S(2)}) copy-start(s32[1024]{0:T(1024)} %param.24) | copy-start | bytes 12292
  175.5 21.0 %collective-permute-start.5 = (bf16[8,448,1344]{2,1,0:T(8,128)(2,1)}, bf16[8,448,1344]{2,1,0:T(8,128)(2,1)}, u32[]{:S(2)}, u32[]{:S(2)}) collective-permute-start(bf16[8,448,1344]{2,1,0:T(8,128)(2,1)} %bitcast_dynamic-update-slice_fusion), channel_id=1, source_target_pairs={{0,8},{8,0},{16,24},{24,16},{32,40},{40,32},{48,56},{56,48},{64,72... | collective-permute-start | bytes 28901384 | tf_op jit(solution)/shard_map/ppermute | solution.py:71
  182.1 1.0 copy-start.12
  230.3 17.9 %copy-start.7 = (bf16[3,128,448]{1,2,0:T(8,128)(2,1)S(1)}, bf16[3,128,448]{1,2,0:T(8,128)(2,1)}, u32[]{:S(2)}) copy-start(bf16[3,128,448]{1,2,0:T(8,128)(2,1)} %param.22) | copy-start | bytes 1032196
  250.2 2.9 copy-start.1
  253.1 3.8 copy-start.2
  257.9 4.5 %copy-start.8 = (pred[512,512]{0,1:T(8,128)(4,1)S(1)}, pred[512,512]{0,1:T(8,128)(4,1)}, u32[]{:S(2)}) copy-start(pred[512,512]{0,1:T(8,128)(4,1)} %and_and_fusion.1) | copy-start | bytes 786436
  262.3 3.5 copy-start.13
  265.8 2.8 slice-start
  265.8 2.8 copy-start.18
  265.8 2.8 copy-start.19
  275.5 0.7 copy-start.14
  275.5 8.5 %copy-start.10 = (s32[1024]{0:T(1024)S(1)}, s32[1024]{0:T(1024)}, u32[]{:S(2)}) copy-start(s32[1024]{0:T(1024)} %param.24) | copy-start | bytes 12292
  276.8 17.9 %all-to-all-start = ((s32[16,1,4]{2,1,0:T(1,128)}), s32[16,1,4]{2,1,0:T(1,128)S(1)}, u32[]{:S(2)}, u32[]{:S(2)}) async-start(s32[16,1,4]{2,1,0:T(1,128)} %broadcast_in_dim.107), calls=%async_computation.1 | async-start | bytes 16384 | tf_op jit(solution)/shard_map/all_to_all | solution.py:169
  294.6 36.6 %all-to-all-start.1 = ((bf16[16,4,14336]{2,1,0:T(4,128)(2,1)}), bf16[16,4,14336]{2,1,0:T(4,128)(2,1)}, u32[]{:S(2)}, u32[]{:S(2)}) async-start(bf16[16,4,14336]{2,1,0:T(4,128)(2,1)} %reshape.332), calls=%async_computation.2 | async-start | bytes 3670016 | tf_op jit(solution)/shard_map/all_to_all | solution.py:168
Sparse Core Ops, SparseCore 0:
  32.3 116.1 all-gather.4
  150.7 79.4 all-gather.2
  275.7 101.4 reduce-scatter.1

commit v8 on v7

--- a/solution.py
+++ b/solution.py
@@ -115,16 +115,22 @@
     folded_all = jnp.dot(
         low_part, mine.reshape(split, 3 * head_cols), preferred_element_type=jnp.float32
     )
-    high_part = with_layout_constraint(
-        lax.all_gather(
-            jnp.concatenate([in_order[:, split:], low_local], 1), "tensor", axis=0, tiled=True
-        ),
-        row_major,
-    )
-    folded_all = folded_all + jnp.dot(
-        high_part[:, :split], other.reshape(split, 3 * head_cols), preferred_element_type=jnp.float32
-    )
-    adapter_update = high_part[:, split:]
+    quarter = split // 2
+    blocks_half = other.shape[0] // 2
+    for q in range(2):
+        lo = split + q * quarter
+        piece = in_order[:, lo : lo + quarter]
+        if q == 1:
+            piece = jnp.concatenate([piece, low_local], 1)
+        high_part = with_layout_constraint(
+            lax.all_gather(piece, "tensor", axis=0, tiled=True), row_major
+        )
+        folded_all = folded_all + jnp.dot(
+            high_part[:, :quarter],
+            other[q * blocks_half : (q + 1) * blocks_half].reshape(quarter, 3 * head_cols),
+            preferred_element_type=jnp.float32,
+        )
+    adapter_update = high_part[:, quarter:]
     folded = [folded_all[:, k * head_cols : (k + 1) * head_cols] for k in range(3)]
     projected = []
     for adapter_selector in range(3):

time: 385 us -> 388 us (level)
  local copies, waits for them, and re-layouts: 53.6 us -> 64.5 us
  waiting for transfers between devices: 200 us -> 194 us
    all_gather x1 -> x2, waiting for transfers between devices: 0.01 us -> 23.6 us  [body(): lax.all_gather(piece, 'tensor', axis=0, tiled=True)]
    all_gather x1, waiting for transfers between devices: 16.7 us -> 0.01 us  [body(): lax.all_gather(in_order[:, :split], 'tensor', axis=0, tiled=True)]
    ppermute x1, waiting for transfers between devices: 12.1 us -> 0.01 us  [gather_weights(): other = lax.ppermute(mine, 'dp', to_core)]
    slice x0 -> x2, local copies, waits for them, and re-layouts: none -> 9.59 us  [the longest x1 8.59 us: body(): other[q * blocks_half:(q + 1) * blocks_half].reshape(quarter, 3 * head_cols)]
    dot_general x1 -> x2, matrix products: 17.2 us -> 22.6 us  [body(): jnp.dot(high_part[:, :quarter], other[q * blocks_half:(q + 1) * blocks_ha...]
  transfers between devices with their start and end apart: 11 -> 12, of which waited for: 7 -> 6; matrix products, arithmetic and copies ran while one was open for 18% -> 23% of each run, Pallas kernels for 0% -> 0%
where the time goes in v8:
time: 388 us; the launch traced here: 387 us
  waiting for transfers between devices  194 us (50%)
  matrix products  69.3 us (18%)
  local copies, waits for them, and re-layouts  64.5 us (17%)
  starting transfers between devices  29.2 us (8%)
  other arithmetic  15.5 us (4%)
  between operations  14.8 us (4%)
    ppermute x1, waiting for transfers between devices, gather_weights(): pair = jnp.stack([weight_shard, lax.ppermute(weight_shard, 'dp', to_yh)])  48.6 us
    ppermute x1, waiting for transfers between devices, gather_weights(): from_prev = lax.ppermute(pair, 'dp', to_next)  47.9 us
    reduce_scatter x1, waiting for transfers between devices, body(): lax.psum_scatter(jnp.dot(attended, output_projection_weight, preferred_el...  31.7 us
    all_to_all x1, waiting for transfers between devices, body(): lax.all_to_all(taken, 'dp', split_axis=0, concat_axis=0, tiled=True)  28.1 us
    all_gather x2, waiting for transfers between devices, body(): lax.all_gather(piece, 'tensor', axis=0, tiled=True)  23.6 us
    dot_general x2, matrix products, body(): jnp.dot(high_part[:, :quarter], other[q * blocks_half:(q + 1) * blocks_ha...  22.6 us
    unnamed x47, local copies, waits for them, and re-layouts  18.3 us
    dot_general x1, matrix products, body(): jnp.dot(low_part, mine.reshape(split, 3 * head_cols), preferred_element_t...  17 us
  transfers between devices with their start and end apart: 12, of which 6 were waited for; matrix products, arithmetic and copies ran while one was open for 23% of the time, Pallas kernels for 0%

profile of v8, /device:TPU:1, one launch (start us, length us, event | category | flops | bytes accessed | tf_op | source)
XLA Modules:
  0.0 387.0 jit_solution(2999620897924825575)
XLA Ops:
  7.3 2.4 copy.27
  9.6 2.2 copy.26
  11.9 1.9 fusion.5
  13.9 3.2 multiply_convert_fusion
  17.2 3.5 gather_fusion
  20.7 3.9 %copy.28 = bf16[128,7168]{1,0:T(8,128)(2,1)} copy(bf16[128,7168]{0,1:T(8,128)(2,1)} %bitcast.72) | data formatting | bytes 3670016 | tf_op jit(solution)/shard_map/jit(_take)/gather | solution.py:104
  24.7 1.7 broadcast_select_fusion
  26.5 1.2 copy-done.3
  27.7 1.0 slice.132
  28.7 3.5 concatenate.27
  32.3 3.7 collective-permute-start
  36.0 48.6 %collective-permute-done = bf16[448,1344]{1,0:T(8,128)(2,1)S(1)} collective-permute-done((bf16[448,1344]{1,0:T(8,128)(2,1)}, bf16[448,1344]{1,0:T(8,128)(2,1)S(1)}, u32[]{:S(2)}, u32[]{:S(2)}) %collective-permute-start) | collective-permute-done | bytes 1204256 | tf_op jit(solution)/shard_map/ppermute | solution.py:64
  84.6 3.5 pad_maximum_fusion
  88.1 1.1 collective-permute-start.1
  89.2 1.6 collective-permute-start.2
  90.8 1.0 fusion.77
  91.9 2.4 constant_dynamic-update-slice_fusion.3
  94.3 47.9 %collective-permute-done.1 = bf16[2,448,1344]{2,1,0:T(8,128)(2,1)} collective-permute-done((bf16[2,448,1344]{2,1,0:T(8,128)(2,1)}, bf16[2,448,1344]{2,1,0:T(8,128)(2,1)}, u32[]{:S(2)}, u32[]{:S(2)}) %collective-permute-start.1) | collective-permute-done | bytes 2408480 | tf_op jit(solution)/shard_map/ppermute | solution.py:65
  142.2 1.4 slice_bitcast_fusion.1
  143.7 1.4 slice_bitcast_fusion
  145.1 2.7 collective-permute-start.4
  147.8 1.2 constant_dynamic-update-slice_fusion.2
  149.0 3.5 constant_dynamic-update-slice_fusion.1
  152.5 3.5 constant_dynamic-update-slice_fusion
  155.9 13.7 %collective-permute-done.3 = bf16[448,1344]{1,0:T(8,128)(2,1)S(1)} collective-permute-done((bf16[448,1344]{1,0:T(8,128)(2,1)S(1)}, bf16[448,1344]{1,0:T(8,128)(2,1)S(1)}, u32[]{:S(2)}, u32[]{:S(2)}) %collective-permute-start.3) | collective-permute-done | bytes 1204256 | tf_op jit(solution)/shard_map/ppermute | solution.py:68
  169.6 1.2 bitcast_dynamic-update-slice_fusion.1
  170.8 1.2 bitcast_dynamic-update-slice_fusion
  172.0 5.4 %collective-permute-start.5 = (bf16[8,448,1344]{2,1,0:T(8,128)(2,1)}, bf16[8,448,1344]{2,1,0:T(8,128)(2,1)}, u32[]{:S(2)}, u32[]{:S(2)}) collective-permute-start(bf16[8,448,1344]{2,1,0:T(8,128)(2,1)} %bitcast_dynamic-update-slice_fusion), channel_id=1, source_target_pairs={{0,8},{8,0},{16,24},{24,16},{32,40},{40,32},{48,56},{56,48},{64,72... | collective-permute-start | bytes 28901384 | tf_op jit(solution)/shard_map/ppermute | solution.py:71
  177.4 1.2 fusion.33
  178.6 0.8 pad_maximum_fusion.4
  180.3 0.3 and_and_fusion.1
  180.6 1.2 and_and_fusion
  181.8 17.0 %fusion.82 = f32[1024,1344]{0,1:T(8,128)} fusion(bf16[1024,3584]{1,0:T(8,128)(2,1)} %all-gather.4.cloned.1.call-done, bf16[3584,1344]{1,0:T(8,128)(2,1)} %bitcast.11), kind=kOutput, calls=%fused_computation.118 | convolution fusion | flops 9865003008 | bytes 22478848 | tf_op jit(solution)/shard_map/dot_general | solution.py:115
  198.8 8.6 %fusion.76 = (bf16[4,448,1344]{2,1,0:T(8,128)(2,1)}, bf16[4,448,1344]{2,1,0:T(8,128)(2,1)}) fusion(bf16[8,448,1344]{2,1,0:T(8,128)(2,1)} %collective-permute-done.5), kind=kLoop, calls=%fused_computation.112 | loop fusion | bytes 19267584 | tf_op jit(solution)/shard_map/slice | solution.py:130
  207.4 10.1 %fusion.83 = f32[1024,1344]{0,1:T(8,128)} fusion(bf16[1024,1792]{1,0:T(8,128)(2,1)} %all-gather.6.cloned.1.call-done, bf16[1792,1344]{1,0:T(8,128)(2,1)} %bitcast.74), kind=kOutput, calls=%fused_computation.119 | convolution fusion | flops 4932501504 | bytes 13991936 | tf_op jit(solution)/shard_map/dot_general | solution.py:128
  217.5 23.6 %all-gather.8.cloned.1.call-done = bf16[1024,2176]{1,0:T(8,128)(2,1)} async-done(((bf16[128,2176]{1,0:T(8,128)(2,1)}), bf16[1024,2176]{1,0:T(8,128)(2,1)}) %all-gather.8.cloned.1.call-update) | async-done | bytes 4456464 | tf_op jit(solution)/shard_map/all_gather | solution.py:126
  241.1 12.5 %add_add_fusion = f32[1024,1344]{0,1:T(8,128)S(1)} fusion(f32[1024,1344]{0,1:T(8,128)} %fusion.82, f32[1024,1344]{0,1:T(8,128)} %fusion.83, bf16[1792,1344]{1,0:T(8,128)(2,1)} %bitcast.73, bf16[1024,2176]{1,0:T(8,128)(2,1)} %all-gather.8.cloned.1.call-done), kind=kOutput, calls=%fused_computation.5 | convolution fusion | flops 4935254016 | bytes 25231360 | tf_op jit(solution)/shard_map/dot_general | solution.py:128
  253.5 1.4 fusion.20
  254.9 0.8 slice.142
  255.7 1.3 fusion.18
  257.1 1.0 slice.151
  258.1 0.8 slice.148
  258.9 1.4 fusion.19
  260.3 1.0 fusion.78
  261.2 4.4 %fusion.80 = (f32[2,512]{1,0:T(2,128)S(1)}, f32[2,512,768]{2,1,0:T(8,128)}) fusion(pred[512,768]{1,0:T(8,128)(4,1)} %and_and_fusion, bf16[512,2,224]{0,2,1:T(8,128)(2,1)} %bitcast.81, bf16[768,2,224]{0,2,1:T(8,128)(2,1)} %bitcast.79), kind=kOutput, calls=%fused_computation.116 | convolution fusion | flops 355468032 | bytes 4689920 | tf_op jit(solution)/shard_map/sub | solution.py:39
  265.6 3.5 fusion.81
  269.1 2.3 fusion.30
  271.4 0.5 slice-done
  271.9 0.8 fusion.32
  272.7 6.1 %convolution_convert_fusion.1 = bf16[1024,3584]{1,0:T(8,128)(2,1)} fusion(bf16[448,3584]{1,0:T(8,128)(2,1)S(1)} %copy-done, bf16[512,448]{0,1:T(8,128)(2,1)S(1)} %bitcast.88, bf16[512,448]{0,1:T(8,128)(2,1)S(1)} %bitcast.87), kind=kOutput, calls=%fused_computation.4 | convolution fusion | flops 3293839360 | bytes 11468800 | tf_op jit(solution)/shard_map/dot_general | solution.py:199
  278.8 0.6 copy-done.13
  279.4 0.6 broadcast_in_dim.107
  280.0 7.3 %all-to-all-start = ((s32[16,1,4]{2,1,0:T(1,128)}), s32[16,1,4]{2,1,0:T(1,128)S(1)}, u32[]{:S(2)}, u32[]{:S(2)}) async-start(s32[16,1,4]{2,1,0:T(1,128)} %broadcast_in_dim.107), calls=%async_computation.1 | async-start | bytes 16384 | tf_op jit(solution)/shard_map/all_to_all | solution.py:175
  288.0 1.6 pad_maximum_fusion.2
  289.7 3.8 fusion.23
  293.5 4.4 %reshape.336 = bf16[16,4,14336]{2,1,0:T(4,128)(2,1)} reshape(bf16[1024,896]{1,0:T(8,128)(2,1)} %fusion.23) | data formatting | bytes 3670016 | tf_op jit(solution)/shard_map/reshape | solution.py:171
  297.9 7.2 %all-to-all-start.1 = ((bf16[16,4,14336]{2,1,0:T(4,128)(2,1)}), bf16[16,4,14336]{2,1,0:T(4,128)(2,1)}, u32[]{:S(2)}, u32[]{:S(2)}) async-start(bf16[16,4,14336]{2,1,0:T(4,128)(2,1)} %reshape.336), calls=%async_computation.2 | async-start | bytes 3670016 | tf_op jit(solution)/shard_map/all_to_all | solution.py:174
  305.1 0.5 broadcast.205
  305.6 0.7 reduce.3
  306.4 28.1 %all-to-all-done.1 = bf16[16,4,14336]{2,1,0:T(4,128)(2,1)} async-done(((bf16[16,4,14336]{2,1,0:T(4,128)(2,1)}), bf16[16,4,14336]{2,1,0:T(4,128)(2,1)}, u32[]{:S(2)}, u32[]{:S(2)}) %all-to-all-start.1) | async-done | bytes 1835040 | tf_op jit(solution)/shard_map/all_to_all | solution.py:174
  334.5 3.9 reshape.337
  338.4 3.6 convolution_convert_fusion
  342.0 6.8 %reshape.338 = bf16[64,16,2,448]{3,2,1,0:T(2,128)(2,1)} reshape(bf16[64,14336]{1,0:T(8,128)(2,1)} %convolution_convert_fusion) | data formatting | bytes 3670016 | tf_op jit(solution)/shard_map/reshape | solution.py:185
  348.7 31.7 %reduce-scatter.2.cloned.1.call-done = bf16[128,3584]{1,0:T(8,128)(2,1)} async-done(((bf16[1024,3584]{1,0:T(8,128)(2,1)}), bf16[128,3584]{1,0:T(8,128)(2,1)}) %reduce-scatter.2.cloned.1.call-update) | async-done | bytes 917520 | tf_op jit(solution)/shard_map/reduce_scatter | solution.py:198
  (82 shorter events, 1.5 us)
Async XLA Ops:
  7.2 265.5 %copy-start = (bf16[448,3584]{1,0:T(8,128)(2,1)S(1)}, bf16[448,3584]{1,0:T(8,128)(2,1)}, u32[]{:S(2)}) copy-start(bf16[448,3584]{1,0:T(8,128)(2,1)} %param.23) | copy-start | bytes 9633796
  7.2 6.7 %copy-start.14 = (s32[16]{0:T(128)S(1)}, s32[16]{0:T(128)}, u32[]{:S(2)}) copy-start(s32[16]{0:T(128)} %constant.102.clone) | copy-start | bytes 196
  7.2 6.7 %copy-start.15 = (s32[16]{0:T(128)S(1)}, s32[16]{0:T(128)}, u32[]{:S(2)}) copy-start(s32[16]{0:T(128)} %constant.101.clone) | copy-start | bytes 196
  7.2 6.7 %copy-start.16 = (s32[16]{0:T(128)S(1)}, s32[16]{0:T(128)}, u32[]{:S(2)}) copy-start(s32[16]{0:T(128)} %constant.100.clone) | copy-start | bytes 196
  7.2 6.6 %copy-start.12 = (f32[7168]{0:T(1024)S(1)}, f32[7168]{0:T(1024)}, u32[]{:S(2)}) copy-start(f32[7168]{0:T(1024)} %param.17) | copy-start | bytes 86020
  7.2 174.6 %all-gather.4.cloned.1.call-start = ((), (), s32[]{:S(2)}) async-start(), calls=%async_computation.3 | async-start | bytes 8257536 | tf_op jit(solution)/shard_map/all_gather | solution.py:113
  26.4 1.2 copy-start.3
  28.7 178.7 %all-gather.6.cloned.1.call-start = ((), (), s32[]{:S(2)}) async-start(), calls=%async_computation.4 | async-start | bytes 4128768 | tf_op jit(solution)/shard_map/all_gather | solution.py:126
  32.3 58.5 %copy-start.4 = (bf16[128,7168]{1,0:T(8,128)(2,1)S(1)}, bf16[128,7168]{1,0:T(8,128)(2,1)}, u32[]{:S(2)}) copy-start(bf16[128,7168]{1,0:T(8,128)(2,1)} %copy-done.3) | copy-start | bytes 5505028
  32.3 52.4 %collective-permute-start = (bf16[448,1344]{1,0:T(8,128)(2,1)}, bf16[448,1344]{1,0:T(8,128)(2,1)S(1)}, u32[]{:S(2)}, u32[]{:S(2)}) collective-permute-start(bf16[448,1344]{1,0:T(8,128)(2,1)} %concatenate.27), channel_id=1, source_target_pairs={{0,16},{8,24},{16,0},{24,8},{32,48},{40,56},{48,32},{56,40},{64,80... | collective-permute-start | bytes 3612680 | tf_op jit(solution)/shard_map/ppermute | solution.py:64
  84.6 7.2 %copy-start.5 = (bf16[448,1344]{1,0:T(8,128)(2,1)}, bf16[448,1344]{1,0:T(8,128)(2,1)S(1)}, u32[]{:S(2)}) copy-start(bf16[448,1344]{1,0:T(8,128)(2,1)S(1)} %collective-permute-done) | copy-start | bytes 3612676
  88.1 54.1 %collective-permute-start.1 = (bf16[2,448,1344]{2,1,0:T(8,128)(2,1)}, bf16[2,448,1344]{2,1,0:T(8,128)(2,1)}, u32[]{:S(2)}, u32[]{:S(2)}) collective-permute-start(bf16[2,448,1344]{2,1,0:T(8,128)(2,1)} %pad_maximum_fusion), channel_id=1, source_target_pairs={{0,32},{8,40},{16,48},{24,56},{32,64},{40,72},{48,80},{56,88},{64,... | collective-permute-start | bytes 7225352 | tf_op jit(solution)/shard_map/ppermute | solution.py:65
  89.2 54.5 %collective-permute-start.2 = (bf16[2,448,1344]{2,1,0:T(8,128)(2,1)}, bf16[2,448,1344]{2,1,0:T(8,128)(2,1)}, u32[]{:S(2)}, u32[]{:S(2)}) collective-permute-start(bf16[2,448,1344]{2,1,0:T(8,128)(2,1)} %pad_maximum_fusion), channel_id=1, source_target_pairs={{0,96},{8,104},{16,112},{24,120},{32,0},{40,8},{48,16},{56,24},{64... | collective-permute-start | bytes 7225352 | tf_op jit(solution)/shard_map/ppermute | solution.py:66
  91.8 149.2 %all-gather.8.cloned.1.call-start = ((), (), s32[]{:S(2)}) async-start(), calls=%async_computation.5 | async-start | bytes 5013504 | tf_op jit(solution)/shard_map/all_gather | solution.py:126
  94.3 53.5 %copy-start.6 = (bf16[448,1344]{1,0:T(8,128)(2,1)S(1)}, bf16[448,1344]{1,0:T(8,128)(2,1)}, u32[]{:S(2)}) copy-start(bf16[448,1344]{1,0:T(8,128)(2,1)} %copy-done.5) | copy-start | bytes 3612676
  143.6 26.0 %collective-permute-start.3 = (bf16[448,1344]{1,0:T(8,128)(2,1)S(1)}, bf16[448,1344]{1,0:T(8,128)(2,1)S(1)}, u32[]{:S(2)}, u32[]{:S(2)}) collective-permute-start(bf16[448,1344]{1,0:T(8,128)(2,1)S(1)} %slice_bitcast_fusion.1), channel_id=1, source_target_pairs={{0,32},{8,40},{16,48},{24,56},{32,64},{40,72},{48,80},{56,88},{64,... | collective-permute-start | bytes 3612680 | tf_op jit(solution)/shard_map/ppermute | solution.py:68
  145.1 25.7 %collective-permute-start.4 = (bf16[448,1344]{1,0:T(8,128)(2,1)S(1)}, bf16[448,1344]{1,0:T(8,128)(2,1)S(1)}, u32[]{:S(2)}, u32[]{:S(2)}) collective-permute-start(bf16[448,1344]{1,0:T(8,128)(2,1)S(1)} %slice_bitcast_fusion), channel_id=1, source_target_pairs={{0,96},{8,104},{16,112},{24,120},{32,0},{40,8},{48,16},{56,24},{64... | collective-permute-start | bytes 3612680 | tf_op jit(solution)/shard_map/ppermute | solution.py:68
  149.0 28.4 %slice-start.1 = ((s8[5505024]{0:T(1024)(128)(4,1)}), s8[4194304]{0:T(1024)(128)(4,1)S(1)}, s32[]{:S(2)}) async-start(s8[5505024]{0:T(1024)(128)(4,1)} %bitcast.85), calls=%async_computation.8 | async-start | bytes 8388608
  152.5 24.9 %slice-start.2 = ((s8[5505024]{0:T(1024)(128)(4,1)}), s8[1310720]{0:T(1024)(128)(4,1)S(1)}, s32[]{:S(2)}) async-start(s8[5505024]{0:T(1024)(128)(4,1)} %bitcast.85), calls=%async_computation.9 | async-start | bytes 2621440
  155.9 21.4 %copy-start.7 = (bf16[128,3584]{1,0:T(8,128)(2,1)S(1)}, bf16[128,3584]{1,0:T(8,128)(2,1)}, u32[]{:S(2)}) copy-start(bf16[128,3584]{1,0:T(8,128)(2,1)} %param.16) | copy-start | bytes 2752516
  155.9 21.4 %copy-start.8 = (bf16[128,3584]{1,0:T(8,128)(2,1)S(1)}, bf16[128,3584]{1,0:T(8,128)(2,1)}, u32[]{:S(2)}) copy-start(bf16[128,3584]{1,0:T(8,128)(2,1)} %param.15) | copy-start | bytes 2752516
  172.0 6.6 %copy-start.9 = (bf16[128,1792]{1,0:T(8,128)(2,1)S(1)}, bf16[128,1792]{1,0:T(8,128)(2,1)}, u32[]{:S(2)}) copy-start(bf16[128,1792]{1,0:T(8,128)(2,1)} %get-tuple-element.6) | copy-start | bytes 1376260
  172.0 7.6 %copy-start.11 = (s32[1024]{0:T(1024)S(1)}, s32[1024]{0:T(1024)}, u32[]{:S(2)}) copy-start(s32[1024]{0:T(1024)} %param.24) | copy-start | bytes 12292
  172.0 26.8 %collective-permute-start.5 = (bf16[8,448,1344]{2,1,0:T(8,128)(2,1)}, bf16[8,448,1344]{2,1,0:T(8,128)(2,1)}, u32[]{:S(2)}, u32[]{:S(2)}) collective-permute-start(bf16[8,448,1344]{2,1,0:T(8,128)(2,1)} %bitcast_dynamic-update-slice_fusion), channel_id=1, source_target_pairs={{0,8},{8,0},{16,24},{24,16},{32,40},{40,32},{48,56},{56,48},{64,72... | collective-permute-start | bytes 28901384 | tf_op jit(solution)/shard_map/ppermute | solution.py:71
  179.5 201.0 %reduce-scatter.2.cloned.1.call-start = ((), (), s32[]{:S(2)}) async-start(), calls=%async_computation.6 | async-start | bytes 8257536 | tf_op jit(solution)/shard_map/reduce_scatter | solution.py:198
  241.1 12.5 %copy-start.10 = (bf16[3,128,448]{1,2,0:T(8,128)(2,1)S(1)}, bf16[3,128,448]{1,2,0:T(8,128)(2,1)}, u32[]{:S(2)}) copy-start(bf16[3,128,448]{1,2,0:T(8,128)(2,1)} %param.22) | copy-start | bytes 1032196
  254.9 3.2 copy-start.1
  257.1 4.1 %copy-start.2 = (bf16[1024,448]{0,1:T(8,128)(2,1)}, bf16[1024,448]{0,1:T(8,128)(2,1)S(1)}, u32[]{:S(2)}) copy-start(bf16[1024,448]{0,1:T(8,128)(2,1)S(1)} %fusion.18) | copy-start | bytes 2752516
  269.1 2.8 slice-start
  269.1 2.8 copy-start.17
  278.8 0.7 copy-start.13
  280.0 17.9 %all-to-all-start = ((s32[16,1,4]{2,1,0:T(1,128)}), s32[16,1,4]{2,1,0:T(1,128)S(1)}, u32[]{:S(2)}, u32[]{:S(2)}) async-start(s32[16,1,4]{2,1,0:T(1,128)} %broadcast_in_dim.107), calls=%async_computation.1 | async-start | bytes 16384 | tf_op jit(solution)/shard_map/all_to_all | solution.py:175
  297.9 36.6 %all-to-all-start.1 = ((bf16[16,4,14336]{2,1,0:T(4,128)(2,1)}), bf16[16,4,14336]{2,1,0:T(4,128)(2,1)}, u32[]{:S(2)}, u32[]{:S(2)}) async-start(bf16[16,4,14336]{2,1,0:T(4,128)(2,1)} %reshape.336), calls=%async_computation.2 | async-start | bytes 3670016 | tf_op jit(solution)/shard_map/all_to_all | solution.py:174
Sparse Core Ops, SparseCore 0:
  28.8 108.7 all-gather.3
  139.3 45.0 all-gather.5
  186.6 54.3 all-gather.7
  278.9 101.4 reduce-scatter.1

commit v9 on v7

--- a/solution.py
+++ b/solution.py
@@ -3,10 +3,11 @@
 import jax
 import jax.numpy as jnp
 from jax import lax
-from jax.sharding import PartitionSpec as P
+from jax.sharding import Mesh, PartitionSpec as P
 from jax.experimental.layout import Layout, with_layout_constraint
 
 HD = 224
+TENSOR = ("yl", "z")
 
 
 epsilon = 1e-05
@@ -110,14 +111,14 @@
     ).astype(jnp.bfloat16)
     row_major = Layout((0, 1))
     low_part = with_layout_constraint(
-        lax.all_gather(in_order[:, :split], "tensor", axis=0, tiled=True), row_major
+        lax.all_gather(in_order[:, :split], TENSOR, axis=0, tiled=True), row_major
     )
     folded_all = jnp.dot(
         low_part, mine.reshape(split, 3 * head_cols), preferred_element_type=jnp.float32
     )
     high_part = with_layout_constraint(
         lax.all_gather(
-            jnp.concatenate([in_order[:, split:], low_local], 1), "tensor", axis=0, tiled=True
+            jnp.concatenate([in_order[:, split:], low_local], 1), TENSOR, axis=0, tiled=True
         ),
         row_major,
     )
@@ -189,35 +190,38 @@
             )
         )
     attended = jnp.concatenate(attended_parts, 0)
-    block_out = lax.psum_scatter(
-        jnp.dot(attended, output_projection_weight, preferred_element_type=jnp.float32).astype(
-            jnp.bfloat16
-        ),
-        "tensor",
-        scatter_dimension=0,
-        tiled=True,
-    )
+    partial_value = jnp.dot(
+        attended, output_projection_weight, preferred_element_type=jnp.float32
+    ).astype(jnp.bfloat16)
+    planes, ring = lax.axis_size("yl"), lax.axis_size("z")
+    by_z = partial_value.reshape(planes, ring, -1, partial_value.shape[1]).transpose(1, 0, 2, 3)
+    within = lax.psum_scatter(
+        by_z.reshape(-1, partial_value.shape[1]), "z", scatter_dimension=0, tiled=True
+    )
+    block_out = lax.psum_scatter(within, "yl", scatter_dimension=0, tiled=True)
     return (block_out, kv_cache)
 
 
 def solution(mesh):
+    dp, tensor = mesh.devices.shape
+    split_mesh = Mesh(mesh.devices.reshape(dp, 2, tensor // 2), ("dp",) + TENSOR)
     return jax.shard_map(
         body,
-        mesh=mesh,
+        mesh=split_mesh,
         in_specs=(
-            P(("dp", "tensor"), None),
-            P(("dp", "tensor"), None),
+            P(("dp",) + TENSOR, None),
+            P(("dp",) + TENSOR, None),
             P(),
-            P("dp", "tensor"),
-            P("dp", "tensor"),
-            P("dp", "tensor"),
+            P("dp", TENSOR),
+            P("dp", TENSOR),
+            P("dp", TENSOR),
             P(),
-            P(None, None, "tensor"),
-            P("tensor", None),
+            P(None, None, TENSOR),
+            P(TENSOR, None),
             P("dp"),
             P("dp"),
             P("dp"),
         ),
-        out_specs=(P(("dp", "tensor"), None), P(None, "dp", None, "tensor")),
+        out_specs=(P(("dp",) + TENSOR, None), P(None, "dp", None, TENSOR)),
         check_vma=False,
     )

time: 385 us -> 417 us (1.083)
  waiting for transfers between devices: 200 us -> 231 us
    reduce_scatter x1 -> x2, waiting for transfers between devices: 31.7 us -> 62.8 us  [the longest x1 62.8 us: body(): lax.psum_scatter(by_z.reshape(-1, partial_value.shape[1]), 'z', scatter_d...]
  transfers between devices with their start and end apart: 11 -> 12, of which waited for: 7 -> 7; matrix products, arithmetic and copies ran while one was open for 18% -> 17% of each run, Pallas kernels for 0% -> 0%
where the time goes in v9:
time: 417 us; the launch traced here: 416 us
  waiting for transfers between devices  231 us (55%)
  matrix products  68.1 us (16%)
  local copies, waits for them, and re-layouts  56.9 us (14%)
  starting transfers between devices  29.5 us (7%)
  other arithmetic  16.2 us (4%)
  between operations  14.8 us (4%)
    reduce_scatter x1, waiting for transfers between devices, body(): lax.psum_scatter(by_z.reshape(-1, partial_value.shape[1]), 'z', scatter_d...  62.8 us
    ppermute x1, waiting for transfers between devices, gather_weights(): from_prev = lax.ppermute(pair, 'dp', to_next)  48.9 us
    ppermute x1, waiting for transfers between devices, gather_weights(): pair = jnp.stack([weight_shard, lax.ppermute(weight_shard, 'dp', to_yh)])  48.6 us
    all_to_all x1, waiting for transfers between devices, body(): lax.all_to_all(taken, 'dp', split_axis=0, concat_axis=0, tiled=True)  27.8 us
    dot_general x1, matrix products, body(): jnp.dot(low_part, mine.reshape(split, 3 * head_cols), preferred_element_t...  17.9 us
    dot_general x1, matrix products, body(): jnp.dot(high_part[:, :split], other.reshape(split, 3 * head_cols), prefer...  17.2 us
    unnamed x47, local copies, waits for them, and re-layouts  16.8 us
    all_gather x1, waiting for transfers between devices, body(): lax.all_gather(in_order[:, :split], TENSOR, axis=0, tiled=True)  16.7 us
  transfers between devices with their start and end apart: 12, of which 7 were waited for; matrix products, arithmetic and copies ran while one was open for 17% of the time, Pallas kernels for 0%

profile of v9, /device:TPU:1, one launch (start us, length us, event | category | flops | bytes accessed | tf_op | source)
XLA Modules:
  0.0 416.3 jit_solution(4575929386296419232)
XLA Ops:
  7.3 2.4 copy.30
  9.6 1.9 fusion.7
  11.5 2.2 copy.29
  13.9 4.4 %fusion.31 = bf16[128,384]{1,0:T(8,128)(2,1)S(1)} fusion(bf16[7168,384]{1,0:T(8,128)(2,1)} %param.21, f32[7168]{0:T(1024)S(1)} %copy-done.11, f32[128]{0:T(128)S(1)} %add_rsqrt_fusion, bf16[128,3584]{1,0:T(8,128)(2,1)} %param.16, bf16[128,3584]{1,0:T(8,128)(2,1)} %param.15), kind=kOutput, calls=%fused_computation.54 | convolution fusion | flops 711114752 | bytes 7467520 | tf_op jit(solution)/shard_map/dot_general | solution.py:109
  18.4 2.5 multiply_convert_fusion
  20.8 3.5 gather_fusion
  24.4 3.9 copy.31
  28.4 1.7 broadcast_select_fusion
  30.1 1.0 fusion.65
  31.2 1.0 pad_maximum_fusion.4
  32.3 3.5 concatenate.27
  35.8 3.7 collective-permute-start
  39.5 48.6 %collective-permute-done = bf16[448,1344]{1,0:T(8,128)(2,1)S(1)} collective-permute-done((bf16[448,1344]{1,0:T(8,128)(2,1)}, bf16[448,1344]{1,0:T(8,128)(2,1)S(1)}, u32[]{:S(2)}, u32[]{:S(2)}) %collective-permute-start) | collective-permute-done | bytes 1204256 | tf_op jit(solution)/shard_map/ppermute | solution.py:65
  88.1 3.5 pad_maximum_fusion
  91.6 1.1 collective-permute-start.1
  92.7 1.6 collective-permute-start.2
  94.4 2.4 constant_dynamic-update-slice_fusion.3
  96.8 48.9 %collective-permute-done.1 = bf16[2,448,1344]{2,1,0:T(8,128)(2,1)} collective-permute-done((bf16[2,448,1344]{2,1,0:T(8,128)(2,1)}, bf16[2,448,1344]{2,1,0:T(8,128)(2,1)}, u32[]{:S(2)}, u32[]{:S(2)}) %collective-permute-start.1) | collective-permute-done | bytes 2408480 | tf_op jit(solution)/shard_map/ppermute | solution.py:66
  145.7 1.4 slice_bitcast_fusion.1
  147.2 1.4 slice_bitcast_fusion
  148.6 2.7 collective-permute-start.4
  151.3 1.2 constant_dynamic-update-slice_fusion.2
  152.5 3.3 constant_dynamic-update-slice_fusion.1
  155.8 3.4 constant_dynamic-update-slice_fusion
  159.2 13.9 %collective-permute-done.3 = bf16[448,1344]{1,0:T(8,128)(2,1)S(1)} collective-permute-done((bf16[448,1344]{1,0:T(8,128)(2,1)S(1)}, bf16[448,1344]{1,0:T(8,128)(2,1)S(1)}, u32[]{:S(2)}, u32[]{:S(2)}) %collective-permute-start.3) | collective-permute-done | bytes 1204256 | tf_op jit(solution)/shard_map/ppermute | solution.py:69
  173.1 1.2 bitcast_dynamic-update-slice_fusion.1
  174.3 1.2 bitcast_dynamic-update-slice_fusion
  175.5 5.4 %collective-permute-start.5 = (bf16[8,448,1344]{2,1,0:T(8,128)(2,1)}, bf16[8,448,1344]{2,1,0:T(8,128)(2,1)}, u32[]{:S(2)}, u32[]{:S(2)}) collective-permute-start(bf16[8,448,1344]{2,1,0:T(8,128)(2,1)} %bitcast_dynamic-update-slice_fusion), channel_id=1, source_target_pairs={{0,8},{8,0},{16,24},{24,16},{32,40},{40,32},{48,56},{56,48},{64,72... | collective-permute-start | bytes 28901384 | tf_op jit(solution)/shard_map/ppermute | solution.py:72
  181.6 0.5 broadcast_compare_fusion.2
  182.2 1.0 and_and_fusion.1
  183.2 1.2 and_and_fusion
  184.3 12.1 %collective-permute-done.5 = bf16[8,448,1344]{2,1,0:T(8,128)(2,1)} collective-permute-done((bf16[8,448,1344]{2,1,0:T(8,128)(2,1)}, bf16[8,448,1344]{2,1,0:T(8,128)(2,1)}, u32[]{:S(2)}, u32[]{:S(2)}) %collective-permute-start.5) | collective-permute-done | bytes 9633824 | tf_op jit(solution)/shard_map/ppermute | solution.py:72
  196.4 17.2 %fusion.2 = f32[1024,1344]{0,1:T(8,128)} fusion(bf16[3584,1344]{1,0:T(8,128)(2,1)} %bitcast.12, bf16[1024,3968]{1,0:T(8,128)(2,1)} %all-gather.5.cloned.1.call-done), kind=kOutput, calls=%fused_computation.5 | convolution fusion | flops 9865003008 | bytes 22937600 | tf_op jit(solution)/shard_map/dot_general | solution.py:125
  213.6 16.7 %all-gather.3.cloned.1.call-done = bf16[1024,3584]{1,0:T(8,128)(2,1)} async-done(((bf16[128,3584]{1,0:T(8,128)(2,1)}), bf16[1024,3584]{1,0:T(8,128)(2,1)}) %all-gather.3.cloned.1.call-update) | async-done | bytes 7340048 | tf_op jit(solution)/shard_map/all_gather | solution.py:114
  230.3 17.9 %convolution_add_fusion = f32[1024,1344]{0,1:T(8,128)} fusion(f32[1024,1344]{0,1:T(8,128)} %fusion.2, bf16[1024,3584]{1,0:T(8,128)(2,1)} %all-gather.3.cloned.1.call-done, bf16[3584,1344]{1,0:T(8,128)(2,1)} %bitcast.11), kind=kOutput, calls=%fused_computation.9 | convolution fusion | flops 9866379264 | bytes 27983872 | tf_op jit(solution)/shard_map/dot_general | solution.py:116
  248.2 2.0 fusion.18
  250.2 0.8 slice.127
  251.0 2.0 fusion.16
  253.1 1.0 slice.136
  254.1 0.8 slice.133
  254.9 2.0 fusion.17
  256.9 1.0 fusion.66
  257.9 4.5 %fusion.68 = (f32[2,512]{1,0:T(2,128)S(1)}, f32[2,512,768]{2,1,0:T(8,128)}) fusion(pred[512,768]{1,0:T(8,128)(4,1)} %and_and_fusion, bf16[512,2,224]{0,2,1:T(8,128)(2,1)} %bitcast.82, bf16[768,2,224]{0,2,1:T(8,128)(2,1)} %bitcast.80), kind=kOutput, calls=%fused_computation.112 | convolution fusion | flops 355468032 | bytes 4689920 | tf_op jit(solution)/shard_map/sub | solution.py:40
  262.3 3.5 fusion.69
  265.8 2.3 fusion.28
  268.1 0.5 slice-done
  268.6 0.8 fusion.30
  269.4 4.3 %convolution_convert_fusion.1 = bf16[1024,3584]{1,0:T(8,128)(2,1)S(1)} fusion(bf16[448,3584]{1,0:T(8,128)(2,1)S(1)} %copy-done, bf16[512,448]{0,1:T(8,128)(2,1)S(1)} %bitcast.87, bf16[512,448]{0,1:T(8,128)(2,1)S(1)} %bitcast.86), kind=kOutput, calls=%fused_computation.4 | convolution fusion | flops 3293839360 | bytes 11468800 | tf_op jit(solution)/shard_map/dot_general | solution.py:193
  273.7 3.4 copy.33
  277.1 0.6 copy-done.14
  277.8 0.6 broadcast_in_dim.107
  278.4 7.3 %all-to-all-start = ((s32[16,1,4]{2,1,0:T(1,128)}), s32[16,1,4]{2,1,0:T(1,128)S(1)}, u32[]{:S(2)}, u32[]{:S(2)}) async-start(s32[16,1,4]{2,1,0:T(1,128)} %broadcast_in_dim.107), calls=%async_computation.2 | async-start | bytes 16384 | tf_op jit(solution)/shard_map/all_to_all | solution.py:170
  285.8 0.2 reduce-window.8
  286.0 62.8 %reduce-scatter.3.cloned.1.call-done = bf16[256,3584]{1,0:T(8,128)(2,1)} async-done(((bf16[1024,3584]{1,0:T(8,128)(2,1)}), bf16[256,3584]{1,0:T(8,128)(2,1)}) %reduce-scatter.3.cloned.1.call-update) | async-done | bytes 1835024 | tf_op jit(solution)/shard_map/reduce_scatter | solution.py:198
  349.2 1.6 pad_maximum_fusion.2
  350.9 3.8 fusion.21
  354.7 4.3 %reshape.340 = bf16[16,4,14336]{2,1,0:T(4,128)(2,1)} reshape(bf16[1024,896]{1,0:T(8,128)(2,1)} %fusion.21) | data formatting | bytes 3670016 | tf_op jit(solution)/shard_map/reshape | solution.py:166
  359.0 7.5 %all-to-all-start.1 = ((bf16[16,4,14336]{2,1,0:T(4,128)(2,1)}), bf16[16,4,14336]{2,1,0:T(4,128)(2,1)}, u32[]{:S(2)}, u32[]{:S(2)}) async-start(bf16[16,4,14336]{2,1,0:T(4,128)(2,1)} %reshape.340), calls=%async_computation.3 | async-start | bytes 3670016 | tf_op jit(solution)/shard_map/all_to_all | solution.py:169
  366.5 0.5 broadcast.205
  367.0 0.7 reduce.3
  367.8 27.8 %all-to-all-done.1 = bf16[16,4,14336]{2,1,0:T(4,128)(2,1)} async-done(((bf16[16,4,14336]{2,1,0:T(4,128)(2,1)}), bf16[16,4,14336]{2,1,0:T(4,128)(2,1)}, u32[]{:S(2)}, u32[]{:S(2)}) %all-to-all-start.1) | async-done | bytes 1835040 | tf_op jit(solution)/shard_map/all_to_all | solution.py:169
  395.6 3.8 reshape.341
  399.4 3.5 convolution_convert_fusion
  403.0 6.8 %reshape.342 = bf16[64,16,2,448]{3,2,1,0:T(2,128)(2,1)} reshape(bf16[64,14336]{1,0:T(8,128)(2,1)} %convolution_convert_fusion) | data formatting | bytes 3670016 | tf_op jit(solution)/shard_map/reshape | solution.py:180
  (79 shorter events, 1.4 us)
Async XLA Ops:
  7.2 262.2 %copy-start = (bf16[448,3584]{1,0:T(8,128)(2,1)S(1)}, bf16[448,3584]{1,0:T(8,128)(2,1)}, u32[]{:S(2)}) copy-start(bf16[448,3584]{1,0:T(8,128)(2,1)} %param.23) | copy-start | bytes 9633796
  7.2 6.7 %copy-start.15 = (s32[16]{0:T(128)S(1)}, s32[16]{0:T(128)}, u32[]{:S(2)}) copy-start(s32[16]{0:T(128)} %constant.102.clone) | copy-start | bytes 196
  7.2 6.6 %copy-start.16 = (s32[16]{0:T(128)S(1)}, s32[16]{0:T(128)}, u32[]{:S(2)}) copy-start(s32[16]{0:T(128)} %constant.101.clone) | copy-start | bytes 196
  7.2 6.6 %copy-start.17 = (s32[16]{0:T(128)S(1)}, s32[16]{0:T(128)}, u32[]{:S(2)}) copy-start(s32[16]{0:T(128)} %constant.100.clone) | copy-start | bytes 196
  7.2 6.5 %copy-start.11 = (f32[7168]{0:T(1024)S(1)}, f32[7168]{0:T(1024)}, u32[]{:S(2)}) copy-start(f32[7168]{0:T(1024)} %param.17) | copy-start | bytes 86020
  7.2 177.1 %all-gather.5.cloned.1.call-start = ((), (), s32[]{:S(2)}) async-start(), calls=%async_computation.5 | async-start | bytes 9142272 | tf_op jit(solution)/shard_map/all_gather | solution.py:120
  13.9 4.5 %copy-start.5 = (bf16[128,3584]{0,1:T(8,128)(2,1)S(1)}, bf16[128,3584]{0,1:T(8,128)(2,1)}, u32[]{:S(2)}) copy-start(bf16[128,3584]{0,1:T(8,128)(2,1)} %copy.30) | copy-start | bytes 2752516
  13.9 4.5 %copy-start.6 = (bf16[128,3584]{0,1:T(8,128)(2,1)S(1)}, bf16[128,3584]{0,1:T(8,128)(2,1)}, u32[]{:S(2)}) copy-start(bf16[128,3584]{0,1:T(8,128)(2,1)} %copy.29) | copy-start | bytes 2752516
  32.2 198.0 %all-gather.3.cloned.1.call-start = ((), (), s32[]{:S(2)}) async-start(), calls=%async_computation.4 | async-start | bytes 8257536 | tf_op jit(solution)/shard_map/all_gather | solution.py:114
  35.8 52.3 %collective-permute-start = (bf16[448,1344]{1,0:T(8,128)(2,1)}, bf16[448,1344]{1,0:T(8,128)(2,1)S(1)}, u32[]{:S(2)}, u32[]{:S(2)}) collective-permute-start(bf16[448,1344]{1,0:T(8,128)(2,1)} %concatenate.27), channel_id=1, source_target_pairs={{0,16},{8,24},{16,0},{24,8},{32,48},{40,56},{48,32},{56,40},{64,80... | collective-permute-start | bytes 3612680 | tf_op jit(solution)/shard_map/ppermute | solution.py:65
  88.1 3.5 copy-start.3
  91.6 54.1 %collective-permute-start.1 = (bf16[2,448,1344]{2,1,0:T(8,128)(2,1)}, bf16[2,448,1344]{2,1,0:T(8,128)(2,1)}, u32[]{:S(2)}, u32[]{:S(2)}) collective-permute-start(bf16[2,448,1344]{2,1,0:T(8,128)(2,1)} %pad_maximum_fusion), channel_id=1, source_target_pairs={{0,32},{8,40},{16,48},{24,56},{32,64},{40,72},{48,80},{56,88},{64,... | collective-permute-start | bytes 7225352 | tf_op jit(solution)/shard_map/ppermute | solution.py:66
  92.7 54.5 %collective-permute-start.2 = (bf16[2,448,1344]{2,1,0:T(8,128)(2,1)}, bf16[2,448,1344]{2,1,0:T(8,128)(2,1)}, u32[]{:S(2)}, u32[]{:S(2)}) collective-permute-start(bf16[2,448,1344]{2,1,0:T(8,128)(2,1)} %pad_maximum_fusion), channel_id=1, source_target_pairs={{0,96},{8,104},{16,112},{24,120},{32,0},{40,8},{48,16},{56,24},{64... | collective-permute-start | bytes 7225352 | tf_op jit(solution)/shard_map/ppermute | solution.py:67
  94.3 254.4 %reduce-scatter.3.cloned.1.call-start = ((), (), s32[]{:S(2)}) async-start(), calls=%async_computation.6 | async-start | bytes 9175040 | tf_op jit(solution)/shard_map/reduce_scatter | solution.py:198
  96.8 54.5 %copy-start.4 = (bf16[448,1344]{1,0:T(8,128)(2,1)S(1)}, bf16[448,1344]{1,0:T(8,128)(2,1)}, u32[]{:S(2)}) copy-start(bf16[448,1344]{1,0:T(8,128)(2,1)} %copy-done.3) | copy-start | bytes 3612676
  147.1 26.0 %collective-permute-start.3 = (bf16[448,1344]{1,0:T(8,128)(2,1)S(1)}, bf16[448,1344]{1,0:T(8,128)(2,1)S(1)}, u32[]{:S(2)}, u32[]{:S(2)}) collective-permute-start(bf16[448,1344]{1,0:T(8,128)(2,1)S(1)} %slice_bitcast_fusion.1), channel_id=1, source_target_pairs={{0,32},{8,40},{16,48},{24,56},{32,64},{40,72},{48,80},{56,88},{64,... | collective-permute-start | bytes 3612680 | tf_op jit(solution)/shard_map/ppermute | solution.py:69
  148.6 25.7 %collective-permute-start.4 = (bf16[448,1344]{1,0:T(8,128)(2,1)S(1)}, bf16[448,1344]{1,0:T(8,128)(2,1)S(1)}, u32[]{:S(2)}, u32[]{:S(2)}) collective-permute-start(bf16[448,1344]{1,0:T(8,128)(2,1)S(1)} %slice_bitcast_fusion), channel_id=1, source_target_pairs={{0,96},{8,104},{16,112},{24,120},{32,0},{40,8},{48,16},{56,24},{64... | collective-permute-start | bytes 3612680 | tf_op jit(solution)/shard_map/ppermute | solution.py:69
  159.2 21.6 %copy-start.9 = (s32[1024]{0:T(1024)S(1)}, s32[1024]{0:T(1024)}, u32[]{:S(2)}) copy-start(s32[1024]{0:T(1024)} %param.24) | copy-start | bytes 12292
  175.5 21.0 %collective-permute-start.5 = (bf16[8,448,1344]{2,1,0:T(8,128)(2,1)}, bf16[8,448,1344]{2,1,0:T(8,128)(2,1)}, u32[]{:S(2)}, u32[]{:S(2)}) collective-permute-start(bf16[8,448,1344]{2,1,0:T(8,128)(2,1)} %bitcast_dynamic-update-slice_fusion), channel_id=1, source_target_pairs={{0,8},{8,0},{16,24},{24,16},{32,40},{40,32},{48,56},{56,48},{64,72... | collective-permute-start | bytes 28901384 | tf_op jit(solution)/shard_map/ppermute | solution.py:72
  182.1 1.0 copy-start.12
  230.3 17.9 %copy-start.7 = (bf16[3,128,448]{1,2,0:T(8,128)(2,1)S(1)}, bf16[3,128,448]{1,2,0:T(8,128)(2,1)}, u32[]{:S(2)}) copy-start(bf16[3,128,448]{1,2,0:T(8,128)(2,1)} %param.22) | copy-start | bytes 1032196
  250.2 2.9 copy-start.1
  253.1 3.8 copy-start.2
  257.9 4.5 %copy-start.8 = (pred[512,512]{0,1:T(8,128)(4,1)S(1)}, pred[512,512]{0,1:T(8,128)(4,1)}, u32[]{:S(2)}) copy-start(pred[512,512]{0,1:T(8,128)(4,1)} %and_and_fusion.1) | copy-start | bytes 786436
  262.3 3.5 copy-start.13
  265.8 2.8 slice-start
  265.8 2.8 copy-start.18
  265.8 2.8 copy-start.19
  277.1 0.7 copy-start.14
  277.1 8.6 %copy-start.10 = (s32[1024]{0:T(1024)S(1)}, s32[1024]{0:T(1024)}, u32[]{:S(2)}) copy-start(s32[1024]{0:T(1024)} %param.24) | copy-start | bytes 12292
  278.4 80.6 %all-to-all-start = ((s32[16,1,4]{2,1,0:T(1,128)}), s32[16,1,4]{2,1,0:T(1,128)S(1)}, u32[]{:S(2)}, u32[]{:S(2)}) async-start(s32[16,1,4]{2,1,0:T(1,128)} %broadcast_in_dim.107), calls=%async_computation.2 | async-start | bytes 16384 | tf_op jit(solution)/shard_map/all_to_all | solution.py:170
  285.6 124.1 %reduce-scatter.5.cloned.1.call-start = ((), (), s32[]{:S(2)}) async-start(), calls=%async_computation.7 | async-start | bytes 2752512 | tf_op jit(solution)/shard_map/reduce_scatter | solution.py:201
  359.0 36.6 %all-to-all-start.1 = ((bf16[16,4,14336]{2,1,0:T(4,128)(2,1)}), bf16[16,4,14336]{2,1,0:T(4,128)(2,1)}, u32[]{:S(2)}, u32[]{:S(2)}) async-start(bf16[16,4,14336]{2,1,0:T(4,128)(2,1)} %reshape.340), calls=%async_computation.3 | async-start | bytes 3670016 | tf_op jit(solution)/shard_map/all_to_all | solution.py:169
Sparse Core Ops, SparseCore 0:
  32.3 116.1 all-gather.4
  150.7 79.4 all-gather.2
  277.3 71.4 reduce-scatter.2
  351.6 50.7 reduce-scatter.4

commit v10 on v7

--- a/solution.py
+++ b/solution.py
@@ -109,22 +109,31 @@
         normalized_hidden, adapter_down_maps, preferred_element_type=jnp.float32
     ).astype(jnp.bfloat16)
     row_major = Layout((0, 1))
-    low_part = with_layout_constraint(
-        lax.all_gather(in_order[:, :split], "tensor", axis=0, tiled=True), row_major
-    )
-    folded_all = jnp.dot(
-        low_part, mine.reshape(split, 3 * head_cols), preferred_element_type=jnp.float32
-    )
-    high_part = with_layout_constraint(
+    quarter = split // 2
+    blocks_half = other.shape[0] // 2
+    first_part = with_layout_constraint(
         lax.all_gather(
-            jnp.concatenate([in_order[:, split:], low_local], 1), "tensor", axis=0, tiled=True
+            jnp.concatenate([in_order[:, : split + quarter], low_local], 1),
+            "tensor", axis=0, tiled=True,
         ),
         row_major,
     )
+    folded_all = jnp.dot(
+        first_part[:, :split], mine.reshape(split, 3 * head_cols),
+        preferred_element_type=jnp.float32,
+    ) + jnp.dot(
+        first_part[:, split : split + quarter],
+        other[:blocks_half].reshape(quarter, 3 * head_cols),
+        preferred_element_type=jnp.float32,
+    )
+    last_part = with_layout_constraint(
+        lax.all_gather(in_order[:, split + quarter :], "tensor", axis=0, tiled=True), row_major
+    )
     folded_all = folded_all + jnp.dot(
-        high_part[:, :split], other.reshape(split, 3 * head_cols), preferred_element_type=jnp.float32
-    )
-    adapter_update = high_part[:, split:]
+        last_part, other[blocks_half:].reshape(quarter, 3 * head_cols),
+        preferred_element_type=jnp.float32,
+    )
+    adapter_update = first_part[:, split + quarter :]
     folded = [folded_all[:, k * head_cols : (k + 1) * head_cols] for k in range(3)]
     projected = []
     for adapter_selector in range(3):

time: 385 us -> 380 us (0.987)
  waiting for transfers between devices: 200 us -> 193 us
    all_gather x2, waiting for transfers between devices: 16.7 us -> 1.28 us  [the longest x1 1.28 us: body(): lax.all_gather(in_order[:, split + quarter:], 'tensor', axis=0, tiled=True)]
    slice x1 -> x3, local copies, waits for them, and re-layouts: 1.04 us -> 10.6 us  [the longest x1 8.66 us: body(): other[:blocks_half].reshape(quarter, 3 * head_cols)]
    ppermute x1, waiting for transfers between devices: 13.9 us -> 18.9 us  [gather_weights(): lax.ppermute(from_prev[0], 'dp', to_next)]
    dot_general x2 -> x3, matrix products: 35.1 us -> 39.7 us  [the longest x1 17.2 us: body(): jnp.dot(first_part[:, :split], mine.reshape(split, 3 * head_cols), prefer...]
    unnamed x47 -> x37, local copies, waits for them, and re-layouts: 16.8 us -> 13.3 us
  transfers between devices with their start and end apart: 11 -> 11, of which waited for: 7 -> 7; matrix products, arithmetic and copies ran while one was open for 18% -> 21% of each run, Pallas kernels for 0% -> 0%
where the time goes in v10:
time: 380 us
  waiting for transfers between devices  193 us (51%)
  matrix products  72.6 us (19%)
  local copies, waits for them, and re-layouts  56.9 us (15%)
  starting transfers between devices  29.2 us (8%)
  between operations  14.8 us (4%)
  other arithmetic  13.3 us (4%)
    ppermute x1, waiting for transfers between devices, gather_weights(): from_prev = lax.ppermute(pair, 'dp', to_next)  50 us
    ppermute x1, waiting for transfers between devices, gather_weights(): pair = jnp.stack([weight_shard, lax.ppermute(weight_shard, 'dp', to_yh)])  48.6 us
    reduce_scatter x1, waiting for transfers between devices, body(): lax.psum_scatter(jnp.dot(attended, output_projection_weight, preferred_el...  34.5 us
    all_to_all x1, waiting for transfers between devices, body(): lax.all_to_all(taken, 'dp', split_axis=0, concat_axis=0, tiled=True)  28.1 us
    ppermute x1, waiting for transfers between devices, gather_weights(): lax.ppermute(from_prev[0], 'dp', to_next)  18.9 us
    dot_general x1, matrix products, body(): jnp.dot(first_part[:, :split], mine.reshape(split, 3 * head_cols), prefer...  17.2 us
    unnamed x37, local copies, waits for them, and re-layouts  13.3 us
    dot_general x1, matrix products, body(): jnp.dot(last_part, other[blocks_half:].reshape(quarter, 3 * head_cols), p...  12.5 us
  transfers between devices with their start and end apart: 11, of which 7 were waited for; matrix products, arithmetic and copies ran while one was open for 21% of the time, Pallas kernels for 0%

profile of v10, /device:TPU:1, one launch (start us, length us, event | category | flops | bytes accessed | tf_op | source)
XLA Modules:
  0.0 379.6 jit_solution(16314892431239927340)
XLA Ops:
  7.3 2.4 copy.27
  9.6 1.9 fusion.7
  11.5 2.2 copy.26
  13.9 4.4 %fusion.33 = bf16[128,384]{1,0:T(8,128)(2,1)S(1)} fusion(bf16[7168,384]{1,0:T(8,128)(2,1)} %param.21, f32[7168]{0:T(1024)S(1)} %copy-done.9, f32[128]{0:T(128)S(1)} %add_rsqrt_fusion, bf16[128,3584]{1,0:T(8,128)(2,1)} %param.16, bf16[128,3584]{1,0:T(8,128)(2,1)} %param.15), kind=kOutput, calls=%fused_computation.57 | convolution fusion | flops 711114752 | bytes 7467520 | tf_op jit(solution)/shard_map/dot_general | solution.py:108
  18.4 2.5 multiply_convert_fusion
  20.8 3.5 gather_fusion
  24.4 3.9 %copy.28 = bf16[128,7168]{1,0:T(8,128)(2,1)} copy(bf16[128,7168]{0,1:T(8,128)(2,1)} %bitcast.71) | data formatting | bytes 3670016 | tf_op jit(solution)/shard_map/jit(_take)/gather | solution.py:104
  28.4 1.7 broadcast_select_fusion
  30.1 1.2 copy-done.4
  31.4 1.3 pad_maximum_fusion.3
  32.8 3.5 concatenate.28
  36.3 3.7 collective-permute-start
  40.1 48.6 %collective-permute-done = bf16[448,1344]{1,0:T(8,128)(2,1)S(1)} collective-permute-done((bf16[448,1344]{1,0:T(8,128)(2,1)}, bf16[448,1344]{1,0:T(8,128)(2,1)S(1)}, u32[]{:S(2)}, u32[]{:S(2)}) %collective-permute-start) | collective-permute-done | bytes 1204256 | tf_op jit(solution)/shard_map/ppermute | solution.py:64
  88.7 1.6 pad_maximum_fusion
  90.3 1.1 collective-permute-start.1
  91.4 1.6 collective-permute-start.2
  93.0 1.2 constant_dynamic-update-slice_fusion.3
  94.2 50.0 %collective-permute-done.1 = bf16[2,448,1344]{2,1,0:T(8,128)(2,1)S(1)} collective-permute-done((bf16[2,448,1344]{2,1,0:T(8,128)(2,1)S(1)}, bf16[2,448,1344]{2,1,0:T(8,128)(2,1)S(1)}, u32[]{:S(2)}, u32[]{:S(2)}) %collective-permute-start.1) | collective-permute-done | bytes 2408480 | tf_op jit(solution)/shard_map/ppermute | solution.py:65
  144.5 2.7 collective-permute-start.4
  147.2 1.1 constant_dynamic-update-slice_fusion.2
  148.4 1.6 constant_dynamic-update-slice_fusion.1
  150.0 1.7 constant_dynamic-update-slice_fusion
  151.6 18.9 %collective-permute-done.3 = bf16[448,1344]{1,0:T(8,128)(2,1)S(1)} collective-permute-done((bf16[448,1344]{1,0:T(8,128)(2,1)S(1)}, bf16[448,1344]{1,0:T(8,128)(2,1)S(1)}, u32[]{:S(2)}, u32[]{:S(2)}) %collective-permute-start.3) | collective-permute-done | bytes 1204256 | tf_op jit(solution)/shard_map/ppermute | solution.py:68
  170.5 1.1 bitcast_dynamic-update-slice_fusion.1
  171.6 1.1 bitcast_dynamic-update-slice_fusion
  172.8 5.3 %collective-permute-start.5 = (bf16[8,448,1344]{2,1,0:T(8,128)(2,1)}, bf16[8,448,1344]{2,1,0:T(8,128)(2,1)}, u32[]{:S(2)}, u32[]{:S(2)}) collective-permute-start(bf16[8,448,1344]{2,1,0:T(8,128)(2,1)} %bitcast_dynamic-update-slice_fusion), channel_id=1, source_target_pairs={{0,8},{8,0},{16,24},{24,16},{32,40},{40,32},{48,56},{56,48},{64,72... | collective-permute-start | bytes 28901384 | tf_op jit(solution)/shard_map/ppermute | solution.py:71
  178.0 1.8 slice.138
  180.7 0.3 and_and_fusion.1
  181.0 1.2 and_and_fusion
  182.2 11.4 %collective-permute-done.5 = bf16[8,448,1344]{2,1,0:T(8,128)(2,1)} collective-permute-done((bf16[8,448,1344]{2,1,0:T(8,128)(2,1)}, bf16[8,448,1344]{2,1,0:T(8,128)(2,1)}, u32[]{:S(2)}, u32[]{:S(2)}) %collective-permute-start.5) | collective-permute-done | bytes 9633824 | tf_op jit(solution)/shard_map/ppermute | solution.py:71
  193.6 8.7 %fusion.76 = (bf16[4,448,1344]{2,1,0:T(8,128)(2,1)}, bf16[4,448,1344]{2,1,0:T(8,128)(2,1)}) fusion(bf16[8,448,1344]{2,1,0:T(8,128)(2,1)} %collective-permute-done.5), kind=kLoop, calls=%fused_computation.114 | loop fusion | bytes 19267584 | tf_op jit(solution)/shard_map/slice | solution.py:126
  202.3 10.1 %fusion.10 = f32[1024,1344]{0,1:T(8,128)} fusion(bf16[1792,1344]{1,0:T(8,128)(2,1)} %bitcast.73, bf16[1024,5760]{1,0:T(8,128)(2,1)} %all-gather.3.cloned.1.call-done), kind=kOutput, calls=%fused_computation.16 | convolution fusion | flops 4932501504 | bytes 14221312 | tf_op jit(solution)/shard_map/dot_general | solution.py:124
  212.4 17.2 %fusion.2 = f32[1024,1344]{0,1:T(8,128)} fusion(bf16[3584,1344]{1,0:T(8,128)(2,1)} %bitcast.11, bf16[1024,5760]{1,0:T(8,128)(2,1)} %all-gather.3.cloned.1.call-done), kind=kOutput, calls=%fused_computation.5 | convolution fusion | flops 9865003008 | bytes 22937600 | tf_op jit(solution)/shard_map/dot_general | solution.py:121
  229.5 1.3 all-gather.5.cloned.1.call-done
  230.8 12.5 %add_add_fusion = f32[1024,1344]{0,1:T(8,128)S(1)} fusion(f32[1024,1344]{0,1:T(8,128)} %fusion.2, f32[1024,1344]{0,1:T(8,128)} %fusion.10, bf16[1024,1792]{1,0:T(8,128)(2,1)} %all-gather.5.cloned.1.call-done, bf16[1792,1344]{1,0:T(8,128)(2,1)} %bitcast.72), kind=kOutput, calls=%fused_computation.7 | convolution fusion | flops 4935254016 | bytes 25001984 | tf_op jit(solution)/shard_map/dot_general | solution.py:132
  243.3 1.4 fusion.20
  244.7 0.9 slice.142
  245.6 1.3 fusion.18
  246.9 1.0 slice.151
  247.9 0.8 slice.148
  248.7 1.3 fusion.19
  250.0 1.0 fusion.77
  251.0 4.4 %fusion.79 = (f32[2,512]{1,0:T(2,128)S(1)}, f32[2,512,768]{2,1,0:T(8,128)}) fusion(pred[512,768]{1,0:T(8,128)(4,1)} %and_and_fusion, bf16[512,2,224]{0,2,1:T(8,128)(2,1)} %bitcast.80, bf16[768,2,224]{0,2,1:T(8,128)(2,1)} %bitcast.78), kind=kOutput, calls=%fused_computation.117 | convolution fusion | flops 355468032 | bytes 4689920 | tf_op jit(solution)/shard_map/sub | solution.py:39
  255.4 3.5 fusion.80
  258.9 2.3 fusion.30
  261.2 0.5 slice-done
  261.7 0.8 fusion.32
  262.5 6.1 %convolution_convert_fusion.1 = bf16[1024,3584]{1,0:T(8,128)(2,1)} fusion(bf16[448,3584]{1,0:T(8,128)(2,1)S(1)} %copy-done, bf16[512,448]{0,1:T(8,128)(2,1)S(1)} %bitcast.85, bf16[512,448]{0,1:T(8,128)(2,1)S(1)} %bitcast.84), kind=kOutput, calls=%fused_computation.4 | convolution fusion | flops 3293839360 | bytes 11468800 | tf_op jit(solution)/shard_map/dot_general | solution.py:202
  268.6 0.6 copy-done.10
  269.2 0.6 broadcast_in_dim.107
  269.8 7.3 %all-to-all-start = ((s32[16,1,4]{2,1,0:T(1,128)}), s32[16,1,4]{2,1,0:T(1,128)S(1)}, u32[]{:S(2)}, u32[]{:S(2)}) async-start(s32[16,1,4]{2,1,0:T(1,128)} %broadcast_in_dim.107), calls=%async_computation.1 | async-start | bytes 16384 | tf_op jit(solution)/shard_map/all_to_all | solution.py:178
  277.1 0.1 convert_reduce_fusion
  277.2 0.2 reduce-window.8
  277.8 1.7 pad_maximum_fusion.2
  279.5 3.8 %fusion.23 = bf16[1024,896]{1,0:T(8,128)(2,1)} fusion(bf16[1024,896]{0,1:T(8,128)(2,1)S(1)} %bitcast.77, s32[1024]{0:T(1024)S(1)} %add.125, pred[1024]{0:T(1024)(128)(4,1)S(1)} %lt.81), kind=kOutput, calls=%fused_computation.42 | convolution fusion | flops 1882062848 | bytes 3675136 | tf_op jit(solution)/shard_map/dot_general | solution.py:173
  283.3 4.4 %reshape.336 = bf16[16,4,14336]{2,1,0:T(4,128)(2,1)} reshape(bf16[1024,896]{1,0:T(8,128)(2,1)} %fusion.23) | data formatting | bytes 3670016 | tf_op jit(solution)/shard_map/reshape | solution.py:174
  287.7 7.2 %all-to-all-start.1 = ((bf16[16,4,14336]{2,1,0:T(4,128)(2,1)}), bf16[16,4,14336]{2,1,0:T(4,128)(2,1)}, u32[]{:S(2)}, u32[]{:S(2)}) async-start(bf16[16,4,14336]{2,1,0:T(4,128)(2,1)} %reshape.336), calls=%async_computation.2 | async-start | bytes 3670016 | tf_op jit(solution)/shard_map/all_to_all | solution.py:177
  294.9 0.5 broadcast.205
  295.4 0.7 reduce.3
  296.2 28.1 %all-to-all-done.1 = bf16[16,4,14336]{2,1,0:T(4,128)(2,1)} async-done(((bf16[16,4,14336]{2,1,0:T(4,128)(2,1)}), bf16[16,4,14336]{2,1,0:T(4,128)(2,1)}, u32[]{:S(2)}, u32[]{:S(2)}) %all-to-all-start.1) | async-done | bytes 1835040 | tf_op jit(solution)/shard_map/all_to_all | solution.py:177
  324.3 3.9 %reshape.337 = bf16[64,14336]{1,0:T(8,128)(2,1)} reshape(bf16[16,4,14336]{2,1,0:T(4,128)(2,1)} %all-to-all-done.1) | data formatting | bytes 3670016 | tf_op jit(solution)/shard_map/reshape | solution.py:184
  328.2 3.6 convolution_convert_fusion
  331.8 6.8 %reshape.338 = bf16[64,16,2,448]{3,2,1,0:T(2,128)(2,1)} reshape(bf16[64,14336]{1,0:T(8,128)(2,1)} %convolution_convert_fusion) | data formatting | bytes 3670016 | tf_op jit(solution)/shard_map/reshape | solution.py:188
  338.6 34.5 %reduce-scatter.2.cloned.1.call-done = bf16[128,3584]{1,0:T(8,128)(2,1)} async-done(((bf16[1024,3584]{1,0:T(8,128)(2,1)}), bf16[128,3584]{1,0:T(8,128)(2,1)}) %reduce-scatter.2.cloned.1.call-update) | async-done | bytes 917520 | tf_op jit(solution)/shard_map/reduce_scatter | solution.py:201
  (68 shorter events, 1.4 us)
Async XLA Ops:
  7.2 255.3 %copy-start = (bf16[448,3584]{1,0:T(8,128)(2,1)S(1)}, bf16[448,3584]{1,0:T(8,128)(2,1)}, u32[]{:S(2)}) copy-start(bf16[448,3584]{1,0:T(8,128)(2,1)} %param.23) | copy-start | bytes 9633796
  7.2 6.7 %copy-start.11 = (s32[16]{0:T(128)S(1)}, s32[16]{0:T(128)}, u32[]{:S(2)}) copy-start(s32[16]{0:T(128)} %constant.102.clone) | copy-start | bytes 196
  7.2 6.6 %copy-start.12 = (s32[16]{0:T(128)S(1)}, s32[16]{0:T(128)}, u32[]{:S(2)}) copy-start(s32[16]{0:T(128)} %constant.101.clone) | copy-start | bytes 196
  7.2 6.6 %copy-start.13 = (s32[16]{0:T(128)S(1)}, s32[16]{0:T(128)}, u32[]{:S(2)}) copy-start(s32[16]{0:T(128)} %constant.100.clone) | copy-start | bytes 196
  7.2 6.5 %copy-start.9 = (f32[7168]{0:T(1024)S(1)}, f32[7168]{0:T(1024)}, u32[]{:S(2)}) copy-start(f32[7168]{0:T(1024)} %param.17) | copy-start | bytes 86020
  7.2 195.0 %all-gather.3.cloned.1.call-start = ((), (), s32[]{:S(2)}) async-start(), calls=%async_computation.3 | async-start | bytes 13271040 | tf_op jit(solution)/shard_map/all_gather | solution.py:115
  13.9 4.5 %copy-start.5 = (bf16[128,3584]{0,1:T(8,128)(2,1)S(1)}, bf16[128,3584]{0,1:T(8,128)(2,1)}, u32[]{:S(2)}) copy-start(bf16[128,3584]{0,1:T(8,128)(2,1)} %copy.27) | copy-start | bytes 2752516
  13.9 4.5 %copy-start.6 = (bf16[128,3584]{0,1:T(8,128)(2,1)S(1)}, bf16[128,3584]{0,1:T(8,128)(2,1)}, u32[]{:S(2)}) copy-start(bf16[128,3584]{0,1:T(8,128)(2,1)} %copy.26) | copy-start | bytes 2752516
  30.1 1.2 copy-start.4
  32.7 198.1 %all-gather.5.cloned.1.call-start = ((), (), s32[]{:S(2)}) async-start(), calls=%async_computation.4 | async-start | bytes 4128768 | tf_op jit(solution)/shard_map/all_gather | solution.py:130
  36.3 56.7 %copy-start.1 = (bf16[448,1344]{1,0:T(8,128)(2,1)S(1)}, bf16[448,1344]{1,0:T(8,128)(2,1)}, u32[]{:S(2)}) copy-start(bf16[448,1344]{1,0:T(8,128)(2,1)} %concatenate.28) | copy-start | bytes 3612676
  36.3 52.4 %collective-permute-start = (bf16[448,1344]{1,0:T(8,128)(2,1)}, bf16[448,1344]{1,0:T(8,128)(2,1)S(1)}, u32[]{:S(2)}, u32[]{:S(2)}) collective-permute-start(bf16[448,1344]{1,0:T(8,128)(2,1)} %concatenate.28), channel_id=1, source_target_pairs={{0,16},{8,24},{16,0},{24,8},{32,48},{40,56},{48,32},{56,40},{64,80... | collective-permute-start | bytes 3612680 | tf_op jit(solution)/shard_map/ppermute | solution.py:64
  90.3 53.9 %collective-permute-start.1 = (bf16[2,448,1344]{2,1,0:T(8,128)(2,1)S(1)}, bf16[2,448,1344]{2,1,0:T(8,128)(2,1)S(1)}, u32[]{:S(2)}, u32[]{:S(2)}) collective-permute-start(bf16[2,448,1344]{2,1,0:T(8,128)(2,1)S(1)} %pad_maximum_fusion), channel_id=1, source_target_pairs={{0,32},{8,40},{16,48},{24,56},{32,64},{40,72},{48,80},{56,88},{64,... | collective-permute-start | bytes 7225352 | tf_op jit(solution)/shard_map/ppermute | solution.py:65
  91.4 53.0 %collective-permute-start.2 = (bf16[2,448,1344]{2,1,0:T(8,128)(2,1)S(1)}, bf16[2,448,1344]{2,1,0:T(8,128)(2,1)S(1)}, u32[]{:S(2)}, u32[]{:S(2)}) collective-permute-start(bf16[2,448,1344]{2,1,0:T(8,128)(2,1)S(1)} %pad_maximum_fusion), channel_id=1, source_target_pairs={{0,96},{8,104},{16,112},{24,120},{32,0},{40,8},{48,16},{56,24},{64... | collective-permute-start | bytes 7225352 | tf_op jit(solution)/shard_map/ppermute | solution.py:66
  144.3 26.2 %collective-permute-start.3 = (bf16[448,1344]{1,0:T(8,128)(2,1)S(1)}, bf16[448,1344]{1,0:T(8,128)(2,1)S(1)}, u32[]{:S(2)}, u32[]{:S(2)}) collective-permute-start(bf16[448,1344]{1,0:T(8,128)(2,1)S(1)} %slice_bitcast_fusion.1), channel_id=1, source_target_pairs={{0,32},{8,40},{16,48},{24,56},{32,64},{40,72},{48,80},{56,88},{64,... | collective-permute-start | bytes 3612680 | tf_op jit(solution)/shard_map/ppermute | solution.py:68
  144.5 27.1 %collective-permute-start.4 = (bf16[448,1344]{1,0:T(8,128)(2,1)S(1)}, bf16[448,1344]{1,0:T(8,128)(2,1)S(1)}, u32[]{:S(2)}, u32[]{:S(2)}) collective-permute-start(bf16[448,1344]{1,0:T(8,128)(2,1)S(1)} %slice_bitcast_fusion), channel_id=1, source_target_pairs={{0,96},{8,104},{16,112},{24,120},{32,0},{40,8},{48,16},{56,24},{64... | collective-permute-start | bytes 3612680 | tf_op jit(solution)/shard_map/ppermute | solution.py:68
  151.6 28.3 %copy-start.8 = (s32[1024]{0:T(1024)S(1)}, s32[1024]{0:T(1024)}, u32[]{:S(2)}) copy-start(s32[1024]{0:T(1024)} %param.24) | copy-start | bytes 12292
  172.8 20.9 %collective-permute-start.5 = (bf16[8,448,1344]{2,1,0:T(8,128)(2,1)}, bf16[8,448,1344]{2,1,0:T(8,128)(2,1)}, u32[]{:S(2)}, u32[]{:S(2)}) collective-permute-start(bf16[8,448,1344]{2,1,0:T(8,128)(2,1)} %bitcast_dynamic-update-slice_fusion), channel_id=1, source_target_pairs={{0,8},{8,0},{16,24},{24,16},{32,40},{40,32},{48,56},{56,48},{64,72... | collective-permute-start | bytes 28901384 | tf_op jit(solution)/shard_map/ppermute | solution.py:71
  179.9 193.2 %reduce-scatter.2.cloned.1.call-start = ((), (), s32[]{:S(2)}) async-start(), calls=%async_computation.5 | async-start | bytes 8257536 | tf_op jit(solution)/shard_map/reduce_scatter | solution.py:201
  230.8 12.5 %copy-start.7 = (bf16[3,128,448]{1,2,0:T(8,128)(2,1)S(1)}, bf16[3,128,448]{1,2,0:T(8,128)(2,1)}, u32[]{:S(2)}) copy-start(bf16[3,128,448]{1,2,0:T(8,128)(2,1)} %param.22) | copy-start | bytes 1032196
  244.7 3.2 copy-start.2
  246.9 4.1 %copy-start.3 = (bf16[1024,448]{0,1:T(8,128)(2,1)}, bf16[1024,448]{0,1:T(8,128)(2,1)S(1)}, u32[]{:S(2)}) copy-start(bf16[1024,448]{0,1:T(8,128)(2,1)S(1)} %fusion.18) | copy-start | bytes 2752516
  258.9 2.8 slice-start
  258.9 2.8 copy-start.14
  268.6 0.7 copy-start.10
  269.8 17.9 %all-to-all-start = ((s32[16,1,4]{2,1,0:T(1,128)}), s32[16,1,4]{2,1,0:T(1,128)S(1)}, u32[]{:S(2)}, u32[]{:S(2)}) async-start(s32[16,1,4]{2,1,0:T(1,128)} %broadcast_in_dim.107), calls=%async_computation.1 | async-start | bytes 16384 | tf_op jit(solution)/shard_map/all_to_all | solution.py:178
  287.7 36.6 %all-to-all-start.1 = ((bf16[16,4,14336]{2,1,0:T(4,128)(2,1)}), bf16[16,4,14336]{2,1,0:T(4,128)(2,1)}, u32[]{:S(2)}, u32[]{:S(2)}) async-start(bf16[16,4,14336]{2,1,0:T(4,128)(2,1)} %reshape.336), calls=%async_computation.2 | async-start | bytes 3670016 | tf_op jit(solution)/shard_map/all_to_all | solution.py:177
Sparse Core Ops, SparseCore 0:
  32.9 150.5 all-gather.2
  185.7 45.0 all-gather.4
  268.7 104.3 reduce-scatter.1

commit v11 on v10

--- a/solution.py
+++ b/solution.py
@@ -109,8 +109,8 @@
         normalized_hidden, adapter_down_maps, preferred_element_type=jnp.float32
     ).astype(jnp.bfloat16)
     row_major = Layout((0, 1))
-    quarter = split // 2
-    blocks_half = other.shape[0] // 2
+    blocks_half = other.shape[0] - 2
+    quarter = blocks_half * block_rows
     first_part = with_layout_constraint(
         lax.all_gather(
             jnp.concatenate([in_order[:, : split + quarter], low_local], 1),
@@ -130,7 +130,7 @@
         lax.all_gather(in_order[:, split + quarter :], "tensor", axis=0, tiled=True), row_major
     )
     folded_all = folded_all + jnp.dot(
-        last_part, other[blocks_half:].reshape(quarter, 3 * head_cols),
+        last_part, other[blocks_half:].reshape(split - quarter, 3 * head_cols),
         preferred_element_type=jnp.float32,
     )
     adapter_update = first_part[:, split + quarter :]

time: 380 us -> 385 us (1.013)
  starting transfers between devices: 29.2 us -> 35.4 us
    all_to_all x1, starting transfers between devices: 7.26 us -> 13.3 us  [body(): lax.all_to_all(row_send, 'dp', split_axis=0, concat_axis=0, tiled=True)]
    dot_general x1, matrix products: 12.5 us -> 8.59 us  [body(): jnp.dot(last_part, other[blocks_half:].reshape(split - quarter, 3 * head_...]
  transfers between devices with their start and end apart: 11 -> 11, of which waited for: 7 -> 7; matrix products, arithmetic and copies ran while one was open for 21% -> 22% of each run, Pallas kernels for 0% -> 0%
where the time goes in v11:
time: 385 us; the launch traced here: 384 us
  waiting for transfers between devices  190 us (49%)
  matrix products  72.5 us (19%)
  local copies, waits for them, and re-layouts  58.3 us (15%)
  starting transfers between devices  35.4 us (9%)
  between operations  14.8 us (4%)
  other arithmetic  13.5 us (4%)
    ppermute x1, waiting for transfers between devices, gather_weights(): from_prev = lax.ppermute(pair, 'dp', to_next)  50 us
    ppermute x1, waiting for transfers between devices, gather_weights(): pair = jnp.stack([weight_shard, lax.ppermute(weight_shard, 'dp', to_yh)])  48.6 us
    reduce_scatter x1, waiting for transfers between devices, body(): lax.psum_scatter(jnp.dot(attended, output_projection_weight, preferred_el...  32.2 us
    all_to_all x1, waiting for transfers between devices, body(): lax.all_to_all(taken, 'dp', split_axis=0, concat_axis=0, tiled=True)  28.1 us
    ppermute x1, waiting for transfers between devices, gather_weights(): lax.ppermute(from_prev[0], 'dp', to_next)  18.7 us
    dot_general x1, matrix products, body(): jnp.dot(first_part[:, :split], mine.reshape(split, 3 * head_cols), prefer...  17.1 us
    dot_general x1, matrix products, body(): jnp.dot(first_part[:, split:split + quarter], other[:blocks_half].reshape...  13.8 us
    unnamed x37, local copies, waits for them, and re-layouts  13.3 us
  transfers between devices with their start and end apart: 11, of which 7 were waited for; matrix products, arithmetic and copies ran while one was open for 22% of the time, Pallas kernels for 0%

profile of v11, /device:TPU:1, one launch (start us, length us, event | category | flops | bytes accessed | tf_op | source)
XLA Modules:
  0.0 384.0 jit_solution(13149088883121099219)
XLA Ops:
  7.3 2.4 copy.27
  9.6 1.9 fusion.9
  11.5 2.2 copy.26
  13.9 4.4 %fusion.33 = bf16[128,384]{1,0:T(8,128)(2,1)S(1)} fusion(bf16[7168,384]{1,0:T(8,128)(2,1)} %param.21, f32[7168]{0:T(1024)S(1)} %copy-done.9, f32[128]{0:T(128)S(1)} %add_rsqrt_fusion, bf16[128,3584]{1,0:T(8,128)(2,1)} %param.16, bf16[128,3584]{1,0:T(8,128)(2,1)} %param.15), kind=kOutput, calls=%fused_computation.57 | convolution fusion | flops 711114752 | bytes 7467520 | tf_op jit(solution)/shard_map/dot_general | solution.py:108
  18.4 2.5 multiply_convert_fusion
  20.8 3.6 gather_fusion
  24.4 3.9 %copy.28 = bf16[128,7168]{1,0:T(8,128)(2,1)} copy(bf16[128,7168]{0,1:T(8,128)(2,1)} %bitcast.71) | data formatting | bytes 3670016 | tf_op jit(solution)/shard_map/jit(_take)/gather | solution.py:104
  28.4 1.7 broadcast_select_fusion
  30.1 1.2 copy-done.4
  31.5 1.3 pad_maximum_fusion.3
  32.9 3.5 concatenate.28
  36.4 3.7 collective-permute-start
  40.1 48.6 %collective-permute-done = bf16[448,1344]{1,0:T(8,128)(2,1)S(1)} collective-permute-done((bf16[448,1344]{1,0:T(8,128)(2,1)}, bf16[448,1344]{1,0:T(8,128)(2,1)S(1)}, u32[]{:S(2)}, u32[]{:S(2)}) %collective-permute-start) | collective-permute-done | bytes 1204256 | tf_op jit(solution)/shard_map/ppermute | solution.py:64
  88.8 1.7 pad_maximum_fusion
  90.4 1.1 collective-permute-start.1
  91.6 1.6 collective-permute-start.2
  93.2 1.2 constant_dynamic-update-slice_fusion.3
  94.3 50.0 %collective-permute-done.1 = bf16[2,448,1344]{2,1,0:T(8,128)(2,1)S(1)} collective-permute-done((bf16[2,448,1344]{2,1,0:T(8,128)(2,1)S(1)}, bf16[2,448,1344]{2,1,0:T(8,128)(2,1)S(1)}, u32[]{:S(2)}, u32[]{:S(2)}) %collective-permute-start.1) | collective-permute-done | bytes 2408480 | tf_op jit(solution)/shard_map/ppermute | solution.py:65
  144.6 2.7 collective-permute-start.4
  147.4 1.2 constant_dynamic-update-slice_fusion.2
  148.6 1.6 constant_dynamic-update-slice_fusion.1
  150.2 1.7 constant_dynamic-update-slice_fusion
  151.9 18.7 %collective-permute-done.3 = bf16[448,1344]{1,0:T(8,128)(2,1)S(1)} collective-permute-done((bf16[448,1344]{1,0:T(8,128)(2,1)S(1)}, bf16[448,1344]{1,0:T(8,128)(2,1)S(1)}, u32[]{:S(2)}, u32[]{:S(2)}) %collective-permute-start.3) | collective-permute-done | bytes 1204256 | tf_op jit(solution)/shard_map/ppermute | solution.py:68
  170.6 1.2 bitcast_dynamic-update-slice_fusion.1
  171.8 1.2 bitcast_dynamic-update-slice_fusion
  173.0 5.3 %collective-permute-start.5 = (bf16[8,448,1344]{2,1,0:T(8,128)(2,1)}, bf16[8,448,1344]{2,1,0:T(8,128)(2,1)}, u32[]{:S(2)}, u32[]{:S(2)}) collective-permute-start(bf16[8,448,1344]{2,1,0:T(8,128)(2,1)} %bitcast_dynamic-update-slice_fusion), channel_id=1, source_target_pairs={{0,8},{8,0},{16,24},{24,16},{32,40},{40,32},{48,56},{56,48},{64,72... | collective-permute-start | bytes 28901384 | tf_op jit(solution)/shard_map/ppermute | solution.py:71
  178.3 1.7 slice.138
  179.9 0.2 reduce-scatter.2.cloned.1.call-start
  180.9 0.3 and_and_fusion.1
  181.3 1.2 and_and_fusion
  182.4 11.4 %collective-permute-done.5 = bf16[8,448,1344]{2,1,0:T(8,128)(2,1)} collective-permute-done((bf16[8,448,1344]{2,1,0:T(8,128)(2,1)}, bf16[8,448,1344]{2,1,0:T(8,128)(2,1)}, u32[]{:S(2)}, u32[]{:S(2)}) %collective-permute-start.5) | collective-permute-done | bytes 9633824 | tf_op jit(solution)/shard_map/ppermute | solution.py:71
  193.8 6.6 %slice.137 = bf16[6,448,1344]{2,1,0:T(8,128)(2,1)} slice(bf16[8,448,1344]{2,1,0:T(8,128)(2,1)} %collective-permute-done.5), slice={[0:6], [0:448], [0:1344]} | slice | bytes 14450688 | tf_op jit(solution)/shard_map/slice | solution.py:126
  200.5 3.4 slice.139
  203.9 13.8 %fusion.4 = f32[1024,1344]{0,1:T(8,128)} fusion(bf16[2688,1344]{1,0:T(8,128)(2,1)} %bitcast.72, bf16[1024,6656]{1,0:T(8,128)(2,1)} %all-gather.3.cloned.1.call-done), kind=kOutput, calls=%fused_computation.7 | convolution fusion | flops 7398752256 | bytes 18579456 | tf_op jit(solution)/shard_map/dot_general | solution.py:124
  217.7 17.1 %fusion.2 = f32[1024,1344]{0,1:T(8,128)} fusion(bf16[3584,1344]{1,0:T(8,128)(2,1)} %bitcast.11, bf16[1024,6656]{1,0:T(8,128)(2,1)} %all-gather.3.cloned.1.call-done), kind=kOutput, calls=%fused_computation.5 | convolution fusion | flops 9865003008 | bytes 22937600 | tf_op jit(solution)/shard_map/dot_general | solution.py:121
  234.8 0.5 all-gather.5.cloned.1.call-done
  235.3 8.6 %add_add_fusion = f32[1024,1344]{0,1:T(8,128)S(1)} fusion(f32[1024,1344]{0,1:T(8,128)} %fusion.2, f32[1024,1344]{0,1:T(8,128)} %fusion.4, bf16[1024,896]{1,0:T(8,128)(2,1)} %all-gather.5.cloned.1.call-done, bf16[896,1344]{1,0:T(8,128)(2,1)} %bitcast.76), kind=kOutput, calls=%fused_computation.9 | convolution fusion | flops 2469003264 | bytes 20758528 | tf_op jit(solution)/shard_map/dot_general | solution.py:132
  243.9 1.4 fusion.20
  245.3 0.9 slice.142
  246.1 1.3 fusion.18
  247.5 1.0 slice.151
  248.5 0.8 slice.148
  249.3 1.3 fusion.19
  250.7 1.0 fusion.76
  251.7 4.4 %fusion.78 = (f32[2,512]{1,0:T(2,128)S(1)}, f32[2,512,768]{2,1,0:T(8,128)}) fusion(pred[512,768]{1,0:T(8,128)(4,1)} %and_and_fusion, bf16[512,2,224]{0,2,1:T(8,128)(2,1)} %bitcast.80, bf16[768,2,224]{0,2,1:T(8,128)(2,1)} %bitcast.78), kind=kOutput, calls=%fused_computation.116 | convolution fusion | flops 355468032 | bytes 4689920 | tf_op jit(solution)/shard_map/sub | solution.py:39
  256.1 3.5 fusion.79
  259.5 2.3 fusion.30
  261.8 0.5 slice-done
  262.3 0.8 fusion.32
  263.1 6.1 %convolution_convert_fusion.1 = bf16[1024,3584]{1,0:T(8,128)(2,1)} fusion(bf16[448,3584]{1,0:T(8,128)(2,1)S(1)} %copy-done, bf16[512,448]{0,1:T(8,128)(2,1)S(1)} %bitcast.85, bf16[512,448]{0,1:T(8,128)(2,1)S(1)} %bitcast.84), kind=kOutput, calls=%fused_computation.4 | convolution fusion | flops 3293839360 | bytes 11468800 | tf_op jit(solution)/shard_map/dot_general | solution.py:202
  269.3 0.6 copy-done.10
  269.9 0.6 broadcast_in_dim.107
  270.5 13.3 %all-to-all-start = ((s32[16,1,4]{2,1,0:T(1,128)}), s32[16,1,4]{2,1,0:T(1,128)S(1)}, u32[]{:S(2)}, u32[]{:S(2)}) async-start(s32[16,1,4]{2,1,0:T(1,128)} %broadcast_in_dim.107), calls=%async_computation.1 | async-start | bytes 16384 | tf_op jit(solution)/shard_map/all_to_all | solution.py:178
  284.5 1.6 pad_maximum_fusion.2
  286.1 3.8 fusion.23
  290.0 4.4 %reshape.336 = bf16[16,4,14336]{2,1,0:T(4,128)(2,1)} reshape(bf16[1024,896]{1,0:T(8,128)(2,1)} %fusion.23) | data formatting | bytes 3670016 | tf_op jit(solution)/shard_map/reshape | solution.py:174
  294.4 7.2 %all-to-all-start.1 = ((bf16[16,4,14336]{2,1,0:T(4,128)(2,1)}), bf16[16,4,14336]{2,1,0:T(4,128)(2,1)}, u32[]{:S(2)}, u32[]{:S(2)}) async-start(bf16[16,4,14336]{2,1,0:T(4,128)(2,1)} %reshape.336), calls=%async_computation.2 | async-start | bytes 3670016 | tf_op jit(solution)/shard_map/all_to_all | solution.py:177
  301.6 0.5 broadcast.205
  302.1 0.7 reduce.3
  302.9 28.1 %all-to-all-done.1 = bf16[16,4,14336]{2,1,0:T(4,128)(2,1)} async-done(((bf16[16,4,14336]{2,1,0:T(4,128)(2,1)}), bf16[16,4,14336]{2,1,0:T(4,128)(2,1)}, u32[]{:S(2)}, u32[]{:S(2)}) %all-to-all-start.1) | async-done | bytes 1835040 | tf_op jit(solution)/shard_map/all_to_all | solution.py:177
  331.0 3.9 %reshape.337 = bf16[64,14336]{1,0:T(8,128)(2,1)} reshape(bf16[16,4,14336]{2,1,0:T(4,128)(2,1)} %all-to-all-done.1) | data formatting | bytes 3670016 | tf_op jit(solution)/shard_map/reshape | solution.py:184
  334.9 3.6 convolution_convert_fusion
  338.5 6.8 %reshape.338 = bf16[64,16,2,448]{3,2,1,0:T(2,128)(2,1)} reshape(bf16[64,14336]{1,0:T(8,128)(2,1)} %convolution_convert_fusion) | data formatting | bytes 3670016 | tf_op jit(solution)/shard_map/reshape | solution.py:188
  345.3 32.2 %reduce-scatter.2.cloned.1.call-done = bf16[128,3584]{1,0:T(8,128)(2,1)} async-done(((bf16[1024,3584]{1,0:T(8,128)(2,1)}), bf16[128,3584]{1,0:T(8,128)(2,1)}) %reduce-scatter.2.cloned.1.call-update) | async-done | bytes 917520 | tf_op jit(solution)/shard_map/reduce_scatter | solution.py:201
  (69 shorter events, 1.7 us)
Async XLA Ops:
  7.2 255.9 %copy-start = (bf16[448,3584]{1,0:T(8,128)(2,1)S(1)}, bf16[448,3584]{1,0:T(8,128)(2,1)}, u32[]{:S(2)}) copy-start(bf16[448,3584]{1,0:T(8,128)(2,1)} %param.23) | copy-start | bytes 9633796
  7.2 6.7 %copy-start.11 = (s32[16]{0:T(128)S(1)}, s32[16]{0:T(128)}, u32[]{:S(2)}) copy-start(s32[16]{0:T(128)} %constant.102.clone) | copy-start | bytes 196
  7.2 6.6 %copy-start.12 = (s32[16]{0:T(128)S(1)}, s32[16]{0:T(128)}, u32[]{:S(2)}) copy-start(s32[16]{0:T(128)} %constant.101.clone) | copy-start | bytes 196
  7.2 6.6 %copy-start.13 = (s32[16]{0:T(128)S(1)}, s32[16]{0:T(128)}, u32[]{:S(2)}) copy-start(s32[16]{0:T(128)} %constant.100.clone) | copy-start | bytes 196
  7.2 6.5 %copy-start.9 = (f32[7168]{0:T(1024)S(1)}, f32[7168]{0:T(1024)}, u32[]{:S(2)}) copy-start(f32[7168]{0:T(1024)} %param.17) | copy-start | bytes 86020
  7.2 196.6 %all-gather.3.cloned.1.call-start = ((), (), s32[]{:S(2)}) async-start(), calls=%async_computation.3 | async-start | bytes 15335424 | tf_op jit(solution)/shard_map/all_gather | solution.py:115
  13.9 4.5 %copy-start.5 = (bf16[128,3584]{0,1:T(8,128)(2,1)S(1)}, bf16[128,3584]{0,1:T(8,128)(2,1)}, u32[]{:S(2)}) copy-start(bf16[128,3584]{0,1:T(8,128)(2,1)} %copy.27) | copy-start | bytes 2752516
  13.9 4.5 %copy-start.6 = (bf16[128,3584]{0,1:T(8,128)(2,1)S(1)}, bf16[128,3584]{0,1:T(8,128)(2,1)}, u32[]{:S(2)}) copy-start(bf16[128,3584]{0,1:T(8,128)(2,1)} %copy.26) | copy-start | bytes 2752516
  30.1 1.2 copy-start.4
  32.8 202.5 %all-gather.5.cloned.1.call-start = ((), (), s32[]{:S(2)}) async-start(), calls=%async_computation.4 | async-start | bytes 2064384 | tf_op jit(solution)/shard_map/all_gather | solution.py:130
  36.4 52.3 %collective-permute-start = (bf16[448,1344]{1,0:T(8,128)(2,1)}, bf16[448,1344]{1,0:T(8,128)(2,1)S(1)}, u32[]{:S(2)}, u32[]{:S(2)}) collective-permute-start(bf16[448,1344]{1,0:T(8,128)(2,1)} %concatenate.28), channel_id=1, source_target_pairs={{0,16},{8,24},{16,0},{24,8},{32,48},{40,56},{48,32},{56,40},{64,80... | collective-permute-start | bytes 3612680 | tf_op jit(solution)/shard_map/ppermute | solution.py:64
  88.8 4.4 %copy-start.1 = (bf16[448,1344]{1,0:T(8,128)(2,1)S(1)}, bf16[448,1344]{1,0:T(8,128)(2,1)}, u32[]{:S(2)}) copy-start(bf16[448,1344]{1,0:T(8,128)(2,1)} %concatenate.28) | copy-start | bytes 3612676
  90.4 53.9 %collective-permute-start.1 = (bf16[2,448,1344]{2,1,0:T(8,128)(2,1)S(1)}, bf16[2,448,1344]{2,1,0:T(8,128)(2,1)S(1)}, u32[]{:S(2)}, u32[]{:S(2)}) collective-permute-start(bf16[2,448,1344]{2,1,0:T(8,128)(2,1)S(1)} %pad_maximum_fusion), channel_id=1, source_target_pairs={{0,32},{8,40},{16,48},{24,56},{32,64},{40,72},{48,80},{56,88},{64,... | collective-permute-start | bytes 7225352 | tf_op jit(solution)/shard_map/ppermute | solution.py:65
  91.6 53.0 %collective-permute-start.2 = (bf16[2,448,1344]{2,1,0:T(8,128)(2,1)S(1)}, bf16[2,448,1344]{2,1,0:T(8,128)(2,1)S(1)}, u32[]{:S(2)}, u32[]{:S(2)}) collective-permute-start(bf16[2,448,1344]{2,1,0:T(8,128)(2,1)S(1)} %pad_maximum_fusion), channel_id=1, source_target_pairs={{0,96},{8,104},{16,112},{24,120},{32,0},{40,8},{48,16},{56,24},{64... | collective-permute-start | bytes 7225352 | tf_op jit(solution)/shard_map/ppermute | solution.py:66
  144.5 26.2 %collective-permute-start.3 = (bf16[448,1344]{1,0:T(8,128)(2,1)S(1)}, bf16[448,1344]{1,0:T(8,128)(2,1)S(1)}, u32[]{:S(2)}, u32[]{:S(2)}) collective-permute-start(bf16[448,1344]{1,0:T(8,128)(2,1)S(1)} %slice_bitcast_fusion.1), channel_id=1, source_target_pairs={{0,32},{8,40},{16,48},{24,56},{32,64},{40,72},{48,80},{56,88},{64,... | collective-permute-start | bytes 3612680 | tf_op jit(solution)/shard_map/ppermute | solution.py:68
  144.6 27.2 %collective-permute-start.4 = (bf16[448,1344]{1,0:T(8,128)(2,1)S(1)}, bf16[448,1344]{1,0:T(8,128)(2,1)S(1)}, u32[]{:S(2)}, u32[]{:S(2)}) collective-permute-start(bf16[448,1344]{1,0:T(8,128)(2,1)S(1)} %slice_bitcast_fusion), channel_id=1, source_target_pairs={{0,96},{8,104},{16,112},{24,120},{32,0},{40,8},{48,16},{56,24},{64... | collective-permute-start | bytes 3612680 | tf_op jit(solution)/shard_map/ppermute | solution.py:68
  151.9 28.3 %copy-start.8 = (s32[1024]{0:T(1024)S(1)}, s32[1024]{0:T(1024)}, u32[]{:S(2)}) copy-start(s32[1024]{0:T(1024)} %param.24) | copy-start | bytes 12292
  173.0 20.9 %collective-permute-start.5 = (bf16[8,448,1344]{2,1,0:T(8,128)(2,1)}, bf16[8,448,1344]{2,1,0:T(8,128)(2,1)}, u32[]{:S(2)}, u32[]{:S(2)}) collective-permute-start(bf16[8,448,1344]{2,1,0:T(8,128)(2,1)} %bitcast_dynamic-update-slice_fusion), channel_id=1, source_target_pairs={{0,8},{8,0},{16,24},{24,16},{32,40},{40,32},{48,56},{56,48},{64,72... | collective-permute-start | bytes 28901384 | tf_op jit(solution)/shard_map/ppermute | solution.py:71
  179.9 197.5 %reduce-scatter.2.cloned.1.call-start = ((), (), s32[]{:S(2)}) async-start(), calls=%async_computation.5 | async-start | bytes 8257536 | tf_op jit(solution)/shard_map/reduce_scatter | solution.py:201
  235.3 8.6 %copy-start.7 = (bf16[3,128,448]{1,2,0:T(8,128)(2,1)S(1)}, bf16[3,128,448]{1,2,0:T(8,128)(2,1)}, u32[]{:S(2)}) copy-start(bf16[3,128,448]{1,2,0:T(8,128)(2,1)} %param.22) | copy-start | bytes 1032196
  245.3 2.2 copy-start.2
  247.5 3.2 copy-start.3
  259.5 2.8 slice-start
  259.5 2.8 copy-start.14
  269.2 0.7 copy-start.10
  270.5 23.9 %all-to-all-start = ((s32[16,1,4]{2,1,0:T(1,128)}), s32[16,1,4]{2,1,0:T(1,128)S(1)}, u32[]{:S(2)}, u32[]{:S(2)}) async-start(s32[16,1,4]{2,1,0:T(1,128)} %broadcast_in_dim.107), calls=%async_computation.1 | async-start | bytes 16384 | tf_op jit(solution)/shard_map/all_to_all | solution.py:178
  294.4 36.6 %all-to-all-start.1 = ((bf16[16,4,14336]{2,1,0:T(4,128)(2,1)}), bf16[16,4,14336]{2,1,0:T(4,128)(2,1)}, u32[]{:S(2)}, u32[]{:S(2)}) async-start(bf16[16,4,14336]{2,1,0:T(4,128)(2,1)} %reshape.336), calls=%async_computation.2 | async-start | bytes 3670016 | tf_op jit(solution)/shard_map/all_to_all | solution.py:177
Sparse Core Ops, SparseCore 0:
  32.9 167.7 all-gather.2
  203.0 32.3 all-gather.4
  269.4 108.0 reduce-scatter.1

commit v12 on v10

--- a/solution.py
+++ b/solution.py
@@ -126,6 +126,21 @@
         other[:blocks_half].reshape(quarter, 3 * head_cols),
         preferred_element_type=jnp.float32,
     )
+    adapter_update = first_part[:, split + quarter :]
+    folded_all = folded_all + jnp.concatenate(
+        [
+            jnp.dot(
+                adapter_update[
+                    :,
+                    adapter_selector * adapter_rank_width : (adapter_selector + 1) * adapter_rank_width,
+                ],
+                adapter_up_maps[adapter_selector],
+                preferred_element_type=jnp.float32,
+            )
+            for adapter_selector in range(3)
+        ],
+        1,
+    )
     last_part = with_layout_constraint(
         lax.all_gather(in_order[:, split + quarter :], "tensor", axis=0, tiled=True), row_major
     )
@@ -133,19 +148,9 @@
         last_part, other[blocks_half:].reshape(quarter, 3 * head_cols),
         preferred_element_type=jnp.float32,
     )
-    adapter_update = first_part[:, split + quarter :]
-    folded = [folded_all[:, k * head_cols : (k + 1) * head_cols] for k in range(3)]
-    projected = []
-    for adapter_selector in range(3):
-        adapter = jnp.dot(
-            adapter_update[
-                :,
-                adapter_selector * adapter_rank_width : (adapter_selector + 1) * adapter_rank_width,
-            ],
-            adapter_up_maps[adapter_selector],
-            preferred_element_type=jnp.float32,
-        )
-        projected.append((folded[adapter_selector] + adapter).astype(jnp.bfloat16))
+    projected = [
+        folded_all[:, k * head_cols : (k + 1) * head_cols].astype(jnp.bfloat16) for k in range(3)
+    ]
     query, keys, values = projected
     stream = query.shape[0]
     position = jnp.arange(stream, dtype=jnp.int32)

time: 380 us -> 383 us (level)
  matrix products: 72.6 us -> 76.6 us
    dot_general x3, matrix products: 4.05 us -> 7.9 us  [body(): jnp.dot(adapter_update[:, adapter_selector * adapter_rank_width:(adapter_...]
    slice x5 -> x1, local copies, waits for them, and re-layouts: 11 us -> 8.65 us  [body(): other[blocks_half:].reshape(quarter, 3 * head_cols)]
    unnamed x37 -> x47, local copies, waits for them, and re-layouts: 13.3 us -> 12.1 us
  transfers between devices with their start and end apart: 11 -> 11, of which waited for: 7 -> 6; matrix products, arithmetic and copies ran while one was open for 21% -> 23% of each run, Pallas kernels for 0% -> 0%
where the time goes in v12:
time: 383 us; the launch traced here: 382 us
  waiting for transfers between devices  192 us (50%)
  matrix products  76.6 us (20%)
  local copies, waits for them, and re-layouts  55.8 us (15%)
  starting transfers between devices  29.1 us (8%)
  between operations  14.8 us (4%)
  other arithmetic  13.9 us (4%)
    ppermute x1, waiting for transfers between devices, gather_weights(): from_prev = lax.ppermute(pair, 'dp', to_next)  50 us
    ppermute x1, waiting for transfers between devices, gather_weights(): pair = jnp.stack([weight_shard, lax.ppermute(weight_shard, 'dp', to_yh)])  48.6 us
    reduce_scatter x1, waiting for transfers between devices, body(): lax.psum_scatter(jnp.dot(attended, output_projection_weight, preferred_el...  35.7 us
    all_to_all x1, waiting for transfers between devices, body(): lax.all_to_all(taken, 'dp', split_axis=0, concat_axis=0, tiled=True)  28.1 us
    ppermute x1, waiting for transfers between devices, gather_weights(): lax.ppermute(from_prev[0], 'dp', to_next)  18.9 us
    dot_general x1, matrix products, body(): jnp.dot(first_part[:, :split], mine.reshape(split, 3 * head_cols), prefer...  17.1 us
    unnamed x47, local copies, waits for them, and re-layouts  12.1 us
    dot_general x1, matrix products, body(): jnp.dot(last_part, other[blocks_half:].reshape(quarter, 3 * head_cols), p...  11.4 us
  transfers between devices with their start and end apart: 11, of which 6 were waited for; matrix products, arithmetic and copies ran while one was open for 23% of the time, Pallas kernels for 0%

profile of v12, /device:TPU:1, one launch (start us, length us, event | category | flops | bytes accessed | tf_op | source)
XLA Modules:
  0.0 381.7 jit_solution(3540527378089230121)
XLA Ops:
  7.3 2.4 copy.26
  9.7 1.9 fusion.9
  11.6 2.2 copy.27
  13.9 3.2 multiply_convert_fusion
  17.1 3.5 gather_fusion
  20.7 3.9 %copy.28 = bf16[128,7168]{1,0:T(8,128)(2,1)} copy(bf16[128,7168]{0,1:T(8,128)(2,1)} %bitcast.70) | data formatting | bytes 3670016 | tf_op jit(solution)/shard_map/jit(_take)/gather | solution.py:104
  24.6 0.1 broadcast_in_dim.62
  24.7 1.8 broadcast_select_fusion
  26.7 4.3 %fusion.32 = bf16[128,384]{1,0:T(8,128)(2,1)S(1)} fusion(bf16[7168,384]{1,0:T(8,128)(2,1)} %param.21, f32[7168]{0:T(1024)S(1)} %copy-done.11, f32[128]{0:T(128)S(1)} %add_rsqrt_fusion, bf16[128,3584]{1,0:T(8,128)(2,1)S(1)} %copy-done.5, bf16[128,3584]{1,0:T(8,128)(2,1)S(1)} %copy-done.6), kind=kOutput, calls=%fused_computation.53 | convolution fusion | flops 711114752 | bytes 7467520 | tf_op jit(solution)/shard_map/dot_general | solution.py:108
  31.1 1.2 pad_maximum_fusion.3
  32.4 3.5 concatenate.31
  35.9 3.7 collective-permute-start
  39.7 48.6 %collective-permute-done = bf16[448,1344]{1,0:T(8,128)(2,1)S(1)} collective-permute-done((bf16[448,1344]{1,0:T(8,128)(2,1)}, bf16[448,1344]{1,0:T(8,128)(2,1)S(1)}, u32[]{:S(2)}, u32[]{:S(2)}) %collective-permute-start) | collective-permute-done | bytes 1204256 | tf_op jit(solution)/shard_map/ppermute | solution.py:64
  88.3 1.6 pad_maximum_fusion
  89.9 1.1 collective-permute-start.1
  91.0 1.6 collective-permute-start.2
  92.6 1.2 constant_dynamic-update-slice_fusion.3
  93.8 50.0 %collective-permute-done.1 = bf16[2,448,1344]{2,1,0:T(8,128)(2,1)S(1)} collective-permute-done((bf16[2,448,1344]{2,1,0:T(8,128)(2,1)S(1)}, bf16[2,448,1344]{2,1,0:T(8,128)(2,1)S(1)}, u32[]{:S(2)}, u32[]{:S(2)}) %collective-permute-start.1) | collective-permute-done | bytes 2408480 | tf_op jit(solution)/shard_map/ppermute | solution.py:65
  143.8 0.1 slice_bitcast_fusion.1
  144.0 0.1 slice_bitcast_fusion
  144.1 2.7 collective-permute-start.4
  146.8 1.1 constant_dynamic-update-slice_fusion.2
  148.0 1.6 constant_dynamic-update-slice_fusion.1
  149.6 1.6 constant_dynamic-update-slice_fusion
  151.2 18.9 %collective-permute-done.3 = bf16[448,1344]{1,0:T(8,128)(2,1)S(1)} collective-permute-done((bf16[448,1344]{1,0:T(8,128)(2,1)S(1)}, bf16[448,1344]{1,0:T(8,128)(2,1)S(1)}, u32[]{:S(2)}, u32[]{:S(2)}) %collective-permute-start.3) | collective-permute-done | bytes 1204256 | tf_op jit(solution)/shard_map/ppermute | solution.py:68
  170.1 1.1 bitcast_dynamic-update-slice_fusion.1
  171.2 1.2 bitcast_dynamic-update-slice_fusion
  172.4 5.3 %collective-permute-start.5 = (bf16[8,448,1344]{2,1,0:T(8,128)(2,1)}, bf16[8,448,1344]{2,1,0:T(8,128)(2,1)}, u32[]{:S(2)}, u32[]{:S(2)}) collective-permute-start(bf16[8,448,1344]{2,1,0:T(8,128)(2,1)} %bitcast_dynamic-update-slice_fusion), channel_id=1, source_target_pairs={{0,8},{8,0},{16,24},{24,16},{32,40},{40,32},{48,56},{56,48},{64,72... | collective-permute-start | bytes 28901384 | tf_op jit(solution)/shard_map/ppermute | solution.py:71
  177.7 1.8 slice.147
  180.3 0.6 broadcast_compare_fusion.2
  180.9 1.0 and_and_fusion.1
  181.9 1.2 and_and_fusion
  183.1 10.2 %collective-permute-done.5 = bf16[8,448,1344]{2,1,0:T(8,128)(2,1)} collective-permute-done((bf16[8,448,1344]{2,1,0:T(8,128)(2,1)}, bf16[8,448,1344]{2,1,0:T(8,128)(2,1)}, u32[]{:S(2)}, u32[]{:S(2)}) %collective-permute-start.5) | collective-permute-done | bytes 9633824 | tf_op jit(solution)/shard_map/ppermute | solution.py:71
  193.2 8.7 %fusion.69 = (bf16[4,448,1344]{2,1,0:T(8,128)(2,1)}, bf16[4,448,1344]{2,1,0:T(8,128)(2,1)}) fusion(bf16[8,448,1344]{2,1,0:T(8,128)(2,1)} %collective-permute-done.5), kind=kLoop, calls=%fused_computation.112 | loop fusion | bytes 19267584 | tf_op jit(solution)/shard_map/slice | solution.py:148
  201.9 2.7 fusion.41
  204.6 2.6 fusion.43
  207.2 2.6 fusion.45
  209.8 8.7 %fusion.12 = f32[1024,1344]{0,1:T(8,128)} fusion(bf16[1792,1344]{1,0:T(8,128)(2,1)S(1)} %bitcast.72, bf16[1024,5760]{1,0:T(8,128)(2,1)} %all-gather.3.cloned.1.call-done), kind=kOutput, calls=%fused_computation.18 | convolution fusion | flops 4932501504 | bytes 13991936 | tf_op jit(solution)/shard_map/dot_general | solution.py:124
  218.5 17.1 %fusion.2 = f32[1024,1344]{0,1:T(8,128)} fusion(bf16[3584,1344]{1,0:T(8,128)(2,1)} %bitcast.11, bf16[1024,5760]{1,0:T(8,128)(2,1)} %all-gather.3.cloned.1.call-done), kind=kOutput, calls=%fused_computation.5 | convolution fusion | flops 9865003008 | bytes 22937600 | tf_op jit(solution)/shard_map/dot_general | solution.py:121
  235.6 11.4 %fusion.5 = bf16[1024,1344]{0,1:T(8,128)(2,1)S(1)} fusion(f32[1024,448]{0,1:T(8,128)} %fusion.41, f32[1024,448]{0,1:T(8,128)} %fusion.43, f32[1024,448]{0,1:T(8,128)} %fusion.45, f32[1024,1344]{0,1:T(8,128)} %fusion.2, f32[1024,1344]{0,1:T(8,128)} %fusion.12, bf16[1024,1792]{1,0:T(8,128)(2,1)} %all-gather.5.cloned.1.call-done, bf16[1792,1344]{1,0:T(8,128)(2,1)} %bitcast.71), kind=kOutput, calls=%fused_computation.9 | convolution fusion | flops 4940759040 | bytes 27754496 | tf_op jit(solution)/shard_map/dot_general | solution.py:147
  247.0 1.3 fusion.70
  248.3 1.3 fusion.71
  249.6 3.5 fusion.74
  253.1 2.9 fusion.29
  256.0 4.4 %fusion.73 = (f32[2,512]{1,0:T(2,128)S(1)}, f32[2,512,768]{2,1,0:T(8,128)}) fusion(pred[512,768]{1,0:T(8,128)(4,1)} %and_and_fusion, bf16[512,2,224]{0,2,1:T(8,128)(2,1)} %bitcast.79, bf16[768,2,224]{0,2,1:T(8,128)(2,1)} %bitcast.78), kind=kOutput, calls=%fused_computation.116 | convolution fusion | flops 355468032 | bytes 4689920 | tf_op jit(solution)/shard_map/sub | solution.py:39
  260.4 2.9 fusion.31
  263.3 6.1 %convolution_convert_fusion.1 = bf16[1024,3584]{1,0:T(8,128)(2,1)} fusion(bf16[448,3584]{1,0:T(8,128)(2,1)S(1)} %copy-done, bf16[512,448]{0,1:T(8,128)(2,1)S(1)} %bitcast.85, bf16[512,448]{0,1:T(8,128)(2,1)S(1)} %bitcast.84), kind=kOutput, calls=%fused_computation.4 | convolution fusion | flops 3293839360 | bytes 11468800 | tf_op jit(solution)/shard_map/dot_general | solution.py:207
  269.5 0.6 copy-done.14
  270.1 0.6 broadcast_in_dim.107
  270.7 7.2 %all-to-all-start = ((s32[16,1,4]{2,1,0:T(1,128)}), s32[16,1,4]{2,1,0:T(1,128)S(1)}, u32[]{:S(2)}, u32[]{:S(2)}) async-start(s32[16,1,4]{2,1,0:T(1,128)} %broadcast_in_dim.107), calls=%async_computation.1 | async-start | bytes 16384 | tf_op jit(solution)/shard_map/all_to_all | solution.py:183
  277.9 0.1 convert_reduce_fusion
  278.0 0.2 reduce-window.8
  278.6 1.6 slice_bitcast_fusion.3
  280.2 0.2 pad_maximum_fusion.2
  280.4 3.8 %fusion.22 = bf16[1024,896]{1,0:T(8,128)(2,1)} fusion(bf16[1024,896]{0,1:T(8,128)(2,1)S(1)} %bitcast.76, s32[1024]{0:T(1024)S(1)} %add.117, pred[1024]{0:T(1024)(128)(4,1)S(1)} %lt.81), kind=kOutput, calls=%fused_computation.38 | convolution fusion | flops 1882062848 | bytes 3675136 | tf_op jit(solution)/shard_map/dot_general | solution.py:178
  284.2 4.4 %reshape.336 = bf16[16,4,14336]{2,1,0:T(4,128)(2,1)} reshape(bf16[1024,896]{1,0:T(8,128)(2,1)} %fusion.22) | data formatting | bytes 3670016 | tf_op jit(solution)/shard_map/reshape | solution.py:179
  288.6 7.2 %all-to-all-start.1 = ((bf16[16,4,14336]{2,1,0:T(4,128)(2,1)}), bf16[16,4,14336]{2,1,0:T(4,128)(2,1)}, u32[]{:S(2)}, u32[]{:S(2)}) async-start(bf16[16,4,14336]{2,1,0:T(4,128)(2,1)} %reshape.336), calls=%async_computation.2 | async-start | bytes 3670016 | tf_op jit(solution)/shard_map/all_to_all | solution.py:182
  295.8 0.5 broadcast.205
  296.3 0.7 reduce.3
  297.1 28.1 %all-to-all-done.1 = bf16[16,4,14336]{2,1,0:T(4,128)(2,1)} async-done(((bf16[16,4,14336]{2,1,0:T(4,128)(2,1)}), bf16[16,4,14336]{2,1,0:T(4,128)(2,1)}, u32[]{:S(2)}, u32[]{:S(2)}) %all-to-all-start.1) | async-done | bytes 1835040 | tf_op jit(solution)/shard_map/all_to_all | solution.py:182
  325.2 3.8 %reshape.337 = bf16[64,14336]{1,0:T(8,128)(2,1)} reshape(bf16[16,4,14336]{2,1,0:T(4,128)(2,1)} %all-to-all-done.1) | data formatting | bytes 3670016 | tf_op jit(solution)/shard_map/reshape | solution.py:189
  329.1 3.6 convolution_convert_fusion
  332.6 6.8 %reshape.338 = bf16[64,16,2,448]{3,2,1,0:T(2,128)(2,1)} reshape(bf16[64,14336]{1,0:T(8,128)(2,1)} %convolution_convert_fusion) | data formatting | bytes 3670016 | tf_op jit(solution)/shard_map/reshape | solution.py:193
  339.4 35.7 %reduce-scatter.2.cloned.1.call-done = bf16[128,3584]{1,0:T(8,128)(2,1)} async-done(((bf16[1024,3584]{1,0:T(8,128)(2,1)}), bf16[128,3584]{1,0:T(8,128)(2,1)}) %reduce-scatter.2.cloned.1.call-update) | async-done | bytes 917520 | tf_op jit(solution)/shard_map/reduce_scatter | solution.py:206
  (75 shorter events, 1.2 us)
Async XLA Ops:
  7.2 256.1 %copy-start = (bf16[448,3584]{1,0:T(8,128)(2,1)S(1)}, bf16[448,3584]{1,0:T(8,128)(2,1)}, u32[]{:S(2)}) copy-start(bf16[448,3584]{1,0:T(8,128)(2,1)} %param.23) | copy-start | bytes 9633796
  7.2 6.6 %copy-start.15 = (s32[16]{0:T(128)S(1)}, s32[16]{0:T(128)}, u32[]{:S(2)}) copy-start(s32[16]{0:T(128)} %constant.100.clone) | copy-start | bytes 196
  7.2 6.6 %copy-start.16 = (s32[16]{0:T(128)S(1)}, s32[16]{0:T(128)}, u32[]{:S(2)}) copy-start(s32[16]{0:T(128)} %constant.101.clone) | copy-start | bytes 196
  7.2 6.6 %copy-start.17 = (s32[16]{0:T(128)S(1)}, s32[16]{0:T(128)}, u32[]{:S(2)}) copy-start(s32[16]{0:T(128)} %constant.102.clone) | copy-start | bytes 196
  7.2 6.6 %copy-start.11 = (f32[7168]{0:T(1024)S(1)}, f32[7168]{0:T(1024)}, u32[]{:S(2)}) copy-start(f32[7168]{0:T(1024)} %param.17) | copy-start | bytes 86020
  7.2 194.7 %all-gather.3.cloned.1.call-start = ((), (), s32[]{:S(2)}) async-start(), calls=%async_computation.3 | async-start | bytes 13271040 | tf_op jit(solution)/shard_map/all_gather | solution.py:115
  24.7 2.0 copy-start.5
  24.7 2.0 copy-start.6
  26.6 4.5 %copy-start.3 = (bf16[128,7168]{1,0:T(8,128)(2,1)}, bf16[128,7168]{1,0:T(8,128)(2,1)S(1)}, u32[]{:S(2)}) copy-start(bf16[128,7168]{1,0:T(8,128)(2,1)S(1)} %broadcast_select_fusion) | copy-start | bytes 5505028
  32.3 203.3 %all-gather.5.cloned.1.call-start = ((), (), s32[]{:S(2)}) async-start(), calls=%async_computation.4 | async-start | bytes 4128768 | tf_op jit(solution)/shard_map/all_gather | solution.py:145
  35.9 56.7 %copy-start.1 = (bf16[448,1344]{1,0:T(8,128)(2,1)S(1)}, bf16[448,1344]{1,0:T(8,128)(2,1)}, u32[]{:S(2)}) copy-start(bf16[448,1344]{1,0:T(8,128)(2,1)} %concatenate.31) | copy-start | bytes 3612676
  35.9 52.4 %collective-permute-start = (bf16[448,1344]{1,0:T(8,128)(2,1)}, bf16[448,1344]{1,0:T(8,128)(2,1)S(1)}, u32[]{:S(2)}, u32[]{:S(2)}) collective-permute-start(bf16[448,1344]{1,0:T(8,128)(2,1)} %concatenate.31), channel_id=1, source_target_pairs={{0,16},{8,24},{16,0},{24,8},{32,48},{40,56},{48,32},{56,40},{64,80... | collective-permute-start | bytes 3612680 | tf_op jit(solution)/shard_map/ppermute | solution.py:64
  89.9 53.9 %collective-permute-start.1 = (bf16[2,448,1344]{2,1,0:T(8,128)(2,1)S(1)}, bf16[2,448,1344]{2,1,0:T(8,128)(2,1)S(1)}, u32[]{:S(2)}, u32[]{:S(2)}) collective-permute-start(bf16[2,448,1344]{2,1,0:T(8,128)(2,1)S(1)} %pad_maximum_fusion), channel_id=1, source_target_pairs={{0,32},{8,40},{16,48},{24,56},{32,64},{40,72},{48,80},{56,88},{64,... | collective-permute-start | bytes 7225352 | tf_op jit(solution)/shard_map/ppermute | solution.py:65
  91.0 53.0 %collective-permute-start.2 = (bf16[2,448,1344]{2,1,0:T(8,128)(2,1)S(1)}, bf16[2,448,1344]{2,1,0:T(8,128)(2,1)S(1)}, u32[]{:S(2)}, u32[]{:S(2)}) collective-permute-start(bf16[2,448,1344]{2,1,0:T(8,128)(2,1)S(1)} %pad_maximum_fusion), channel_id=1, source_target_pairs={{0,96},{8,104},{16,112},{24,120},{32,0},{40,8},{48,16},{56,24},{64... | collective-permute-start | bytes 7225352 | tf_op jit(solution)/shard_map/ppermute | solution.py:66
  143.9 26.2 %collective-permute-start.3 = (bf16[448,1344]{1,0:T(8,128)(2,1)S(1)}, bf16[448,1344]{1,0:T(8,128)(2,1)S(1)}, u32[]{:S(2)}, u32[]{:S(2)}) collective-permute-start(bf16[448,1344]{1,0:T(8,128)(2,1)S(1)} %slice_bitcast_fusion.1), channel_id=1, source_target_pairs={{0,32},{8,40},{16,48},{24,56},{32,64},{40,72},{48,80},{56,88},{64,... | collective-permute-start | bytes 3612680 | tf_op jit(solution)/shard_map/ppermute | solution.py:68
  144.1 27.1 %collective-permute-start.4 = (bf16[448,1344]{1,0:T(8,128)(2,1)S(1)}, bf16[448,1344]{1,0:T(8,128)(2,1)S(1)}, u32[]{:S(2)}, u32[]{:S(2)}) collective-permute-start(bf16[448,1344]{1,0:T(8,128)(2,1)S(1)} %slice_bitcast_fusion), channel_id=1, source_target_pairs={{0,96},{8,104},{16,112},{24,120},{32,0},{40,8},{48,16},{56,24},{64... | collective-permute-start | bytes 3612680 | tf_op jit(solution)/shard_map/ppermute | solution.py:68
  151.2 29.1 %copy-start.9 = (s32[1024]{0:T(1024)S(1)}, s32[1024]{0:T(1024)}, u32[]{:S(2)}) copy-start(s32[1024]{0:T(1024)} %param.24) | copy-start | bytes 12292
  172.4 20.8 %collective-permute-start.5 = (bf16[8,448,1344]{2,1,0:T(8,128)(2,1)}, bf16[8,448,1344]{2,1,0:T(8,128)(2,1)}, u32[]{:S(2)}, u32[]{:S(2)}) collective-permute-start(bf16[8,448,1344]{2,1,0:T(8,128)(2,1)} %bitcast_dynamic-update-slice_fusion), channel_id=1, source_target_pairs={{0,8},{8,0},{16,24},{24,16},{32,40},{40,32},{48,56},{56,48},{64,72... | collective-permute-start | bytes 28901384 | tf_op jit(solution)/shard_map/ppermute | solution.py:71
  179.5 195.6 %reduce-scatter.2.cloned.1.call-start = ((), (), s32[]{:S(2)}) async-start(), calls=%async_computation.5 | async-start | bytes 8257536 | tf_op jit(solution)/shard_map/reduce_scatter | solution.py:206
  180.9 2.2 copy-start.12
  183.1 18.8 %copy-start.7 = (bf16[3,128,448]{1,2,0:T(8,128)(2,1)S(1)}, bf16[3,128,448]{1,2,0:T(8,128)(2,1)}, u32[]{:S(2)}) copy-start(bf16[3,128,448]{1,2,0:T(8,128)(2,1)} %param.22) | copy-start | bytes 1032196
  201.9 7.9 %copy-start.4 = (bf16[4,448,1344]{2,1,0:T(8,128)(2,1)S(1)}, bf16[4,448,1344]{2,1,0:T(8,128)(2,1)}, u32[]{:S(2)}) copy-start(bf16[4,448,1344]{2,1,0:T(8,128)(2,1)} %get-tuple-element.5) | copy-start | bytes 14450692
  247.0 2.6 copy-start.2
  247.0 2.6 copy-start.8
  249.6 3.5 copy-start.13
  256.0 4.4 %copy-start.18 = (pred[512]{0:T(512)(128)(4,1)S(1)}, pred[512]{0:T(512)(128)(4,1)}, u32[]{:S(2)}) copy-start(pred[512]{0:T(512)(128)(4,1)} %get-tuple-element.20) | copy-start | bytes 1540
  260.4 2.9 copy-start.19
  269.4 0.7 copy-start.14
  269.4 8.4 %copy-start.10 = (s32[1024]{0:T(1024)S(1)}, s32[1024]{0:T(1024)}, u32[]{:S(2)}) copy-start(s32[1024]{0:T(1024)} %param.24) | copy-start | bytes 12292
  270.7 17.9 %all-to-all-start = ((s32[16,1,4]{2,1,0:T(1,128)}), s32[16,1,4]{2,1,0:T(1,128)S(1)}, u32[]{:S(2)}, u32[]{:S(2)}) async-start(s32[16,1,4]{2,1,0:T(1,128)} %broadcast_in_dim.107), calls=%async_computation.1 | async-start | bytes 16384 | tf_op jit(solution)/shard_map/all_to_all | solution.py:183
  288.6 36.6 %all-to-all-start.1 = ((bf16[16,4,14336]{2,1,0:T(4,128)(2,1)}), bf16[16,4,14336]{2,1,0:T(4,128)(2,1)}, u32[]{:S(2)}, u32[]{:S(2)}) async-start(bf16[16,4,14336]{2,1,0:T(4,128)(2,1)} %reshape.336), calls=%async_computation.2 | async-start | bytes 3670016 | tf_op jit(solution)/shard_map/all_to_all | solution.py:182
Sparse Core Ops, SparseCore 0:
  32.4 150.5 all-gather.2
  185.2 45.0 all-gather.4
  269.6 105.5 reduce-scatter.1

commit v13 on v10

--- a/solution.py
+++ b/solution.py
@@ -113,7 +113,7 @@
     blocks_half = other.shape[0] // 2
     first_part = with_layout_constraint(
         lax.all_gather(
-            jnp.concatenate([in_order[:, : split + quarter], low_local], 1),
+            in_order[:, : split + quarter],
             "tensor", axis=0, tiled=True,
         ),
         row_major,
@@ -127,13 +127,17 @@
         preferred_element_type=jnp.float32,
     )
     last_part = with_layout_constraint(
-        lax.all_gather(in_order[:, split + quarter :], "tensor", axis=0, tiled=True), row_major
+        lax.all_gather(
+            jnp.concatenate([in_order[:, split + quarter :], low_local], 1),
+            "tensor", axis=0, tiled=True,
+        ),
+        row_major,
     )
     folded_all = folded_all + jnp.dot(
-        last_part, other[blocks_half:].reshape(quarter, 3 * head_cols),
+        last_part[:, : split - quarter], other[blocks_half:].reshape(quarter, 3 * head_cols),
         preferred_element_type=jnp.float32,
     )
-    adapter_update = first_part[:, split + quarter :]
+    adapter_update = last_part[:, split - quarter :]
     folded = [folded_all[:, k * head_cols : (k + 1) * head_cols] for k in range(3)]
     projected = []
     for adapter_selector in range(3):

time: 380 us -> 381 us (level)
  waiting for transfers between devices: 193 us -> 197 us
    all_gather x2, waiting for transfers between devices: 1.28 us -> 8.49 us  [the longest x1 8.48 us: body(): lax.all_gather(jnp.concatenate([in_order[:, split + quarter:], low_local]...]
    unnamed x37 -> x41, local copies, waits for them, and re-layouts: 13.3 us -> 13.3 us
where the time goes in v13:
time: 381 us; the launch traced here: 380 us
  waiting for transfers between devices  197 us (52%)
  matrix products  69.5 us (18%)
  local copies, waits for them, and re-layouts  56.2 us (15%)
  starting transfers between devices  29.2 us (8%)
  between operations  14.8 us (4%)
  other arithmetic  13.6 us (4%)
    ppermute x1, waiting for transfers between devices, gather_weights(): from_prev = lax.ppermute(pair, 'dp', to_next)  50 us
    ppermute x1, waiting for transfers between devices, gather_weights(): pair = jnp.stack([weight_shard, lax.ppermute(weight_shard, 'dp', to_yh)])  48.6 us
    reduce_scatter x1, waiting for transfers between devices, body(): lax.psum_scatter(jnp.dot(attended, output_projection_weight, preferred_el...  31.8 us
    all_to_all x1, waiting for transfers between devices, body(): lax.all_to_all(taken, 'dp', split_axis=0, concat_axis=0, tiled=True)  28.1 us
    ppermute x1, waiting for transfers between devices, gather_weights(): lax.ppermute(from_prev[0], 'dp', to_next)  18.8 us
    dot_general x1, matrix products, body(): jnp.dot(first_part[:, :split], mine.reshape(split, 3 * head_cols), prefer...  17.2 us
    unnamed x41, local copies, waits for them, and re-layouts  13.3 us
    dot_general x1, matrix products, body(): jnp.dot(last_part[:, :split - quarter], other[blocks_half:].reshape(quart...  12.5 us
  transfers between devices with their start and end apart: 11, of which 7 were waited for; matrix products, arithmetic and copies ran while one was open for 21% of the time, Pallas kernels for 0%

profile of v13, /device:TPU:1, one launch (start us, length us, event | category | flops | bytes accessed | tf_op | source)
XLA Modules:
  0.0 380.3 jit_solution(18272814946142611586)
XLA Ops:
  7.3 2.4 copy.27
  9.6 2.2 copy.26
  11.9 1.9 fusion.7
  13.9 3.2 multiply_convert_fusion
  17.2 3.6 gather_fusion
  20.7 3.9 %copy.28 = bf16[128,7168]{1,0:T(8,128)(2,1)} copy(bf16[128,7168]{0,1:T(8,128)(2,1)} %bitcast.70) | data formatting | bytes 3670016 | tf_op jit(solution)/shard_map/jit(_take)/gather | solution.py:104
  24.8 1.7 broadcast_select_fusion
  26.5 1.2 copy-done.4
  27.7 1.2 slice.136
  29.0 3.5 concatenate.27
  32.5 3.7 collective-permute-start
  36.3 48.6 %collective-permute-done = bf16[448,1344]{1,0:T(8,128)(2,1)S(1)} collective-permute-done((bf16[448,1344]{1,0:T(8,128)(2,1)}, bf16[448,1344]{1,0:T(8,128)(2,1)S(1)}, u32[]{:S(2)}, u32[]{:S(2)}) %collective-permute-start) | collective-permute-done | bytes 1204256 | tf_op jit(solution)/shard_map/ppermute | solution.py:64
  84.9 1.6 pad_maximum_fusion
  86.5 1.1 collective-permute-start.1
  87.6 1.6 collective-permute-start.2
  89.2 1.1 constant_dynamic-update-slice_fusion.3
  90.4 50.0 %collective-permute-done.1 = bf16[2,448,1344]{2,1,0:T(8,128)(2,1)S(1)} collective-permute-done((bf16[2,448,1344]{2,1,0:T(8,128)(2,1)S(1)}, bf16[2,448,1344]{2,1,0:T(8,128)(2,1)S(1)}, u32[]{:S(2)}, u32[]{:S(2)}) %collective-permute-start.1) | collective-permute-done | bytes 2408480 | tf_op jit(solution)/shard_map/ppermute | solution.py:65
  140.7 2.7 collective-permute-start.4
  143.4 1.2 constant_dynamic-update-slice_fusion.2
  144.6 1.6 constant_dynamic-update-slice_fusion.1
  146.2 1.7 constant_dynamic-update-slice_fusion
  147.9 18.8 %collective-permute-done.3 = bf16[448,1344]{1,0:T(8,128)(2,1)S(1)} collective-permute-done((bf16[448,1344]{1,0:T(8,128)(2,1)S(1)}, bf16[448,1344]{1,0:T(8,128)(2,1)S(1)}, u32[]{:S(2)}, u32[]{:S(2)}) %collective-permute-start.3) | collective-permute-done | bytes 1204256 | tf_op jit(solution)/shard_map/ppermute | solution.py:68
  166.7 1.1 bitcast_dynamic-update-slice_fusion.1
  167.8 1.1 bitcast_dynamic-update-slice_fusion
  168.9 5.3 %collective-permute-start.5 = (bf16[8,448,1344]{2,1,0:T(8,128)(2,1)}, bf16[8,448,1344]{2,1,0:T(8,128)(2,1)}, u32[]{:S(2)}, u32[]{:S(2)}) collective-permute-start(bf16[8,448,1344]{2,1,0:T(8,128)(2,1)} %bitcast_dynamic-update-slice_fusion), channel_id=1, source_target_pairs={{0,8},{8,0},{16,24},{24,16},{32,40},{40,32},{48,56},{56,48},{64,72... | collective-permute-start | bytes 28901384 | tf_op jit(solution)/shard_map/ppermute | solution.py:71
  174.3 1.2 fusion.37
  175.5 0.8 pad_maximum_fusion.4
  177.2 0.3 and_and_fusion.1
  177.5 1.2 and_and_fusion
  178.7 11.1 %collective-permute-done.5 = bf16[8,448,1344]{2,1,0:T(8,128)(2,1)} collective-permute-done((bf16[8,448,1344]{2,1,0:T(8,128)(2,1)}, bf16[8,448,1344]{2,1,0:T(8,128)(2,1)}, u32[]{:S(2)}, u32[]{:S(2)}) %collective-permute-start.5) | collective-permute-done | bytes 9633824 | tf_op jit(solution)/shard_map/ppermute | solution.py:71
  189.8 8.6 %fusion.80 = (bf16[4,448,1344]{2,1,0:T(8,128)(2,1)}, bf16[4,448,1344]{2,1,0:T(8,128)(2,1)}) fusion(bf16[8,448,1344]{2,1,0:T(8,128)(2,1)} %collective-permute-done.5), kind=kLoop, calls=%fused_computation.116 | loop fusion | bytes 19267584 | tf_op jit(solution)/shard_map/slice | solution.py:137
  198.4 10.1 %fusion.14 = f32[1024,1344]{0,1:T(8,128)} fusion(bf16[1792,1344]{1,0:T(8,128)(2,1)} %bitcast.72, bf16[1024,5376]{1,0:T(8,128)(2,1)} %all-gather.3.cloned.1.call-done), kind=kOutput, calls=%fused_computation.18 | convolution fusion | flops 4932501504 | bytes 14221312 | tf_op jit(solution)/shard_map/dot_general | solution.py:124
  208.5 17.2 %fusion.2 = f32[1024,1344]{0,1:T(8,128)} fusion(bf16[3584,1344]{1,0:T(8,128)(2,1)} %bitcast.11, bf16[1024,5376]{1,0:T(8,128)(2,1)} %all-gather.3.cloned.1.call-done), kind=kOutput, calls=%fused_computation.5 | convolution fusion | flops 9865003008 | bytes 22937600 | tf_op jit(solution)/shard_map/dot_general | solution.py:121
  225.7 8.5 %all-gather.5.cloned.1.call-done = bf16[1024,2176]{1,0:T(8,128)(2,1)} async-done(((bf16[128,2176]{1,0:T(8,128)(2,1)}), bf16[1024,2176]{1,0:T(8,128)(2,1)}) %all-gather.5.cloned.1.call-update) | async-done | bytes 4456464 | tf_op jit(solution)/shard_map/all_gather | solution.py:130
  234.2 12.5 %add_add_fusion = f32[1024,1344]{0,1:T(8,128)S(1)} fusion(f32[1024,1344]{0,1:T(8,128)} %fusion.2, f32[1024,1344]{0,1:T(8,128)} %fusion.14, bf16[1792,1344]{1,0:T(8,128)(2,1)} %bitcast.71, bf16[1024,2176]{1,0:T(8,128)(2,1)} %all-gather.5.cloned.1.call-done), kind=kOutput, calls=%fused_computation.7 | convolution fusion | flops 4935254016 | bytes 25231360 | tf_op jit(solution)/shard_map/dot_general | solution.py:136
  246.7 1.4 fusion.24
  248.0 0.9 slice.147
  248.9 1.3 fusion.22
  250.3 1.0 slice.156
  251.3 0.8 slice.153
  252.1 1.3 fusion.23
  253.4 1.0 fusion.81
  254.4 4.5 %fusion.83 = (f32[2,512]{1,0:T(2,128)S(1)}, f32[2,512,768]{2,1,0:T(8,128)}) fusion(pred[512,768]{1,0:T(8,128)(4,1)} %and_and_fusion, bf16[512,2,224]{0,2,1:T(8,128)(2,1)} %bitcast.79, bf16[768,2,224]{0,2,1:T(8,128)(2,1)} %bitcast.77), kind=kOutput, calls=%fused_computation.119 | convolution fusion | flops 355468032 | bytes 4689920 | tf_op jit(solution)/shard_map/sub | solution.py:39
  258.9 3.5 fusion.84
  262.4 2.3 fusion.34
  264.7 0.5 slice-done
  265.2 0.8 fusion.36
  266.0 6.1 %convolution_convert_fusion.1 = bf16[1024,3584]{1,0:T(8,128)(2,1)} fusion(bf16[448,3584]{1,0:T(8,128)(2,1)S(1)} %copy-done, bf16[512,448]{0,1:T(8,128)(2,1)S(1)} %bitcast.86, bf16[512,448]{0,1:T(8,128)(2,1)S(1)} %bitcast.85), kind=kOutput, calls=%fused_computation.4 | convolution fusion | flops 3293839360 | bytes 11468800 | tf_op jit(solution)/shard_map/dot_general | solution.py:206
  272.1 0.6 copy-done.10
  272.7 0.6 broadcast_in_dim.107
  273.3 7.3 %all-to-all-start = ((s32[16,1,4]{2,1,0:T(1,128)}), s32[16,1,4]{2,1,0:T(1,128)S(1)}, u32[]{:S(2)}, u32[]{:S(2)}) async-start(s32[16,1,4]{2,1,0:T(1,128)} %broadcast_in_dim.107), calls=%async_computation.1 | async-start | bytes 16384 | tf_op jit(solution)/shard_map/all_to_all | solution.py:182
  280.6 0.1 convert_reduce_fusion
  280.7 0.2 reduce-window.8
  281.3 1.6 pad_maximum_fusion.2
  283.0 3.8 %fusion.27 = bf16[1024,896]{1,0:T(8,128)(2,1)} fusion(bf16[1024,896]{0,1:T(8,128)(2,1)S(1)} %bitcast.76, s32[1024]{0:T(1024)S(1)} %add.125, pred[1024]{0:T(1024)(128)(4,1)S(1)} %lt.81), kind=kOutput, calls=%fused_computation.44 | convolution fusion | flops 1882062848 | bytes 3675136 | tf_op jit(solution)/shard_map/dot_general | solution.py:177
  286.8 4.3 %reshape.336 = bf16[16,4,14336]{2,1,0:T(4,128)(2,1)} reshape(bf16[1024,896]{1,0:T(8,128)(2,1)} %fusion.27) | data formatting | bytes 3670016 | tf_op jit(solution)/shard_map/reshape | solution.py:178
  291.1 7.2 %all-to-all-start.1 = ((bf16[16,4,14336]{2,1,0:T(4,128)(2,1)}), bf16[16,4,14336]{2,1,0:T(4,128)(2,1)}, u32[]{:S(2)}, u32[]{:S(2)}) async-start(bf16[16,4,14336]{2,1,0:T(4,128)(2,1)} %reshape.336), calls=%async_computation.2 | async-start | bytes 3670016 | tf_op jit(solution)/shard_map/all_to_all | solution.py:181
  298.3 0.5 broadcast.205
  298.9 0.7 reduce.3
  299.6 28.1 %all-to-all-done.1 = bf16[16,4,14336]{2,1,0:T(4,128)(2,1)} async-done(((bf16[16,4,14336]{2,1,0:T(4,128)(2,1)}), bf16[16,4,14336]{2,1,0:T(4,128)(2,1)}, u32[]{:S(2)}, u32[]{:S(2)}) %all-to-all-start.1) | async-done | bytes 1835040 | tf_op jit(solution)/shard_map/all_to_all | solution.py:181
  327.8 3.9 %reshape.337 = bf16[64,14336]{1,0:T(8,128)(2,1)} reshape(bf16[16,4,14336]{2,1,0:T(4,128)(2,1)} %all-to-all-done.1) | data formatting | bytes 3670016 | tf_op jit(solution)/shard_map/reshape | solution.py:188
  331.6 3.6 convolution_convert_fusion
  335.2 6.8 %reshape.338 = bf16[64,16,2,448]{3,2,1,0:T(2,128)(2,1)} reshape(bf16[64,14336]{1,0:T(8,128)(2,1)} %convolution_convert_fusion) | data formatting | bytes 3670016 | tf_op jit(solution)/shard_map/reshape | solution.py:192
  341.9 31.8 %reduce-scatter.2.cloned.1.call-done = bf16[128,3584]{1,0:T(8,128)(2,1)} async-done(((bf16[1024,3584]{1,0:T(8,128)(2,1)}), bf16[128,3584]{1,0:T(8,128)(2,1)}) %reduce-scatter.2.cloned.1.call-update) | async-done | bytes 917520 | tf_op jit(solution)/shard_map/reduce_scatter | solution.py:205
  (74 shorter events, 1.4 us)
Async XLA Ops:
  7.2 258.8 %copy-start = (bf16[448,3584]{1,0:T(8,128)(2,1)S(1)}, bf16[448,3584]{1,0:T(8,128)(2,1)}, u32[]{:S(2)}) copy-start(bf16[448,3584]{1,0:T(8,128)(2,1)} %param.23) | copy-start | bytes 9633796
  7.2 6.7 %copy-start.11 = (s32[16]{0:T(128)S(1)}, s32[16]{0:T(128)}, u32[]{:S(2)}) copy-start(s32[16]{0:T(128)} %constant.102.clone) | copy-start | bytes 196
  7.2 6.7 %copy-start.12 = (s32[16]{0:T(128)S(1)}, s32[16]{0:T(128)}, u32[]{:S(2)}) copy-start(s32[16]{0:T(128)} %constant.101.clone) | copy-start | bytes 196
  7.2 6.7 %copy-start.13 = (s32[16]{0:T(128)S(1)}, s32[16]{0:T(128)}, u32[]{:S(2)}) copy-start(s32[16]{0:T(128)} %constant.100.clone) | copy-start | bytes 196
  7.2 6.6 %copy-start.9 = (f32[7168]{0:T(1024)S(1)}, f32[7168]{0:T(1024)}, u32[]{:S(2)}) copy-start(f32[7168]{0:T(1024)} %param.17) | copy-start | bytes 86020
  7.2 191.2 %all-gather.3.cloned.1.call-start = ((), (), s32[]{:S(2)}) async-start(), calls=%async_computation.3 | async-start | bytes 12386304 | tf_op jit(solution)/shard_map/all_gather | solution.py:115
  26.5 1.2 copy-start.4
  29.0 205.2 %all-gather.5.cloned.1.call-start = ((), (), s32[]{:S(2)}) async-start(), calls=%async_computation.4 | async-start | bytes 5013504 | tf_op jit(solution)/shard_map/all_gather | solution.py:130
  32.5 56.7 %copy-start.1 = (bf16[448,1344]{1,0:T(8,128)(2,1)S(1)}, bf16[448,1344]{1,0:T(8,128)(2,1)}, u32[]{:S(2)}) copy-start(bf16[448,1344]{1,0:T(8,128)(2,1)} %concatenate.27) | copy-start | bytes 3612676
  32.5 52.3 %collective-permute-start = (bf16[448,1344]{1,0:T(8,128)(2,1)}, bf16[448,1344]{1,0:T(8,128)(2,1)S(1)}, u32[]{:S(2)}, u32[]{:S(2)}) collective-permute-start(bf16[448,1344]{1,0:T(8,128)(2,1)} %concatenate.27), channel_id=1, source_target_pairs={{0,16},{8,24},{16,0},{24,8},{32,48},{40,56},{48,32},{56,40},{64,80... | collective-permute-start | bytes 3612680 | tf_op jit(solution)/shard_map/ppermute | solution.py:64
  86.5 53.9 %collective-permute-start.1 = (bf16[2,448,1344]{2,1,0:T(8,128)(2,1)S(1)}, bf16[2,448,1344]{2,1,0:T(8,128)(2,1)S(1)}, u32[]{:S(2)}, u32[]{:S(2)}) collective-permute-start(bf16[2,448,1344]{2,1,0:T(8,128)(2,1)S(1)} %pad_maximum_fusion), channel_id=1, source_target_pairs={{0,32},{8,40},{16,48},{24,56},{32,64},{40,72},{48,80},{56,88},{64,... | collective-permute-start | bytes 7225352 | tf_op jit(solution)/shard_map/ppermute | solution.py:65
  87.6 52.9 %collective-permute-start.2 = (bf16[2,448,1344]{2,1,0:T(8,128)(2,1)S(1)}, bf16[2,448,1344]{2,1,0:T(8,128)(2,1)S(1)}, u32[]{:S(2)}, u32[]{:S(2)}) collective-permute-start(bf16[2,448,1344]{2,1,0:T(8,128)(2,1)S(1)} %pad_maximum_fusion), channel_id=1, source_target_pairs={{0,96},{8,104},{16,112},{24,120},{32,0},{40,8},{48,16},{56,24},{64... | collective-permute-start | bytes 7225352 | tf_op jit(solution)/shard_map/ppermute | solution.py:66
  140.5 26.2 %collective-permute-start.3 = (bf16[448,1344]{1,0:T(8,128)(2,1)S(1)}, bf16[448,1344]{1,0:T(8,128)(2,1)S(1)}, u32[]{:S(2)}, u32[]{:S(2)}) collective-permute-start(bf16[448,1344]{1,0:T(8,128)(2,1)S(1)} %slice_bitcast_fusion.1), channel_id=1, source_target_pairs={{0,32},{8,40},{16,48},{24,56},{32,64},{40,72},{48,80},{56,88},{64,... | collective-permute-start | bytes 3612680 | tf_op jit(solution)/shard_map/ppermute | solution.py:68
  140.7 27.1 %collective-permute-start.4 = (bf16[448,1344]{1,0:T(8,128)(2,1)S(1)}, bf16[448,1344]{1,0:T(8,128)(2,1)S(1)}, u32[]{:S(2)}, u32[]{:S(2)}) collective-permute-start(bf16[448,1344]{1,0:T(8,128)(2,1)S(1)} %slice_bitcast_fusion), channel_id=1, source_target_pairs={{0,96},{8,104},{16,112},{24,120},{32,0},{40,8},{48,16},{56,24},{64... | collective-permute-start | bytes 3612680 | tf_op jit(solution)/shard_map/ppermute | solution.py:68
  144.6 29.6 %slice-start.2 = ((s8[5505024]{0:T(1024)(128)(4,1)}), s8[4194304]{0:T(1024)(128)(4,1)S(1)}, s32[]{:S(2)}) async-start(s8[5505024]{0:T(1024)(128)(4,1)} %bitcast.83), calls=%async_computation.8 | async-start | bytes 8388608
  146.2 28.0 %slice-start.3 = ((s8[5505024]{0:T(1024)(128)(4,1)}), s8[1310720]{0:T(1024)(128)(4,1)S(1)}, s32[]{:S(2)}) async-start(s8[5505024]{0:T(1024)(128)(4,1)} %bitcast.83), calls=%async_computation.9 | async-start | bytes 2621440
  147.9 26.3 %copy-start.5 = (bf16[128,3584]{1,0:T(8,128)(2,1)S(1)}, bf16[128,3584]{1,0:T(8,128)(2,1)}, u32[]{:S(2)}) copy-start(bf16[128,3584]{1,0:T(8,128)(2,1)} %param.16) | copy-start | bytes 2752516
  147.9 26.3 %copy-start.6 = (bf16[128,3584]{1,0:T(8,128)(2,1)S(1)}, bf16[128,3584]{1,0:T(8,128)(2,1)}, u32[]{:S(2)}) copy-start(bf16[128,3584]{1,0:T(8,128)(2,1)} %param.15) | copy-start | bytes 2752516
  168.9 20.9 %collective-permute-start.5 = (bf16[8,448,1344]{2,1,0:T(8,128)(2,1)}, bf16[8,448,1344]{2,1,0:T(8,128)(2,1)}, u32[]{:S(2)}, u32[]{:S(2)}) collective-permute-start(bf16[8,448,1344]{2,1,0:T(8,128)(2,1)} %bitcast_dynamic-update-slice_fusion), channel_id=1, source_target_pairs={{0,8},{8,0},{16,24},{24,16},{32,40},{40,32},{48,56},{56,48},{64,72... | collective-permute-start | bytes 28901384 | tf_op jit(solution)/shard_map/ppermute | solution.py:71
  174.3 1.3 slice-start.1
  174.3 2.2 copy-start.8
  176.4 197.3 %reduce-scatter.2.cloned.1.call-start = ((), (), s32[]{:S(2)}) async-start(), calls=%async_computation.5 | async-start | bytes 8257536 | tf_op jit(solution)/shard_map/reduce_scatter | solution.py:205
  234.2 12.5 %copy-start.7 = (bf16[3,128,448]{1,2,0:T(8,128)(2,1)S(1)}, bf16[3,128,448]{1,2,0:T(8,128)(2,1)}, u32[]{:S(2)}) copy-start(bf16[3,128,448]{1,2,0:T(8,128)(2,1)} %param.22) | copy-start | bytes 1032196
  248.0 3.3 copy-start.2
  250.2 4.2 %copy-start.3 = (bf16[1024,448]{0,1:T(8,128)(2,1)}, bf16[1024,448]{0,1:T(8,128)(2,1)S(1)}, u32[]{:S(2)}) copy-start(bf16[1024,448]{0,1:T(8,128)(2,1)S(1)} %fusion.22) | copy-start | bytes 2752516
  262.4 2.8 slice-start
  262.4 2.8 copy-start.14
  272.1 0.7 copy-start.10
  273.3 17.8 %all-to-all-start = ((s32[16,1,4]{2,1,0:T(1,128)}), s32[16,1,4]{2,1,0:T(1,128)S(1)}, u32[]{:S(2)}, u32[]{:S(2)}) async-start(s32[16,1,4]{2,1,0:T(1,128)} %broadcast_in_dim.107), calls=%async_computation.1 | async-start | bytes 16384 | tf_op jit(solution)/shard_map/all_to_all | solution.py:182
  291.1 36.6 %all-to-all-start.1 = ((bf16[16,4,14336]{2,1,0:T(4,128)(2,1)}), bf16[16,4,14336]{2,1,0:T(4,128)(2,1)}, u32[]{:S(2)}, u32[]{:S(2)}) async-start(bf16[16,4,14336]{2,1,0:T(4,128)(2,1)} %reshape.336), calls=%async_computation.2 | async-start | bytes 3670016 | tf_op jit(solution)/shard_map/all_to_all | solution.py:181
Sparse Core Ops, SparseCore 0:
  29.1 143.1 all-gather.2
  176.5 57.6 all-gather.4
  272.2 101.4 reduce-scatter.1
